TPU v7x, 1024 devices: a whole 4x8x16 slice. The times are simulated.
1024 devices in a mesh: section: 2 (over z_hi), dp: 32 (over x, y), seq: 16 (over z_lo, core).
Axes of the slice: x: 4, y: 8, z: 16 (z_hi: 2, z_lo: 8; z = z_hi * 8 + z_lo), core: 2. Of those that a mesh axis runs over, the one named last changes fastest.
Arguments:
- saved_inputs: bfloat16 [2, 64, 2048, 768], P('section', 'dp', 'seq'), may hold values from -50 to 50
- pooled_adjoint: bfloat16 [64, 1024, 768], P('dp', 'seq'), may hold values from -6 to 6
- weights: bfloat16 [2, 768, 2304], P('section', 'dp'), may hold values from -0.125 to 0.125
Outputs:
- input_adjoint: bfloat16 [2, 64, 2048, 768], P('section', 'dp', 'seq')
- weight_grad: bfloat16 [2, 768, 2304], P('section', 'dp')
All inputs are finite; a program needn't handle non-finite values.
Results may differ from a plain program's by a relative error of at most 0.023.
Values may be sent and summed in bfloat16 or wider, within the bound.
No kernel may reach another device: no remote copies, remote signals or barrier semaphores. Data moves between devices by JAX's collectives and lax.ppermute only.
A program may use at most 32 MiB of HBM per device.

v0:
```python
import jax
import jax.numpy as jnp
from jax import lax
from jax.sharding import PartitionSpec as P

DILATION_STEP = 16


def with_halo(array, sides, width):
    for axis, dim in sides:
        count, length = (lax.axis_size(axis), array.shape[dim])
        up = [(i, (i + 1) % count) for i in range(count - 1)]
        down = [(j, i) for i, j in up]
        last = lax.slice_in_dim(array, length - width, length, axis=dim)
        initial = lax.slice_in_dim(array, 0, width, axis=dim)
        before = lax.ppermute(last, axis, up)
        after = lax.ppermute(initial, axis, down)
        array = jnp.concatenate([before, array, after], axis=dim)
    return array


def from_behind(value, axis, steps):
    count = lax.axis_size(axis)
    initial, last = (max(0, -steps), min(count, count - steps))
    return lax.ppermute(value, axis, [(source, source + steps) for source in range(initial, last)])


def gelu_gate(value):
    inner = 0.7978845608 * (value + 0.044715 * value * value * value)
    return 0.5 * value * (1.0 + jnp.tanh(inner))


def gelu_derivative(value):
    inner = 0.7978845608 * (value + 0.044715 * value * value * value)
    tangent = jnp.tanh(inner)
    return 0.5 * (1.0 + tangent) + 0.5 * value * (1.0 - tangent * tangent) * 0.7978845608 * (
        1.0 + 0.134145 * value * value
    )


def select_position(array, position_index):
    return lax.dynamic_index_in_dim(array, position_index, 0, keepdims=False)


def local(saved_inputs, pooled_adjoint, weights):
    section_id = lax.axis_index("section")
    is_last = section_id == lax.axis_size("section") - 1
    micro_batch = saved_inputs.shape[1]
    batch_rows = saved_inputs.shape[2]
    channel_width = weights.shape[2] // 3
    dilation_amount = DILATION_STEP
    full_kernel = lax.all_gather(weights[0], "dp", axis=0, tiled=True)
    value_rows = saved_inputs[0].astype(jnp.float32)
    norm_scale = lax.rsqrt(jnp.mean(value_rows * value_rows, axis=-1, keepdims=True) + 1e-05)
    normalized_input = value_rows * norm_scale
    layer_activation = gelu_gate(normalized_input).astype(jnp.bfloat16)
    activation_widened_full = jnp.zeros(
        (micro_batch, batch_rows + 2 * dilation_amount, channel_width), jnp.bfloat16
    )
    grad_total = jnp.zeros((channel_width, 3 * channel_width), jnp.float32)
    results = jnp.zeros((micro_batch, batch_rows, channel_width), jnp.bfloat16)
    incoming = jnp.zeros((batch_rows, channel_width), jnp.bfloat16)
    for step_index in range(micro_batch + 1):
        slot_raw = step_index - 1 + section_id
        is_valid = (slot_raw >= 0) & (slot_raw < micro_batch)
        position_index = jnp.clip(slot_raw, 0, micro_batch - 1)
        upsampled = jnp.repeat(select_position(pooled_adjoint, position_index), 2, axis=0) * 0.5
        cotangent_state = jnp.where(is_last, upsampled, incoming)
        stacked_rows = jnp.stack(
            [select_position(layer_activation, position_index), cotangent_state], axis=0
        )
        paired_widened = with_halo(stacked_rows, (("seq", 1),), dilation_amount)
        activation_widened = paired_widened[0]
        cotangent_widened = paired_widened[1]
        current_act = select_position(activation_widened_full, position_index)
        activation_widened_full = lax.dynamic_update_index_in_dim(
            activation_widened_full,
            jnp.where(is_valid, activation_widened, current_act),
            position_index,
            0,
        )
        cotangent_kernel_taps = jnp.concatenate(
            [
                cotangent_widened[
                    (2 - kernel_offset) * dilation_amount : (2 - kernel_offset) * dilation_amount
                    + batch_rows
                ]
                for kernel_offset in range(3)
            ],
            axis=-1,
        )
        reverse_propagate = jnp.einsum(
            "pj,cj->pc", cotangent_kernel_taps, full_kernel, preferred_element_type=jnp.float32
        )
        position_normalized = select_position(normalized_input, position_index)
        position_scale = select_position(norm_scale, position_index)
        derivative_gradient = reverse_propagate * gelu_derivative(position_normalized)
        centered_average = jnp.mean(
            derivative_gradient * position_normalized, axis=-1, keepdims=True
        )
        block_output = (
            cotangent_state.astype(jnp.float32)
            + position_scale * (derivative_gradient - position_normalized * centered_average)
        ).astype(jnp.bfloat16)
        current = select_position(results, position_index)
        results = lax.dynamic_update_index_in_dim(
            results, jnp.where(is_valid, block_output, current), position_index, 0
        )
        activation_kernel_taps = jnp.stack(
            [
                activation_widened[
                    kernel_offset * dilation_amount : kernel_offset * dilation_amount + batch_rows
                ]
                for kernel_offset in range(3)
            ],
            axis=0,
        )
        grad_term = jnp.einsum(
            "kpc,po->cko",
            activation_kernel_taps,
            cotangent_state,
            preferred_element_type=jnp.float32,
        )
        grad_total = grad_total + jnp.where(
            is_valid, grad_term.reshape(channel_width, 3 * channel_width), 0.0
        )
        if step_index < micro_batch:
            incoming = from_behind(block_output, "section", -1)
    owned = lax.psum_scatter(
        grad_total.astype(jnp.bfloat16), "dp", scatter_dimension=0, tiled=True
    ).astype(jnp.float32)
    summed = lax.psum(owned, "seq")
    weight_grad = (summed / (micro_batch * lax.axis_size("dp"))).astype(jnp.bfloat16)
    return (results[None], weight_grad[None])


def solution(mesh):
    in_specs = (P("section", "dp", "seq", None), P("dp", "seq", None), P("section", "dp", None))
    out_specs = (P("section", "dp", "seq", None), P("section", "dp", None))
    return jax.shard_map(local, mesh=mesh, in_specs=in_specs, out_specs=out_specs, check_vma=False)
```

profile of v0, /device:TPU:1, one launch (start us, length us, event | category | flops | bytes accessed | tf_op | source)
XLA Modules:
  0.0 515.6 jit_solution(618062991544402857)
XLA Ops:
  7.2 0.0 copy-start
  7.2 0.0 all-gather.3.cloned.1.call-start
  7.2 0.7 all-gather.3.cloned.1.call-update
  7.9 0.0 reduce-scatter.2.cloned.1.call-start
  8.0 1.0 multiply_bitcast_fusion
  9.0 0.1 broadcast_in_dim.45
  9.1 0.1 select_n.110
  9.2 0.0 copy-done
  9.2 0.2 fusion.21
  9.4 0.4 convert_multiply_fusion
  9.7 0.1 constant_dynamic-slice_fusion
  9.8 16.0 %collective-permute-start = (bf16[2,16,768]{2,1,0:T(8,128)(2,1)S(1)}, bf16[2,16,768]{2,1,0:T(8,128)(2,1)S(1)}, u32[]{:S(2)}, u32[]{:S(2)}) collective-permute-start(bf16[2,16,768]{2,1,0:T(8,128)(2,1)S(1)} %get-tuple-element.21), channel_id=1, source_target_pairs={{1,0},{2,1},{3,2},{4,3},{5,4},{6,5},{7,6},{8,7},{9,8},{10,9},{11,1... | collective-permute-start | bytes 147464 | tf_op jit(solution)/shard_map/ppermute | solution.py:17
  25.9 1.9 collective-permute-start.1
  27.8 0.1 select_n.109
  27.9 0.0 collective-permute-done
  27.9 1.1 collective-permute-done.1
  29.0 84.8 %all-gather.3.cloned.1.call-done = bf16[1,768,2304]{2,1,0:T(8,128)(2,1)} async-done(((bf16[1,24,2304]{2,1,0:T(8,128)(2,1)}), bf16[1,768,2304]{2,1,0:T(8,128)(2,1)}) %all-gather.3.cloned.1.call-update) | async-done | bytes 3538960 | tf_op jit(solution)/shard_map/all_gather | solution.py:52
  113.8 3.4 fusion.113
  117.2 0.2 bitcast_dynamic-update-slice_fusion.1
  117.4 1.3 collective-permute-start.2
  118.7 0.1 broadcast_in_dim.51
  118.8 0.1 mul.311
  118.9 0.1 broadcast_in_dim.48
  119.0 0.1 mul.289
  119.1 14.3 %collective-permute-done.2 = bf16[128,768]{1,0:T(8,128)(2,1)S(1)} collective-permute-done((bf16[128,768]{1,0:T(8,128)(2,1)S(1)}, bf16[128,768]{1,0:T(8,128)(2,1)S(1)}, u32[]{:S(2)}, u32[]{:S(2)}) %collective-permute-start.2) | collective-permute-done | bytes 196640 | tf_op jit(solution)/shard_map/ppermute | solution.py:25
  133.5 7.1 %collective-permute-start.3 = (bf16[2,16,768]{2,1,0:T(8,128)(2,1)S(1)}, bf16[2,16,768]{2,1,0:T(8,128)(2,1)S(1)}, u32[]{:S(2)}, u32[]{:S(2)}) collective-permute-start(bf16[2,16,768]{2,1,0:T(8,128)(2,1)S(1)} %get-tuple-element.17), channel_id=1, source_target_pairs={{1,0},{2,1},{3,2},{4,3},{5,4},{6,5},{7,6},{8,7},{9,8},{10,9},{11,1... | collective-permute-start | bytes 147464 | tf_op jit(solution)/shard_map/ppermute | solution.py:17
  140.5 13.2 %collective-permute-start.4 = (bf16[2,16,768]{2,1,0:T(8,128)(2,1)S(1)}, bf16[2,16,768]{2,1,0:T(8,128)(2,1)S(1)}, u32[]{:S(2)}, u32[]{:S(2)}) collective-permute-start(bf16[2,16,768]{2,1,0:T(8,128)(2,1)S(1)} %get-tuple-element.18), channel_id=1, source_target_pairs={{0,1},{1,2},{2,3},{3,4},{4,5},{5,6},{6,7},{7,8},{8,9},{9,10},{10,1... | collective-permute-start | bytes 147464 | tf_op jit(solution)/shard_map/ppermute | solution.py:16
  153.8 0.0 collective-permute-done.3
  153.8 1.1 collective-permute-done.4
  154.9 3.4 fusion.106
  158.4 0.2 bitcast_dynamic-update-slice_fusion
  158.6 1.3 collective-permute-start.5
  159.9 1.1 fusion.30
  161.0 13.0 %collective-permute-done.5 = bf16[128,768]{1,0:T(8,128)(2,1)S(1)} collective-permute-done((bf16[128,768]{1,0:T(8,128)(2,1)S(1)}, bf16[128,768]{1,0:T(8,128)(2,1)S(1)}, u32[]{:S(2)}, u32[]{:S(2)}) %collective-permute-start.5) | collective-permute-done | bytes 196640 | tf_op jit(solution)/shard_map/ppermute | solution.py:25
  174.0 1.9 collective-permute-start.6
  176.0 16.7 %collective-permute-start.7 = (bf16[2,16,768]{2,1,0:T(8,128)(2,1)S(1)}, bf16[2,16,768]{2,1,0:T(8,128)(2,1)S(1)}, u32[]{:S(2)}, u32[]{:S(2)}) collective-permute-start(bf16[2,16,768]{2,1,0:T(8,128)(2,1)S(1)} %get-tuple-element.11), channel_id=1, source_target_pairs={{0,1},{1,2},{2,3},{3,4},{4,5},{5,6},{6,7},{7,8},{8,9},{9,10},{10,1... | collective-permute-start | bytes 147464 | tf_op jit(solution)/shard_map/ppermute | solution.py:16
  192.7 1.1 fusion.37
  193.8 0.0 collective-permute-done.6
  193.8 0.0 collective-permute-done.7
  193.8 3.1 add_convert_fusion
  197.0 5.8 %copy.8 = bf16[768,2304]{1,0:T(8,128)(2,1)} copy(bf16[768,2304]{0,1:T(8,128)(2,1)} %bitcast.163) | data formatting | bytes 7077888 | tf_op jit(solution)/shard_map/convert_element_type | solution.py:130
  202.8 0.0 reduce-scatter.2.cloned.1.call-update
  202.8 3.4 fusion.99
  206.3 0.2 fusion.121
  206.5 0.0 copy-start.1
  206.5 209.4 %reduce-scatter.2.cloned.1.call-done = bf16[24,2304]{1,0:T(8,128)(2,1)} async-done(((bf16[768,2304]{1,0:T(8,128)(2,1)}), bf16[24,2304]{1,0:T(8,128)(2,1)}) %reduce-scatter.2.cloned.1.call-update) | async-done | bytes 110608 | tf_op jit(solution)/shard_map/reduce_scatter | solution.py:129
  415.9 92.3 %all-reduce.1 = f32[24,2304]{1,0:T(8,128)S(1)} all-reduce(bf16[24,2304]{1,0:T(8,128)(2,1)} %reduce-scatter.2.cloned.1.call-done), channel_id=1, replica_groups=mesh['section'=2,'dp'=32,'seq'=16] {'seq'}, use_global_device_ids=true, to_apply=%region_5.6 | all-reduce | flops 55296 | bytes 331776 | tf_op jit(solution)/shard_map/psum | solution.py:132
  508.1 0.7 fusion.125
  508.8 0.0 copy-done.1
  (16 shorter events, 0.3 us)
Async XLA Ops:
  7.2 2.0 copy-start
  7.2 106.6 %all-gather.3.cloned.1.call-start = ((), (), s32[]{:S(2)}) async-start(), calls=%async_computation.2 | async-start | bytes 3649536 | tf_op jit(solution)/shard_map/all_gather | solution.py:52
  7.9 408.0 %reduce-scatter.2.cloned.1.call-start = ((), (), s32[]{:S(2)}) async-start(), calls=%async_computation.1 | async-start | bytes 3649536 | tf_op jit(solution)/shard_map/reduce_scatter | solution.py:129
  9.8 18.1 %collective-permute-start = (bf16[2,16,768]{2,1,0:T(8,128)(2,1)S(1)}, bf16[2,16,768]{2,1,0:T(8,128)(2,1)S(1)}, u32[]{:S(2)}, u32[]{:S(2)}) collective-permute-start(bf16[2,16,768]{2,1,0:T(8,128)(2,1)S(1)} %get-tuple-element.21), channel_id=1, source_target_pairs={{1,0},{2,1},{3,2},{4,3},{5,4},{6,5},{7,6},{8,7},{9,8},{10,9},{11,1... | collective-permute-start | bytes 147464 | tf_op jit(solution)/shard_map/ppermute | solution.py:17
  25.9 3.1 collective-permute-start.1
  117.4 16.0 %collective-permute-start.2 = (bf16[128,768]{1,0:T(8,128)(2,1)S(1)}, bf16[128,768]{1,0:T(8,128)(2,1)S(1)}, u32[]{:S(2)}, u32[]{:S(2)}) collective-permute-start(bf16[128,768]{1,0:T(8,128)(2,1)S(1)} %get-tuple-element.5), channel_id=1, source_target_pairs={{512,0},{513,1},{514,2},{515,3},{516,4},{517,5},{518,6},{519,7},{5... | collective-permute-start | bytes 589832 | tf_op jit(solution)/shard_map/ppermute | solution.py:25
  133.5 20.3 %collective-permute-start.3 = (bf16[2,16,768]{2,1,0:T(8,128)(2,1)S(1)}, bf16[2,16,768]{2,1,0:T(8,128)(2,1)S(1)}, u32[]{:S(2)}, u32[]{:S(2)}) collective-permute-start(bf16[2,16,768]{2,1,0:T(8,128)(2,1)S(1)} %get-tuple-element.17), channel_id=1, source_target_pairs={{1,0},{2,1},{3,2},{4,3},{5,4},{6,5},{7,6},{8,7},{9,8},{10,9},{11,1... | collective-permute-start | bytes 147464 | tf_op jit(solution)/shard_map/ppermute | solution.py:17
  140.5 14.4 %collective-permute-start.4 = (bf16[2,16,768]{2,1,0:T(8,128)(2,1)S(1)}, bf16[2,16,768]{2,1,0:T(8,128)(2,1)S(1)}, u32[]{:S(2)}, u32[]{:S(2)}) collective-permute-start(bf16[2,16,768]{2,1,0:T(8,128)(2,1)S(1)} %get-tuple-element.18), channel_id=1, source_target_pairs={{0,1},{1,2},{2,3},{3,4},{4,5},{5,6},{6,7},{7,8},{8,9},{9,10},{10,1... | collective-permute-start | bytes 147464 | tf_op jit(solution)/shard_map/ppermute | solution.py:16
  158.6 15.4 %collective-permute-start.5 = (bf16[128,768]{1,0:T(8,128)(2,1)S(1)}, bf16[128,768]{1,0:T(8,128)(2,1)S(1)}, u32[]{:S(2)}, u32[]{:S(2)}) collective-permute-start(bf16[128,768]{1,0:T(8,128)(2,1)S(1)} %get-tuple-element.3), channel_id=1, source_target_pairs={{512,0},{513,1},{514,2},{515,3},{516,4},{517,5},{518,6},{519,7},{5... | collective-permute-start | bytes 589832 | tf_op jit(solution)/shard_map/ppermute | solution.py:25
  174.0 19.7 %collective-permute-start.6 = (bf16[2,16,768]{2,1,0:T(8,128)(2,1)S(1)}, bf16[2,16,768]{2,1,0:T(8,128)(2,1)S(1)}, u32[]{:S(2)}, u32[]{:S(2)}) collective-permute-start(bf16[2,16,768]{2,1,0:T(8,128)(2,1)S(1)} %get-tuple-element.10), channel_id=1, source_target_pairs={{1,0},{2,1},{3,2},{4,3},{5,4},{6,5},{7,6},{8,7},{9,8},{10,9},{11,1... | collective-permute-start | bytes 147464 | tf_op jit(solution)/shard_map/ppermute | solution.py:17
  176.0 17.8 %collective-permute-start.7 = (bf16[2,16,768]{2,1,0:T(8,128)(2,1)S(1)}, bf16[2,16,768]{2,1,0:T(8,128)(2,1)S(1)}, u32[]{:S(2)}, u32[]{:S(2)}) collective-permute-start(bf16[2,16,768]{2,1,0:T(8,128)(2,1)S(1)} %get-tuple-element.11), channel_id=1, source_target_pairs={{0,1},{1,2},{2,3},{3,4},{4,5},{5,6},{6,7},{7,8},{8,9},{9,10},{10,1... | collective-permute-start | bytes 147464 | tf_op jit(solution)/shard_map/ppermute | solution.py:16
  206.5 302.3 %copy-start.1 = (bf16[1,2,128,768]{3,2,1,0:T(8,128)(2,1)}, bf16[1,2,128,768]{3,2,1,0:T(8,128)(2,1)S(1)}, u32[]{:S(2)}) copy-start(bf16[1,2,128,768]{3,2,1,0:T(8,128)(2,1)S(1)} %fusion.121) | copy-start | bytes 1179652
Sparse Core Ops, SparseCore 0:
  12.3 101.3 all-gather.2
  202.9 212.9 reduce-scatter.1
where the time goes:
time: 523 us; the launch traced here: 516 us
  waiting for transfers between devices  324 us (62%)
  blocking collectives  92.3 us (18%)
  starting transfers between devices  59.5 us (11%)
  matrix products  15.6 us (3%)
  between operations  14.4 us (3%)
  local copies, waits for them, and re-layouts  6.57 us (1%)
    reduce_scatter x1, waiting for transfers between devices, local(): lax.psum_scatter(grad_total.astype(jnp.bfloat16), 'dp', scatter_dimension...  209 us
    psum x1, blocking collectives, local(): summed = lax.psum(owned, 'seq')  92.3 us
    all_gather x1, waiting for transfers between devices, local(): full_kernel = lax.all_gather(weights[0], 'dp', axis=0, tiled=True)  84.8 us
    ppermute x3, starting transfers between devices, with_halo(): before = lax.ppermute(last, axis, up)  31.8 us
    ppermute x2, waiting for transfers between devices, from_behind(): lax.ppermute(value, axis, [(source, source + steps) for source in range(i...  27.3 us
    ppermute x3, starting transfers between devices, with_halo(): after = lax.ppermute(initial, axis, down)  25 us
  transfers between devices with their start and end apart: 10, of which 6 were waited for; matrix products, arithmetic and copies ran while one was open for 2% of the time, Pallas kernels for 0%

commit v1 on v0

--- a/solution.py
+++ b/solution.py
@@ -126,11 +126,18 @@
         )
         if step_index < micro_batch:
             incoming = from_behind(block_output, "section", -1)
-    owned = lax.psum_scatter(
-        grad_total.astype(jnp.bfloat16), "dp", scatter_dimension=0, tiled=True
-    ).astype(jnp.float32)
-    summed = lax.psum(owned, "seq")
-    weight_grad = (summed / (micro_batch * lax.axis_size("dp"))).astype(jnp.bfloat16)
+    n_dp = lax.axis_size("dp")
+    n_seq = lax.axis_size("seq")
+    owned_rows = channel_width // n_dp
+    pieces = grad_total.astype(jnp.bfloat16).reshape(n_dp, owned_rows, 3 * channel_width)
+    received = lax.all_to_all(pieces, "dp", 0, 0, tiled=True)
+    owned = jnp.sum(received.astype(jnp.float32), axis=0)
+    column_chunk = 3 * channel_width // n_seq
+    owned = owned.reshape(owned_rows, n_seq, column_chunk).transpose(1, 0, 2)
+    gathered = lax.all_to_all(owned, "seq", 0, 0, tiled=True)
+    summed = jnp.sum(gathered, axis=0)
+    chunk_grad = (summed / (micro_batch * n_dp)).astype(jnp.bfloat16)
+    weight_grad = lax.all_gather(chunk_grad, "seq", axis=1, tiled=True)
     return (results[None], weight_grad[None])
 
 

time: 523 us -> 370 us (0.71); the launches traced: 516 us -> 369 us
  waiting for transfers between devices: 324 us -> 199 us
  blocking collectives: 92.3 us -> 30.4 us
  starting transfers between devices: 59.5 us -> 82.5 us
  local copies, waits for them, and re-layouts: 6.57 us -> 22.8 us
    reduce_scatter x1 -> x0, waiting for transfers between devices: 209 us -> none  [local(): lax.psum_scatter(grad_total.astype(jnp.bfloat16), 'dp', scatter_dimension...]
    psum x1 -> x0, blocking collectives: 92.3 us -> none  [local(): summed = lax.psum(owned, 'seq')]
    all_to_all x0 -> x2, waiting for transfers between devices: none -> 84 us  [the longest x1 66.2 us: local(): received = lax.all_to_all(pieces, 'dp', 0, 0, tiled=True)]
    all_gather x0 -> x1, blocking collectives: none -> 30.4 us  [local(): weight_grad = lax.all_gather(chunk_grad, 'seq', axis=1, tiled=True)]
    all_to_all x0 -> x2, starting transfers between devices: none -> 22.9 us  [the longest x1 17.6 us: local(): gathered = lax.all_to_all(owned, 'seq', 0, 0, tiled=True)]
    add x0 -> x1, local copies, waits for them, and re-layouts: none -> 5.69 us  [local(): grad_total + jnp.where(is_valid, grad_term.reshape(channel_width, 3 * cha...]
  transfers between devices with their start and end apart: 10 -> 11, of which waited for: 6 -> 7; matrix products, arithmetic and copies ran while one was open for 2% -> 3% of each run, Pallas kernels for 0% -> 0%
where the time goes in v1:
time: 370 us; the launch traced here: 369 us
  waiting for transfers between devices  199 us (54%)
  starting transfers between devices  82.5 us (22%)
  blocking collectives  30.4 us (8%)
  local copies, waits for them, and re-layouts  22.8 us (6%)
  between operations  14.5 us (4%)
  matrix products  14.4 us (4%)
  other arithmetic  5.3 us (1%)
    all_gather x1, waiting for transfers between devices, local(): full_kernel = lax.all_gather(weights[0], 'dp', axis=0, tiled=True)  84.8 us
    all_to_all x1, waiting for transfers between devices, local(): received = lax.all_to_all(pieces, 'dp', 0, 0, tiled=True)  66.2 us
    ppermute x3, starting transfers between devices, with_halo(): before = lax.ppermute(last, axis, up)  32 us
    all_gather x1, blocking collectives, local(): weight_grad = lax.all_gather(chunk_grad, 'seq', axis=1, tiled=True)  30.4 us
    ppermute x2, waiting for transfers between devices, from_behind(): lax.ppermute(value, axis, [(source, source + steps) for source in range(i...  27.3 us
    ppermute x3, starting transfers between devices, with_halo(): after = lax.ppermute(initial, axis, down)  25 us
    all_to_all x1, waiting for transfers between devices, local(): gathered = lax.all_to_all(owned, 'seq', 0, 0, tiled=True)  17.9 us
    all_to_all x1, starting transfers between devices, local(): gathered = lax.all_to_all(owned, 'seq', 0, 0, tiled=True)  17.6 us
  transfers between devices with their start and end apart: 11, of which 7 were waited for; matrix products, arithmetic and copies ran while one was open for 3% of the time, Pallas kernels for 0%

profile of v1, /device:TPU:1, one launch (start us, length us, event | category | flops | bytes accessed | tf_op | source)
XLA Modules:
  0.0 369.0 jit_solution(18123490051558877499)
XLA Ops:
  7.2 0.0 copy-start.8
  7.2 0.0 all-gather.4.cloned.1.call-start
  7.2 0.7 all-gather.4.cloned.1.call-update
  7.9 1.0 multiply_bitcast_fusion
  8.9 0.1 broadcast_in_dim.45
  9.1 0.1 select_n.113
  9.1 0.0 copy-done.8
  9.2 0.2 fusion.22
  9.3 0.4 convert_multiply_fusion
  9.7 0.0 copy-start
  9.7 0.1 constant_dynamic-slice_fusion
  9.8 0.0 copy-start.6
  9.8 16.0 %collective-permute-start = (bf16[2,16,768]{2,1,0:T(8,128)(2,1)S(1)}, bf16[2,16,768]{2,1,0:T(8,128)(2,1)S(1)}, u32[]{:S(2)}, u32[]{:S(2)}) collective-permute-start(bf16[2,16,768]{2,1,0:T(8,128)(2,1)S(1)} %get-tuple-element.21), channel_id=1, source_target_pairs={{1,0},{2,1},{3,2},{4,3},{5,4},{6,5},{7,6},{8,7},{9,8},{10,9},{11,1... | collective-permute-start | bytes 147464 | tf_op jit(solution)/shard_map/ppermute | solution.py:17
  25.8 1.9 collective-permute-start.1
  27.8 0.1 select_n.112
  27.9 0.0 collective-permute-done
  27.9 1.1 collective-permute-done.1
  29.0 84.8 %all-gather.4.cloned.1.call-done = bf16[1,768,2304]{2,1,0:T(8,128)(2,1)} async-done(((bf16[1,24,2304]{2,1,0:T(8,128)(2,1)}), bf16[1,768,2304]{2,1,0:T(8,128)(2,1)}) %all-gather.4.cloned.1.call-update) | async-done | bytes 3538960 | tf_op jit(solution)/shard_map/all_gather | solution.py:52
  113.8 3.4 fusion.114
  117.2 0.2 bitcast_dynamic-update-slice_fusion.1
  117.4 1.3 collective-permute-start.2
  118.7 0.1 broadcast_in_dim.51
  118.8 0.1 mul.311
  118.9 0.1 broadcast_in_dim.48
  119.0 0.1 mul.289
  119.1 14.3 %collective-permute-done.2 = bf16[128,768]{1,0:T(8,128)(2,1)S(1)} collective-permute-done((bf16[128,768]{1,0:T(8,128)(2,1)S(1)}, bf16[128,768]{1,0:T(8,128)(2,1)S(1)}, u32[]{:S(2)}, u32[]{:S(2)}) %collective-permute-start.2) | collective-permute-done | bytes 196640 | tf_op jit(solution)/shard_map/ppermute | solution.py:25
  133.5 7.0 %collective-permute-start.3 = (bf16[2,16,768]{2,1,0:T(8,128)(2,1)S(1)}, bf16[2,16,768]{2,1,0:T(8,128)(2,1)S(1)}, u32[]{:S(2)}, u32[]{:S(2)}) collective-permute-start(bf16[2,16,768]{2,1,0:T(8,128)(2,1)S(1)} %get-tuple-element.17), channel_id=1, source_target_pairs={{1,0},{2,1},{3,2},{4,3},{5,4},{6,5},{7,6},{8,7},{9,8},{10,9},{11,1... | collective-permute-start | bytes 147464 | tf_op jit(solution)/shard_map/ppermute | solution.py:17
  140.5 13.2 %collective-permute-start.4 = (bf16[2,16,768]{2,1,0:T(8,128)(2,1)S(1)}, bf16[2,16,768]{2,1,0:T(8,128)(2,1)S(1)}, u32[]{:S(2)}, u32[]{:S(2)}) collective-permute-start(bf16[2,16,768]{2,1,0:T(8,128)(2,1)S(1)} %get-tuple-element.18), channel_id=1, source_target_pairs={{0,1},{1,2},{2,3},{3,4},{4,5},{5,6},{6,7},{7,8},{8,9},{9,10},{10,1... | collective-permute-start | bytes 147464 | tf_op jit(solution)/shard_map/ppermute | solution.py:16
  153.8 0.0 collective-permute-done.3
  153.8 1.1 collective-permute-done.4
  154.9 3.4 fusion.107
  158.4 0.2 bitcast_dynamic-update-slice_fusion
  158.6 0.0 copy-start.2
  158.6 1.3 collective-permute-start.5
  159.9 1.1 fusion.31
  161.0 0.0 copy-done.2
  161.0 13.0 %collective-permute-done.5 = bf16[128,768]{1,0:T(8,128)(2,1)S(1)} collective-permute-done((bf16[128,768]{1,0:T(8,128)(2,1)S(1)}, bf16[128,768]{1,0:T(8,128)(2,1)S(1)}, u32[]{:S(2)}, u32[]{:S(2)}) %collective-permute-start.5) | collective-permute-done | bytes 196640 | tf_op jit(solution)/shard_map/ppermute | solution.py:25
  174.1 1.9 collective-permute-start.6
  176.0 16.8 %collective-permute-start.7 = (bf16[2,16,768]{2,1,0:T(8,128)(2,1)S(1)}, bf16[2,16,768]{2,1,0:T(8,128)(2,1)S(1)}, u32[]{:S(2)}, u32[]{:S(2)}) collective-permute-start(bf16[2,16,768]{2,1,0:T(8,128)(2,1)S(1)} %get-tuple-element.11), channel_id=1, source_target_pairs={{0,1},{1,2},{2,3},{3,4},{4,5},{5,6},{6,7},{7,8},{8,9},{9,10},{10,1... | collective-permute-start | bytes 147464 | tf_op jit(solution)/shard_map/ppermute | solution.py:16
  192.9 1.1 fusion.38
  194.0 0.0 collective-permute-done.6
  194.0 0.0 copy-start.13
  194.0 0.0 collective-permute-done.7
  194.0 0.6 copy-done.13
  194.6 0.6 copy-done.14
  195.2 1.9 fusion
  197.1 5.7 %copy.25 = bf16[768,3,768]{2,1,0:T(4,128)(2,1)} copy(bf16[768,3,768]{0,2,1:T(8,128)(2,1)S(1)} %fusion) | data formatting | bytes 7077888 | tf_op jit(solution)/shard_map/add | solution.py:124
  202.8 10.1 %convert_element_type.47 = bf16[32,24,2304]{2,1,0:T(8,128)(2,1)} reshape(bf16[768,3,768]{2,1,0:T(4,128)(2,1)} %copy.25) | data formatting | bytes 7077888 | tf_op jit(solution)/shard_map/convert_element_type | solution.py:132
  212.8 5.3 %all-to-all-start = ((bf16[32,24,2304]{2,1,0:T(8,128)(2,1)}), bf16[32,24,2304]{2,1,0:T(8,128)(2,1)S(1)}, u32[]{:S(2)}, u32[]{:S(2)}) async-start(bf16[32,24,2304]{2,1,0:T(8,128)(2,1)} %convert_element_type.47), calls=%async_computation | async-start | bytes 7077888 | tf_op jit(solution)/shard_map/all_to_all | solution.py:133
  218.2 1.8 copy.36
  219.9 1.8 maximum_bitcast_fusion.1
  221.7 66.2 %all-to-all-done = bf16[32,24,2304]{2,1,0:T(8,128)(2,1)S(1)} async-done(((bf16[32,24,2304]{2,1,0:T(8,128)(2,1)}), bf16[32,24,2304]{2,1,0:T(8,128)(2,1)S(1)}, u32[]{:S(2)}, u32[]{:S(2)}) %all-to-all-start) | async-done | bytes 3538976 | tf_op jit(solution)/shard_map/all_to_all | solution.py:133
  287.9 1.2 convert_reduce_fusion
  289.1 1.3 reshape.147
  290.4 1.0 copy.26
  291.4 17.6 %all-to-all-start.1 = ((f32[16,24,144]{2,1,0:T(8,128)}), f32[16,24,144]{2,1,0:T(8,128)S(1)}, u32[]{:S(2)}, u32[]{:S(2)}) async-start(f32[16,24,144]{2,1,0:T(8,128)} %copy.26), calls=%async_computation.1 | async-start | bytes 786432 | tf_op jit(solution)/shard_map/all_to_all | solution.py:137
  309.1 0.0 copy-start.3
  309.1 0.0 copy-start.9
  309.1 3.5 fusion.100
  312.6 0.2 fusion.122
  312.8 0.0 copy-start.10
  312.9 17.9 %all-to-all-done.1 = f32[16,24,144]{2,1,0:T(8,128)S(1)} async-done(((f32[16,24,144]{2,1,0:T(8,128)}), f32[16,24,144]{2,1,0:T(8,128)S(1)}, u32[]{:S(2)}, u32[]{:S(2)}) %all-to-all-start.1) | async-done | bytes 221216 | tf_op jit(solution)/shard_map/all_to_all | solution.py:137
  330.8 30.4 %all-gather.1 = bf16[16,144,24]{1,2,0:T(8,128)(2,1)S(1)} all-gather(bf16[1,144,24]{1,2,0:T(8,128)(2,1)S(1)} %fusion.126), channel_id=1, replica_groups=mesh['section'=2,'dp'=32,'seq'=16] {'seq'}, dimensions={0}, use_global_device_ids=true | all-gather | bytes 117504 | tf_op jit(solution)/shard_map/all_gather | solution.py:140
  361.2 0.9 reshape.151
  (35 shorter events, 0.3 us)
Async XLA Ops:
  7.2 2.0 copy-start.8
  7.2 106.6 %all-gather.4.cloned.1.call-start = ((), (), s32[]{:S(2)}) async-start(), calls=%async_computation.2 | async-start | bytes 3649536 | tf_op jit(solution)/shard_map/all_gather | solution.py:52
  9.7 148.7 %copy-start = (f32[2,128,768]{2,1,0:T(8,128)}, f32[2,128,768]{2,1,0:T(8,128)S(1)}, u32[]{:S(2)}) copy-start(f32[2,128,768]{2,1,0:T(8,128)S(1)} %get-tuple-element.6) | copy-start | bytes 2359300
  9.8 164.3 %copy-start.6 = (bf16[1,128,768]{2,1,0:T(8,128)(2,1)}, bf16[1,128,768]{2,1,0:T(8,128)(2,1)S(1)}, u32[]{:S(2)}) copy-start(bf16[1,128,768]{2,1,0:T(8,128)(2,1)S(1)} %get-tuple-element.12) | copy-start | bytes 589828
  9.8 18.1 %collective-permute-start = (bf16[2,16,768]{2,1,0:T(8,128)(2,1)S(1)}, bf16[2,16,768]{2,1,0:T(8,128)(2,1)S(1)}, u32[]{:S(2)}, u32[]{:S(2)}) collective-permute-start(bf16[2,16,768]{2,1,0:T(8,128)(2,1)S(1)} %get-tuple-element.21), channel_id=1, source_target_pairs={{1,0},{2,1},{3,2},{4,3},{5,4},{6,5},{7,6},{8,7},{9,8},{10,9},{11,1... | collective-permute-start | bytes 147464 | tf_op jit(solution)/shard_map/ppermute | solution.py:17
  25.8 3.1 collective-permute-start.1
  117.4 16.0 %collective-permute-start.2 = (bf16[128,768]{1,0:T(8,128)(2,1)S(1)}, bf16[128,768]{1,0:T(8,128)(2,1)S(1)}, u32[]{:S(2)}, u32[]{:S(2)}) collective-permute-start(bf16[128,768]{1,0:T(8,128)(2,1)S(1)} %get-tuple-element.5), channel_id=1, source_target_pairs={{512,0},{513,1},{514,2},{515,3},{516,4},{517,5},{518,6},{519,7},{5... | collective-permute-start | bytes 589832 | tf_op jit(solution)/shard_map/ppermute | solution.py:25
  133.5 20.3 %collective-permute-start.3 = (bf16[2,16,768]{2,1,0:T(8,128)(2,1)S(1)}, bf16[2,16,768]{2,1,0:T(8,128)(2,1)S(1)}, u32[]{:S(2)}, u32[]{:S(2)}) collective-permute-start(bf16[2,16,768]{2,1,0:T(8,128)(2,1)S(1)} %get-tuple-element.17), channel_id=1, source_target_pairs={{1,0},{2,1},{3,2},{4,3},{5,4},{6,5},{7,6},{8,7},{9,8},{10,9},{11,1... | collective-permute-start | bytes 147464 | tf_op jit(solution)/shard_map/ppermute | solution.py:17
  140.5 14.4 %collective-permute-start.4 = (bf16[2,16,768]{2,1,0:T(8,128)(2,1)S(1)}, bf16[2,16,768]{2,1,0:T(8,128)(2,1)S(1)}, u32[]{:S(2)}, u32[]{:S(2)}) collective-permute-start(bf16[2,16,768]{2,1,0:T(8,128)(2,1)S(1)} %get-tuple-element.18), channel_id=1, source_target_pairs={{0,1},{1,2},{2,3},{3,4},{4,5},{5,6},{6,7},{7,8},{8,9},{9,10},{10,1... | collective-permute-start | bytes 147464 | tf_op jit(solution)/shard_map/ppermute | solution.py:16
  158.6 2.4 copy-start.2
  158.6 15.4 %collective-permute-start.5 = (bf16[128,768]{1,0:T(8,128)(2,1)S(1)}, bf16[128,768]{1,0:T(8,128)(2,1)S(1)}, u32[]{:S(2)}, u32[]{:S(2)}) collective-permute-start(bf16[128,768]{1,0:T(8,128)(2,1)S(1)} %get-tuple-element.3), channel_id=1, source_target_pairs={{512,0},{513,1},{514,2},{515,3},{516,4},{517,5},{518,6},{519,7},{5... | collective-permute-start | bytes 589832 | tf_op jit(solution)/shard_map/ppermute | solution.py:25
  174.0 20.0 %copy-start.4 = (bf16[128,768]{1,0:T(8,128)(2,1)}, bf16[128,768]{1,0:T(8,128)(2,1)S(1)}, u32[]{:S(2)}) copy-start(bf16[128,768]{1,0:T(8,128)(2,1)S(1)} %broadcast_select_fusion) | copy-start | bytes 589828
  174.1 19.9 %collective-permute-start.6 = (bf16[2,16,768]{2,1,0:T(8,128)(2,1)S(1)}, bf16[2,16,768]{2,1,0:T(8,128)(2,1)S(1)}, u32[]{:S(2)}, u32[]{:S(2)}) collective-permute-start(bf16[2,16,768]{2,1,0:T(8,128)(2,1)S(1)} %get-tuple-element.10), channel_id=1, source_target_pairs={{1,0},{2,1},{3,2},{4,3},{5,4},{6,5},{7,6},{8,7},{9,8},{10,9},{11,1... | collective-permute-start | bytes 147464 | tf_op jit(solution)/shard_map/ppermute | solution.py:17
  176.0 19.2 %copy-start.7 = (bf16[1,128,768]{2,1,0:T(8,128)(2,1)S(1)}, bf16[1,128,768]{2,1,0:T(8,128)(2,1)}, u32[]{:S(2)}) copy-start(bf16[1,128,768]{2,1,0:T(8,128)(2,1)} %copy-done.6) | copy-start | bytes 589828
  176.0 18.0 %collective-permute-start.7 = (bf16[2,16,768]{2,1,0:T(8,128)(2,1)S(1)}, bf16[2,16,768]{2,1,0:T(8,128)(2,1)S(1)}, u32[]{:S(2)}, u32[]{:S(2)}) collective-permute-start(bf16[2,16,768]{2,1,0:T(8,128)(2,1)S(1)} %get-tuple-element.11), channel_id=1, source_target_pairs={{0,1},{1,2},{2,3},{3,4},{4,5},{5,6},{6,7},{7,8},{8,9},{9,10},{10,1... | collective-permute-start | bytes 147464 | tf_op jit(solution)/shard_map/ppermute | solution.py:16
  194.0 0.6 copy-start.13
  194.6 0.6 copy-start.14
  212.8 75.1 %all-to-all-start = ((bf16[32,24,2304]{2,1,0:T(8,128)(2,1)}), bf16[32,24,2304]{2,1,0:T(8,128)(2,1)S(1)}, u32[]{:S(2)}, u32[]{:S(2)}) async-start(bf16[32,24,2304]{2,1,0:T(8,128)(2,1)} %convert_element_type.47), calls=%async_computation | async-start | bytes 7077888 | tf_op jit(solution)/shard_map/all_to_all | solution.py:133
  289.1 20.0 %copy-start.1 = (f32[2,128,768]{2,1,0:T(8,128)S(1)}, f32[2,128,768]{2,1,0:T(8,128)}, u32[]{:S(2)}) copy-start(f32[2,128,768]{2,1,0:T(8,128)} %copy-done) | copy-start | bytes 2359300
  289.1 20.0 %copy-start.5 = (bf16[128,768]{1,0:T(8,128)(2,1)S(1)}, bf16[128,768]{1,0:T(8,128)(2,1)}, u32[]{:S(2)}) copy-start(bf16[128,768]{1,0:T(8,128)(2,1)} %copy-done.4) | copy-start | bytes 589828
  289.1 20.0 %copy-start.11 = (bf16[128,768]{1,0:T(8,128)(2,1)S(1)}, bf16[128,768]{1,0:T(8,128)(2,1)}, u32[]{:S(2)}) copy-start(bf16[128,768]{1,0:T(8,128)(2,1)} %get-tuple-element.8) | copy-start | bytes 589828
  289.1 20.0 %copy-start.12 = (bf16[128,768]{1,0:T(8,128)(2,1)S(1)}, bf16[128,768]{1,0:T(8,128)(2,1)}, u32[]{:S(2)}) copy-start(bf16[128,768]{1,0:T(8,128)(2,1)} %get-tuple-element.9) | copy-start | bytes 589828
  291.4 39.3 %all-to-all-start.1 = ((f32[16,24,144]{2,1,0:T(8,128)}), f32[16,24,144]{2,1,0:T(8,128)S(1)}, u32[]{:S(2)}, u32[]{:S(2)}) async-start(f32[16,24,144]{2,1,0:T(8,128)} %copy.26), calls=%async_computation.1 | async-start | bytes 786432 | tf_op jit(solution)/shard_map/all_to_all | solution.py:137
  309.1 3.5 copy-start.3
  309.1 3.5 copy-start.9
  312.8 49.3 %copy-start.10 = (bf16[1,2,128,768]{3,2,1,0:T(8,128)(2,1)}, bf16[1,2,128,768]{3,2,1,0:T(8,128)(2,1)S(1)}, u32[]{:S(2)}) copy-start(bf16[1,2,128,768]{3,2,1,0:T(8,128)(2,1)S(1)} %fusion.122) | copy-start | bytes 1179652
Sparse Core Ops, SparseCore 0:
  12.3 101.3 all-gather.3

commit v2 on v1

--- a/solution.py
+++ b/solution.py
@@ -49,7 +49,17 @@
     batch_rows = saved_inputs.shape[2]
     channel_width = weights.shape[2] // 3
     dilation_amount = DILATION_STEP
-    full_kernel = lax.all_gather(weights[0], "dp", axis=0, tiled=True)
+    seq_count = lax.axis_size("seq")
+    core_index = lax.axis_index("seq") % 2
+    half_columns = weights.shape[2] // 2
+    own_half = lax.dynamic_slice_in_dim(weights[0], core_index * half_columns, half_columns, axis=1)
+    gathered_half = lax.all_gather(own_half, "dp", axis=0, tiled=True)
+    partner_half = lax.ppermute(gathered_half, "seq", [(j, j ^ 1) for j in range(seq_count)])
+    full_kernel = jnp.where(
+        core_index == 0,
+        jnp.concatenate([gathered_half, partner_half], axis=1),
+        jnp.concatenate([partner_half, gathered_half], axis=1),
+    )
     value_rows = saved_inputs[0].astype(jnp.float32)
     norm_scale = lax.rsqrt(jnp.mean(value_rows * value_rows, axis=-1, keepdims=True) + 1e-05)
     normalized_input = value_rows * norm_scale

time: 370 us -> 387 us (1.046)
  waiting for transfers between devices: 199 us -> 218 us
  starting transfers between devices: 82.5 us -> 77.3 us
  matrix products: 14.4 us -> 18.9 us
    ppermute x3, starting transfers between devices: 25 us -> 5.76 us  [with_halo(): after = lax.ppermute(initial, axis, down)]
    all_gather x1, waiting for transfers between devices: 84.8 us -> 102 us  [local(): gathered_half = lax.all_gather(own_half, 'dp', axis=0, tiled=True)]
    ppermute x0 -> x1, starting transfers between devices: none -> 7.19 us  [local(): lax.ppermute(gathered_half, 'seq', [(j, j ^ 1) for j in range(seq_count)])]
    ppermute x3, starting transfers between devices: 32 us -> 37.9 us  [with_halo(): before = lax.ppermute(last, axis, up)]
  transfers between devices with their start and end apart: 11 -> 12, of which waited for: 7 -> 7; matrix products, arithmetic and copies ran while one was open for 3% -> 3% of each run, Pallas kernels for 0% -> 0%
where the time goes in v2:
time: 387 us; the launch traced here: 386 us
  waiting for transfers between devices  218 us (56%)
  starting transfers between devices  77.3 us (20%)
  blocking collectives  30.4 us (8%)
  local copies, waits for them, and re-layouts  22.7 us (6%)
  matrix products  18.9 us (5%)
  between operations  14.5 us (4%)
  other arithmetic  4.89 us (1%)
    all_gather x1, waiting for transfers between devices, local(): gathered_half = lax.all_gather(own_half, 'dp', axis=0, tiled=True)  102 us
    all_to_all x1, waiting for transfers between devices, local(): received = lax.all_to_all(pieces, 'dp', 0, 0, tiled=True)  69.1 us
    ppermute x3, starting transfers between devices, with_halo(): before = lax.ppermute(last, axis, up)  37.9 us
    all_gather x1, blocking collectives, local(): weight_grad = lax.all_gather(chunk_grad, 'seq', axis=1, tiled=True)  30.4 us
    ppermute x2, waiting for transfers between devices, from_behind(): lax.ppermute(value, axis, [(source, source + steps) for source in range(i...  28 us
    all_to_all x1, starting transfers between devices, local(): gathered = lax.all_to_all(owned, 'seq', 0, 0, tiled=True)  18.1 us
    all_to_all x1, waiting for transfers between devices, local(): gathered = lax.all_to_all(owned, 'seq', 0, 0, tiled=True)  16.5 us
    dot_general x3, matrix products, local(): jnp.einsum('pj,cj->pc', cotangent_kernel_taps, full_kernel, preferred_ele...  13.7 us
  transfers between devices with their start and end apart: 12, of which 7 were waited for; matrix products, arithmetic and copies ran while one was open for 3% of the time, Pallas kernels for 0%

profile of v2, /device:TPU:1, one launch (start us, length us, event | category | flops | bytes accessed | tf_op | source)
XLA Modules:
  0.0 386.3 jit_solution(8847730987702555844)
XLA Ops:
  7.2 0.0 copy-start
  7.2 0.0 copy-start.1
  7.2 0.0 all-gather.4.cloned.1.call-start
  7.3 0.8 copy-done
  8.1 0.6 constant_dynamic-slice_fusion.5
  8.7 0.0 all-gather.4.cloned.1.call-update
  8.7 101.8 %all-gather.4.cloned.1.call-done = bf16[1,768,1152]{2,1,0:T(8,128)(2,1)} async-done(((bf16[1,24,1152]{2,1,0:T(8,128)(2,1)}), bf16[1,768,1152]{2,1,0:T(8,128)(2,1)}) %all-gather.4.cloned.1.call-update) | async-done | bytes 1769488 | tf_op jit(solution)/shard_map/all_gather | solution.py:56
  110.6 7.2 %collective-permute-start.2 = (bf16[768,1152]{1,0:T(8,128)(2,1)}, bf16[768,1152]{1,0:T(8,128)(2,1)}, u32[]{:S(2)}, u32[]{:S(2)}) collective-permute-start(bf16[768,1152]{1,0:T(8,128)(2,1)} %bitcast.158), channel_id=1, source_target_pairs={{0,1},{1,0},{2,3},{3,2},{4,5},{5,4},{6,7},{7,6},{8,9},{9,8},{10,11... | collective-permute-start | bytes 5308424 | tf_op jit(solution)/shard_map/ppermute | solution.py:57
  117.8 1.0 multiply_bitcast_fusion
  118.8 0.1 broadcast_in_dim.45
  118.9 0.1 select_n.131
  119.0 0.0 copy-done.1
  119.0 0.2 fusion.7
  119.2 0.4 convert_multiply_fusion
  119.5 0.1 constant_dynamic-slice_fusion
  119.6 1.9 collective-permute-start
  121.5 3.6 collective-permute-start.1
  125.2 0.1 select_n.130
  125.3 0.0 collective-permute-done
  125.3 1.0 collective-permute-done.1
  126.4 0.0 collective-permute-done.2
  126.4 5.0 %fusion.99 = (f32[128]{0:T(128)S(1)}, f32[128,768]{1,0:T(8,128)S(1)}) fusion(f32[2,128,768]{2,1,0:T(8,128)S(1)} %get-tuple-element.6, s32[]{:T(128)S(6)} %min.10, bf16[768,1152]{1,0:T(8,128)(2,1)} %collective-permute-done.2, bf16[768,1152]{1,0:T(8,128)(2,1)} %bitcast.159, pred[]{:T(512)S(6)} %eq.9, bf16[128,768]{1,0:T(8,128)(2,1)S(1)} %get-tuple-element.20, ...), kind=kOutput, calls=%fused_computation.124 | convolution fusion | flops 472645504 | bytes 4915717 | tf_op jit(solution)/shard_map/pj,cj->pc/dot_general | solution.py:102
  131.4 0.2 bitcast_dynamic-update-slice_fusion.1
  131.6 1.3 collective-permute-start.3
  132.9 0.1 broadcast_in_dim.51
  133.0 0.1 mul.315
  133.1 0.1 broadcast_in_dim.48
  133.2 0.1 mul.293
  133.3 0.0 copy-start.3
  133.3 15.0 %collective-permute-done.3 = bf16[128,768]{1,0:T(8,128)(2,1)S(1)} collective-permute-done((bf16[128,768]{1,0:T(8,128)(2,1)S(1)}, bf16[128,768]{1,0:T(8,128)(2,1)S(1)}, u32[]{:S(2)}, u32[]{:S(2)}) %collective-permute-start.3) | collective-permute-done | bytes 196640 | tf_op jit(solution)/shard_map/ppermute | solution.py:25
  148.4 1.9 collective-permute-start.4
  150.3 17.0 %collective-permute-start.5 = (bf16[2,16,768]{2,1,0:T(8,128)(2,1)S(1)}, bf16[2,16,768]{2,1,0:T(8,128)(2,1)S(1)}, u32[]{:S(2)}, u32[]{:S(2)}) collective-permute-start(bf16[2,16,768]{2,1,0:T(8,128)(2,1)S(1)} %get-tuple-element.18), channel_id=1, source_target_pairs={{0,1},{1,2},{2,3},{3,4},{4,5},{5,6},{6,7},{7,8},{8,9},{9,10},{10,1... | collective-permute-start | bytes 147464 | tf_op jit(solution)/shard_map/ppermute | solution.py:16
  167.3 0.0 collective-permute-done.4
  167.3 1.1 collective-permute-done.5
  168.5 0.0 copy-done.3
  168.5 3.8 fusion.92
  172.3 0.2 bitcast_dynamic-update-slice_fusion
  172.5 1.3 collective-permute-start.6
  173.8 1.1 fusion.16
  174.9 12.9 %collective-permute-done.6 = bf16[128,768]{1,0:T(8,128)(2,1)S(1)} collective-permute-done((bf16[128,768]{1,0:T(8,128)(2,1)S(1)}, bf16[128,768]{1,0:T(8,128)(2,1)S(1)}, u32[]{:S(2)}, u32[]{:S(2)}) %collective-permute-start.6) | collective-permute-done | bytes 196640 | tf_op jit(solution)/shard_map/ppermute | solution.py:25
  187.9 1.9 collective-permute-start.7
  189.8 17.3 %collective-permute-start.8 = (bf16[2,16,768]{2,1,0:T(8,128)(2,1)S(1)}, bf16[2,16,768]{2,1,0:T(8,128)(2,1)S(1)}, u32[]{:S(2)}, u32[]{:S(2)}) collective-permute-start(bf16[2,16,768]{2,1,0:T(8,128)(2,1)S(1)} %get-tuple-element.11), channel_id=1, source_target_pairs={{0,1},{1,2},{2,3},{3,4},{4,5},{5,6},{6,7},{7,8},{8,9},{9,10},{10,1... | collective-permute-start | bytes 147464 | tf_op jit(solution)/shard_map/ppermute | solution.py:16
  207.1 1.1 fusion.23
  208.2 0.0 collective-permute-done.7
  208.2 0.0 collective-permute-done.8
  208.3 3.1 fusion
  211.3 8.2 %copy.25 = bf16[768,3,768]{2,1,0:T(4,128)(2,1)} copy(bf16[768,3,768]{0,2,1:T(8,128)(2,1)} %fusion) | data formatting | bytes 7077888 | tf_op jit(solution)/shard_map/add | solution.py:134
  219.5 10.1 %convert_element_type.47 = bf16[32,24,2304]{2,1,0:T(8,128)(2,1)} reshape(bf16[768,3,768]{2,1,0:T(4,128)(2,1)} %copy.25) | data formatting | bytes 7077888 | tf_op jit(solution)/shard_map/convert_element_type | solution.py:142
  229.6 5.7 %all-to-all-start = ((bf16[32,24,2304]{2,1,0:T(8,128)(2,1)}), bf16[32,24,2304]{2,1,0:T(8,128)(2,1)}, u32[]{:S(2)}, u32[]{:S(2)}) async-start(bf16[32,24,2304]{2,1,0:T(8,128)(2,1)} %convert_element_type.47), calls=%async_computation | async-start | bytes 7077888 | tf_op jit(solution)/shard_map/all_to_all | solution.py:143
  235.4 69.1 %all-to-all-done = bf16[32,24,2304]{2,1,0:T(8,128)(2,1)} async-done(((bf16[32,24,2304]{2,1,0:T(8,128)(2,1)}), bf16[32,24,2304]{2,1,0:T(8,128)(2,1)}, u32[]{:S(2)}, u32[]{:S(2)}) %all-to-all-start) | async-done | bytes 3538976 | tf_op jit(solution)/shard_map/all_to_all | solution.py:143
  304.5 2.5 convert_reduce_fusion
  307.0 0.3 reshape.148
  307.3 1.0 copy.26
  308.3 18.1 %all-to-all-start.1 = ((f32[16,24,144]{2,1,0:T(8,128)}), f32[16,24,144]{2,1,0:T(8,128)S(1)}, u32[]{:S(2)}, u32[]{:S(2)}) async-start(f32[16,24,144]{2,1,0:T(8,128)} %copy.26), calls=%async_computation.1 | async-start | bytes 786432 | tf_op jit(solution)/shard_map/all_to_all | solution.py:147
  326.4 4.9 %fusion.85 = (f32[128]{0:T(128)S(1)}, f32[128,768]{1,0:T(8,128)S(1)}) fusion(f32[2,128,768]{2,1,0:T(8,128)S(1)} %get-tuple-element.6, s32[]{:T(128)S(6)} %min.12, bf16[768,1152]{1,0:T(8,128)(2,1)} %collective-permute-done.2, bf16[768,1152]{1,0:T(8,128)(2,1)} %bitcast.160, pred[]{:T(512)S(6)} %eq.9, bf16[128,768]{1,0:T(8,128)(2,1)S(1)} %get-tuple-element.9, ...), kind=kOutput, calls=%fused_computation.104 | convolution fusion | flops 472645504 | bytes 4915717 | tf_op jit(solution)/shard_map/pj,cj->pc/dot_general | solution.py:102
  331.4 0.2 fusion.107
  331.6 0.0 copy-start.2
  331.6 16.5 %all-to-all-done.1 = f32[16,24,144]{2,1,0:T(8,128)S(1)} async-done(((f32[16,24,144]{2,1,0:T(8,128)}), f32[16,24,144]{2,1,0:T(8,128)S(1)}, u32[]{:S(2)}, u32[]{:S(2)}) %all-to-all-start.1) | async-done | bytes 221216 | tf_op jit(solution)/shard_map/all_to_all | solution.py:147
  348.1 30.4 %all-gather.1 = bf16[16,144,24]{1,2,0:T(8,128)(2,1)S(1)} all-gather(bf16[1,144,24]{1,2,0:T(8,128)(2,1)S(1)} %fusion.111), channel_id=1, replica_groups=mesh['section'=2,'dp'=32,'seq'=16] {'seq'}, dimensions={0}, use_global_device_ids=true | all-gather | bytes 117504 | tf_op jit(solution)/shard_map/all_gather | solution.py:150
  378.6 0.9 reshape.152
  379.5 0.0 copy-done.2
  (19 shorter events, 0.4 us)
Async XLA Ops:
  7.2 0.9 copy-start
  7.2 111.8 %copy-start.1 = (bf16[1,2,128,768]{3,2,1,0:T(8,128)(2,1)S(1)}, bf16[1,2,128,768]{3,2,1,0:T(8,128)(2,1)}, u32[]{:S(2)}) copy-start(bf16[1,2,128,768]{3,2,1,0:T(8,128)(2,1)} %param.3) | copy-start | bytes 1179652
  7.2 103.4 %all-gather.4.cloned.1.call-start = ((), (), s32[]{:S(2)}) async-start(), calls=%async_computation.2 | async-start | bytes 1824768 | tf_op jit(solution)/shard_map/all_gather | solution.py:56
  110.6 15.8 %collective-permute-start.2 = (bf16[768,1152]{1,0:T(8,128)(2,1)}, bf16[768,1152]{1,0:T(8,128)(2,1)}, u32[]{:S(2)}, u32[]{:S(2)}) collective-permute-start(bf16[768,1152]{1,0:T(8,128)(2,1)} %bitcast.158), channel_id=1, source_target_pairs={{0,1},{1,0},{2,3},{3,2},{4,5},{5,4},{6,7},{7,6},{8,9},{9,8},{10,11... | collective-permute-start | bytes 5308424 | tf_op jit(solution)/shard_map/ppermute | solution.py:57
  119.6 5.7 %collective-permute-start = (bf16[2,16,768]{2,1,0:T(8,128)(2,1)S(1)}, bf16[2,16,768]{2,1,0:T(8,128)(2,1)S(1)}, u32[]{:S(2)}, u32[]{:S(2)}) collective-permute-start(bf16[2,16,768]{2,1,0:T(8,128)(2,1)S(1)} %get-tuple-element.21), channel_id=1, source_target_pairs={{1,0},{2,1},{3,2},{4,3},{5,4},{6,5},{7,6},{8,7},{9,8},{10,9},{11,1... | collective-permute-start | bytes 147464 | tf_op jit(solution)/shard_map/ppermute | solution.py:17
  121.5 4.8 %collective-permute-start.1 = (bf16[2,16,768]{2,1,0:T(8,128)(2,1)S(1)}, bf16[2,16,768]{2,1,0:T(8,128)(2,1)S(1)}, u32[]{:S(2)}, u32[]{:S(2)}) collective-permute-start(bf16[2,16,768]{2,1,0:T(8,128)(2,1)S(1)} %get-tuple-element.22), channel_id=1, source_target_pairs={{0,1},{1,2},{2,3},{3,4},{4,5},{5,6},{6,7},{7,8},{8,9},{9,10},{10,1... | collective-permute-start | bytes 147464 | tf_op jit(solution)/shard_map/ppermute | solution.py:16
  131.6 16.8 %collective-permute-start.3 = (bf16[128,768]{1,0:T(8,128)(2,1)S(1)}, bf16[128,768]{1,0:T(8,128)(2,1)S(1)}, u32[]{:S(2)}, u32[]{:S(2)}) collective-permute-start(bf16[128,768]{1,0:T(8,128)(2,1)S(1)} %get-tuple-element.5), channel_id=1, source_target_pairs={{512,0},{513,1},{514,2},{515,3},{516,4},{517,5},{518,6},{519,7},{5... | collective-permute-start | bytes 589832 | tf_op jit(solution)/shard_map/ppermute | solution.py:25
  133.3 35.2 %copy-start.3 = (bf16[1,768,1152]{2,1,0:T(8,128)(2,1)S(1)}, bf16[1,768,1152]{2,1,0:T(8,128)(2,1)}, u32[]{:S(2)}) copy-start(bf16[1,768,1152]{2,1,0:T(8,128)(2,1)} %all-gather.4.cloned.1.call-done) | copy-start | bytes 5308420
  148.4 18.9 %collective-permute-start.4 = (bf16[2,16,768]{2,1,0:T(8,128)(2,1)S(1)}, bf16[2,16,768]{2,1,0:T(8,128)(2,1)S(1)}, u32[]{:S(2)}, u32[]{:S(2)}) collective-permute-start(bf16[2,16,768]{2,1,0:T(8,128)(2,1)S(1)} %get-tuple-element.17), channel_id=1, source_target_pairs={{1,0},{2,1},{3,2},{4,3},{5,4},{6,5},{7,6},{8,7},{9,8},{10,9},{11,1... | collective-permute-start | bytes 147464 | tf_op jit(solution)/shard_map/ppermute | solution.py:17
  150.3 18.1 %collective-permute-start.5 = (bf16[2,16,768]{2,1,0:T(8,128)(2,1)S(1)}, bf16[2,16,768]{2,1,0:T(8,128)(2,1)S(1)}, u32[]{:S(2)}, u32[]{:S(2)}) collective-permute-start(bf16[2,16,768]{2,1,0:T(8,128)(2,1)S(1)} %get-tuple-element.18), channel_id=1, source_target_pairs={{0,1},{1,2},{2,3},{3,4},{4,5},{5,6},{6,7},{7,8},{8,9},{9,10},{10,1... | collective-permute-start | bytes 147464 | tf_op jit(solution)/shard_map/ppermute | solution.py:16
  172.5 15.3 %collective-permute-start.6 = (bf16[128,768]{1,0:T(8,128)(2,1)S(1)}, bf16[128,768]{1,0:T(8,128)(2,1)S(1)}, u32[]{:S(2)}, u32[]{:S(2)}) collective-permute-start(bf16[128,768]{1,0:T(8,128)(2,1)S(1)} %get-tuple-element.3), channel_id=1, source_target_pairs={{512,0},{513,1},{514,2},{515,3},{516,4},{517,5},{518,6},{519,7},{5... | collective-permute-start | bytes 589832 | tf_op jit(solution)/shard_map/ppermute | solution.py:25
  187.9 20.3 %collective-permute-start.7 = (bf16[2,16,768]{2,1,0:T(8,128)(2,1)S(1)}, bf16[2,16,768]{2,1,0:T(8,128)(2,1)S(1)}, u32[]{:S(2)}, u32[]{:S(2)}) collective-permute-start(bf16[2,16,768]{2,1,0:T(8,128)(2,1)S(1)} %get-tuple-element.10), channel_id=1, source_target_pairs={{1,0},{2,1},{3,2},{4,3},{5,4},{6,5},{7,6},{8,7},{9,8},{10,9},{11,1... | collective-permute-start | bytes 147464 | tf_op jit(solution)/shard_map/ppermute | solution.py:17
  189.8 18.4 %collective-permute-start.8 = (bf16[2,16,768]{2,1,0:T(8,128)(2,1)S(1)}, bf16[2,16,768]{2,1,0:T(8,128)(2,1)S(1)}, u32[]{:S(2)}, u32[]{:S(2)}) collective-permute-start(bf16[2,16,768]{2,1,0:T(8,128)(2,1)S(1)} %get-tuple-element.11), channel_id=1, source_target_pairs={{0,1},{1,2},{2,3},{3,4},{4,5},{5,6},{6,7},{7,8},{8,9},{9,10},{10,1... | collective-permute-start | bytes 147464 | tf_op jit(solution)/shard_map/ppermute | solution.py:16
  229.6 74.9 %all-to-all-start = ((bf16[32,24,2304]{2,1,0:T(8,128)(2,1)}), bf16[32,24,2304]{2,1,0:T(8,128)(2,1)}, u32[]{:S(2)}, u32[]{:S(2)}) async-start(bf16[32,24,2304]{2,1,0:T(8,128)(2,1)} %convert_element_type.47), calls=%async_computation | async-start | bytes 7077888 | tf_op jit(solution)/shard_map/all_to_all | solution.py:143
  308.3 39.8 %all-to-all-start.1 = ((f32[16,24,144]{2,1,0:T(8,128)}), f32[16,24,144]{2,1,0:T(8,128)S(1)}, u32[]{:S(2)}, u32[]{:S(2)}) async-start(f32[16,24,144]{2,1,0:T(8,128)} %copy.26), calls=%async_computation.1 | async-start | bytes 786432 | tf_op jit(solution)/shard_map/all_to_all | solution.py:147
  331.6 47.9 %copy-start.2 = (bf16[1,2,128,768]{3,2,1,0:T(8,128)(2,1)}, bf16[1,2,128,768]{3,2,1,0:T(8,128)(2,1)S(1)}, u32[]{:S(2)}) copy-start(bf16[1,2,128,768]{3,2,1,0:T(8,128)(2,1)S(1)} %fusion.107) | copy-start | bytes 1179652
Sparse Core Ops, SparseCore 0:
  12.9 97.6 all-gather.3

commit v3 on v0

--- a/solution.py
+++ b/solution.py
@@ -1,9 +1,10 @@
 import jax
 import jax.numpy as jnp
 from jax import lax
-from jax.sharding import PartitionSpec as P
+from jax.sharding import Mesh, PartitionSpec as P
 
 DILATION_STEP = 16
+SEQ_AXES = ("zl", "core")
 
 
 def with_halo(array, sides, width):
@@ -49,7 +50,8 @@
     batch_rows = saved_inputs.shape[2]
     channel_width = weights.shape[2] // 3
     dilation_amount = DILATION_STEP
-    full_kernel = lax.all_gather(weights[0], "dp", axis=0, tiled=True)
+    full_kernel = lax.all_gather(weights[0], "y", axis=0, tiled=True)
+    full_kernel = lax.all_gather(full_kernel, "x", axis=0, tiled=True)
     value_rows = saved_inputs[0].astype(jnp.float32)
     norm_scale = lax.rsqrt(jnp.mean(value_rows * value_rows, axis=-1, keepdims=True) + 1e-05)
     normalized_input = value_rows * norm_scale
@@ -69,7 +71,7 @@
         stacked_rows = jnp.stack(
             [select_position(layer_activation, position_index), cotangent_state], axis=0
         )
-        paired_widened = with_halo(stacked_rows, (("seq", 1),), dilation_amount)
+        paired_widened = with_halo(stacked_rows, ((SEQ_AXES, 1),), dilation_amount)
         activation_widened = paired_widened[0]
         cotangent_widened = paired_widened[1]
         current_act = select_position(activation_widened_full, position_index)
@@ -126,15 +128,41 @@
         )
         if step_index < micro_batch:
             incoming = from_behind(block_output, "section", -1)
-    owned = lax.psum_scatter(
-        grad_total.astype(jnp.bfloat16), "dp", scatter_dimension=0, tiled=True
-    ).astype(jnp.float32)
-    summed = lax.psum(owned, "seq")
-    weight_grad = (summed / (micro_batch * lax.axis_size("dp"))).astype(jnp.bfloat16)
+    n_x = lax.axis_size("x")
+    n_y = lax.axis_size("y")
+    n_zl = lax.axis_size("zl")
+    n_core = lax.axis_size("core")
+    owned_rows = channel_width // (n_x * n_y)
+    columns = 3 * channel_width
+    pieces = grad_total.astype(jnp.bfloat16).reshape(n_x, n_y * owned_rows, columns)
+    received = lax.all_to_all(pieces, "x", 0, 0, tiled=True)
+    row_group = jnp.sum(received.astype(jnp.float32), axis=0).reshape(n_y, owned_rows, columns)
+    received = lax.all_to_all(row_group, "y", 0, 0, tiled=True)
+    owned = jnp.sum(received, axis=0)
+    half = columns // n_core
+    owned = owned.reshape(owned_rows, n_core, half).transpose(1, 0, 2)
+    owned = jnp.sum(lax.all_to_all(owned, "core", 0, 0, tiled=True), axis=0)
+    chunk = half // n_zl
+    owned = owned.reshape(owned_rows, n_zl, chunk).transpose(1, 0, 2)
+    summed = jnp.sum(lax.all_to_all(owned, "zl", 0, 0, tiled=True), axis=0)
+    chunk_grad = (summed / (micro_batch * n_x * n_y)).astype(jnp.bfloat16)
+    weight_grad = lax.all_gather(chunk_grad, "zl", axis=1, tiled=True)
+    weight_grad = lax.all_gather(weight_grad, "core", axis=1, tiled=True)
     return (results[None], weight_grad[None])
 
 
+def split_mesh(mesh):
+    dp_devices = mesh.devices[0, :, 0]
+    n_x = len({device.coords[0] for device in dp_devices})
+    n_core = len({device.core_on_chip for device in mesh.devices[0, 0, :]})
+    n_section, n_dp, n_seq = mesh.devices.shape
+    shape = (n_section, n_x, n_dp // n_x, n_seq // n_core, n_core)
+    return Mesh(mesh.devices.reshape(shape), ("section", "x", "y", "zl", "core"))
+
+
 def solution(mesh):
-    in_specs = (P("section", "dp", "seq", None), P("dp", "seq", None), P("section", "dp", None))
-    out_specs = (P("section", "dp", "seq", None), P("section", "dp", None))
-    return jax.shard_map(local, mesh=mesh, in_specs=in_specs, out_specs=out_specs, check_vma=False)
+    fine = split_mesh(mesh)
+    dp, seq = ("x", "y"), SEQ_AXES
+    in_specs = (P("section", dp, seq, None), P(dp, seq, None), P("section", dp, None))
+    out_specs = (P("section", dp, seq, None), P("section", dp, None))
+    return jax.shard_map(local, mesh=fine, in_specs=in_specs, out_specs=out_specs, check_vma=False)

time: 523 us -> 370 us (0.71); the launches traced: 516 us -> 369 us
  waiting for transfers between devices: 324 us -> 109 us
  starting transfers between devices: 59.5 us -> 98.6 us
  blocking collectives: 92.3 us -> 110 us
  local copies, waits for them, and re-layouts: 6.57 us -> 17.9 us
    reduce_scatter x1 -> x0, waiting for transfers between devices: 209 us -> none  [local(): lax.psum_scatter(grad_total.astype(jnp.bfloat16), 'dp', scatter_dimension...]
    psum x1 -> x0, blocking collectives: 92.3 us -> none  [local(): summed = lax.psum(owned, 'seq')]
    all_gather x0 -> x3, blocking collectives: none -> 75.9 us  [the longest x1 39.9 us: local(): weight_grad = lax.all_gather(chunk_grad, 'zl', axis=1, tiled=True)]
    all_gather x1, waiting for transfers between devices: 84.8 us -> 41.7 us  [local(): full_kernel = lax.all_gather(full_kernel, 'x', axis=0, tiled=True)]
    all_to_all x0 -> x2, waiting for transfers between devices: none -> 37.2 us  [the longest x1 26.2 us: local(): received = lax.all_to_all(row_group, 'y', 0, 0, tiled=True)]
    all_to_all x0 -> x2, starting transfers between devices: none -> 36.5 us  [the longest x1 29.6 us: local(): summed = jnp.sum(lax.all_to_all(owned, 'zl', 0, 0, tiled=True), axis=0)]
    all_to_all x0 -> x2, blocking collectives: none -> 34.3 us  [the longest x1 30.6 us: local(): received = lax.all_to_all(pieces, 'x', 0, 0, tiled=True)]
    convert_element_type x1 -> x2, local copies, waits for them, and re-layouts: 5.79 us -> 12.1 us  [local(): grad_total.astype(jnp.bfloat16).reshape(n_x, n_y * owned_rows, columns)]
  transfers between devices with their start and end apart: 10 -> 11, of which waited for: 6 -> 7; matrix products, arithmetic and copies ran while one was open for 2% -> 2% of each run, Pallas kernels for 0% -> 0%
where the time goes in v3:
time: 370 us; the launch traced here: 369 us
  blocking collectives  110 us (30%)
  waiting for transfers between devices  109 us (29%)
  starting transfers between devices  98.6 us (27%)
  local copies, waits for them, and re-layouts  17.9 us (5%)
  matrix products  15 us (4%)
  between operations  14.6 us (4%)
    all_gather x1, waiting for transfers between devices, local(): full_kernel = lax.all_gather(full_kernel, 'x', axis=0, tiled=True)  41.7 us
    all_gather x1, blocking collectives, local(): weight_grad = lax.all_gather(chunk_grad, 'zl', axis=1, tiled=True)  39.9 us
    ppermute x3, starting transfers between devices, with_halo(): before = lax.ppermute(last, axis, up)  34.3 us
    all_to_all x1, blocking collectives, local(): received = lax.all_to_all(pieces, 'x', 0, 0, tiled=True)  30.6 us
    all_to_all x1, starting transfers between devices, local(): summed = jnp.sum(lax.all_to_all(owned, 'zl', 0, 0, tiled=True), axis=0)  29.6 us
    ppermute x2, waiting for transfers between devices, from_behind(): lax.ppermute(value, axis, [(source, source + steps) for source in range(i...  28.3 us
    all_to_all x1, waiting for transfers between devices, local(): received = lax.all_to_all(row_group, 'y', 0, 0, tiled=True)  26.2 us
    ppermute x3, starting transfers between devices, with_halo(): after = lax.ppermute(initial, axis, down)  25.2 us
  transfers between devices with their start and end apart: 11, of which 7 were waited for; matrix products, arithmetic and copies ran while one was open for 2% of the time, Pallas kernels for 0%

profile of v3, /device:TPU:1, one launch (start us, length us, event | category | flops | bytes accessed | tf_op | source)
XLA Modules:
  0.0 368.8 jit_solution(4894906253330665970)
XLA Ops:
  7.2 0.0 all-gather.5.cloned.1.call-start
  7.2 24.6 %all-gather = bf16[1,192,2304]{2,1,0:T(8,128)(2,1)} all-gather(bf16[1,24,2304]{2,1,0:T(8,128)(2,1)} %param.5), channel_id=2, replica_groups=mesh['section'=2,'x'=4,'y'=8,'zl'=8,'core'=2] {'y'}, dimensions={1}, use_global_device_ids=true | all-gather | bytes 995328 | tf_op jit(solution)/shard_map/all_gather | solution.py:53
  31.8 0.0 all-gather.5.cloned.1.call-update
  31.9 0.1 broadcast_in_dim.45
  32.0 0.1 select_n.113
  32.1 0.7 copy-done.9
  32.8 0.2 fusion.22
  32.9 0.4 convert_multiply_fusion
  33.3 0.1 constant_dynamic-slice_fusion
  33.4 19.7 %collective-permute-start = (bf16[2,16,768]{2,1,0:T(8,128)(2,1)S(1)}, bf16[2,16,768]{2,1,0:T(8,128)(2,1)S(1)}, u32[]{:S(2)}, u32[]{:S(2)}) collective-permute-start(bf16[2,16,768]{2,1,0:T(8,128)(2,1)S(1)} %get-tuple-element.21), channel_id=1, source_target_pairs={{1,0},{2,1},{3,2},{4,3},{5,4},{6,5},{7,6},{8,7},{9,8},{10,9},{11,1... | collective-permute-start | bytes 147464 | tf_op jit(solution)/shard_map/ppermute | solution.py:18
  53.1 1.9 collective-permute-start.1
  55.0 0.1 select_n.112
  55.1 0.0 collective-permute-done
  55.1 1.1 collective-permute-done.1
  56.2 41.7 %all-gather.5.cloned.1.call-done = bf16[1,768,2304]{2,1,0:T(8,128)(2,1)} async-done(((bf16[1,192,2304]{2,1,0:T(8,128)(2,1)}), bf16[1,768,2304]{2,1,0:T(8,128)(2,1)}) %all-gather.5.cloned.1.call-update) | async-done | bytes 3538960 | tf_op jit(solution)/shard_map/all_gather | solution.py:54
  97.9 3.4 fusion.114
  101.3 0.2 bitcast_dynamic-update-slice_fusion.1
  101.5 1.3 collective-permute-start.2
  102.8 0.1 broadcast_in_dim.51
  103.0 0.1 mul.311
  103.0 0.1 broadcast_in_dim.48
  103.2 0.1 mul.289
  103.2 15.4 %collective-permute-done.2 = bf16[128,768]{1,0:T(8,128)(2,1)S(1)} collective-permute-done((bf16[128,768]{1,0:T(8,128)(2,1)S(1)}, bf16[128,768]{1,0:T(8,128)(2,1)S(1)}, u32[]{:S(2)}, u32[]{:S(2)}) %collective-permute-start.2) | collective-permute-done | bytes 196640 | tf_op jit(solution)/shard_map/ppermute | solution.py:26
  118.7 3.6 collective-permute-start.3
  122.3 14.9 %collective-permute-start.4 = (bf16[2,16,768]{2,1,0:T(8,128)(2,1)S(1)}, bf16[2,16,768]{2,1,0:T(8,128)(2,1)S(1)}, u32[]{:S(2)}, u32[]{:S(2)}) collective-permute-start(bf16[2,16,768]{2,1,0:T(8,128)(2,1)S(1)} %get-tuple-element.18), channel_id=1, source_target_pairs={{0,1},{1,2},{2,3},{3,4},{4,5},{5,6},{6,7},{7,8},{8,9},{9,10},{10,1... | collective-permute-start | bytes 147464 | tf_op jit(solution)/shard_map/ppermute | solution.py:17
  137.3 1.1 collective-permute-done.4
  138.4 3.4 fusion.107
  141.9 0.2 bitcast_dynamic-update-slice_fusion
  142.1 0.0 copy-start.2
  142.1 1.3 collective-permute-start.5
  143.4 1.1 fusion.31
  144.5 12.9 %collective-permute-done.5 = bf16[128,768]{1,0:T(8,128)(2,1)S(1)} collective-permute-done((bf16[128,768]{1,0:T(8,128)(2,1)S(1)}, bf16[128,768]{1,0:T(8,128)(2,1)S(1)}, u32[]{:S(2)}, u32[]{:S(2)}) %collective-permute-start.5) | collective-permute-done | bytes 196640 | tf_op jit(solution)/shard_map/ppermute | solution.py:26
  157.5 1.9 collective-permute-start.6
  159.4 17.4 %collective-permute-start.7 = (bf16[2,16,768]{2,1,0:T(8,128)(2,1)S(1)}, bf16[2,16,768]{2,1,0:T(8,128)(2,1)S(1)}, u32[]{:S(2)}, u32[]{:S(2)}) collective-permute-start(bf16[2,16,768]{2,1,0:T(8,128)(2,1)S(1)} %get-tuple-element.11), channel_id=1, source_target_pairs={{0,1},{1,2},{2,3},{3,4},{4,5},{5,6},{6,7},{7,8},{8,9},{9,10},{10,1... | collective-permute-start | bytes 147464 | tf_op jit(solution)/shard_map/ppermute | solution.py:17
  176.9 1.1 fusion.38
  178.0 0.0 collective-permute-done.6
  178.0 0.0 copy-start.14
  178.0 0.0 collective-permute-done.7
  178.0 0.6 copy-done.14
  178.6 0.6 copy-done.16
  179.2 1.9 fusion
  181.1 5.5 %reshape.164 = bf16[4,192,2304]{1,0,2:T(4,128)(2,1)} reshape(bf16[768,3,768]{0,2,1:T(8,128)(2,1)S(1)} %fusion) | data formatting | bytes 7077888 | tf_op jit(solution)/shard_map/convert_element_type | solution.py:137
  186.6 6.7 %copy.42 = bf16[4,192,2304]{2,1,0:T(8,128)(2,1)S(1)} copy(bf16[4,192,2304]{1,0,2:T(4,128)(2,1)} %reshape.164) | data formatting | bytes 7077888 | tf_op jit(solution)/shard_map/convert_element_type | solution.py:137
  193.3 30.6 %all_to_all.20 = bf16[4,192,2304]{2,1,0:T(8,128)(2,1)S(1)} all-to-all(bf16[4,192,2304]{2,1,0:T(8,128)(2,1)S(1)} %copy.42), channel_id=1, replica_groups=mesh['section'=2,'x'=4,'y'=8,'zl'=8,'core'=2] {'x'}, dimensions={0} | all-to-all | bytes 7077888 | tf_op jit(solution)/shard_map/all_to_all | solution.py:138
  223.9 1.7 convert_reduce_fusion
  225.7 6.9 %all-to-all-start.1 = ((f32[8,24,2304]{2,1,0:T(8,128)}), f32[8,24,2304]{2,1,0:T(8,128)S(1)}, u32[]{:S(2)}, u32[]{:S(2)}) async-start(f32[8,24,2304]{2,1,0:T(8,128)} %bitcast.30), calls=%async_computation.1 | async-start | bytes 3538944 | tf_op jit(solution)/shard_map/all_to_all | solution.py:140
  232.6 0.7 copy.45
  233.4 0.5 copy-done.1
  233.8 4.1 %fusion.100 = (f32[128]{0:T(128)S(1)}, f32[128,768]{1,0:T(8,128)}) fusion(f32[2,128,768]{2,1,0:T(8,128)S(1)} %copy-done.1, s32[]{:T(128)S(6)} %min.12, bf16[1,768,2304]{2,1,0:T(8,128)(2,1)} %all-gather.5.cloned.1.call-done, bf16[128,768]{1,0:T(8,128)(2,1)S(1)} %get-tuple-element.9, bf16[128,768]{1,0:T(8,128)(2,1)S(1)} %copy-done.5, ...), kind=kOutput, calls=%fused_computation.109 | convolution fusion | flops 456720256 | bytes 4915716 | tf_op jit(solution)/shard_map/pj,cj->pc/dot_general | solution.py:94
  237.9 26.2 %all-to-all-done.1 = f32[8,24,2304]{2,1,0:T(8,128)S(1)} async-done(((f32[8,24,2304]{2,1,0:T(8,128)}), f32[8,24,2304]{2,1,0:T(8,128)S(1)}, u32[]{:S(2)}, u32[]{:S(2)}) %all-to-all-start.1) | async-done | bytes 1769504 | tf_op jit(solution)/shard_map/all_to_all | solution.py:140
  264.1 0.1 reduce_sum.77
  264.2 0.1 reshape.154
  264.3 0.0 copy-start.11
  264.3 3.7 all_to_all.21
  268.0 0.1 reshape.155
  268.2 0.7 copy.34
  268.9 29.6 %all-to-all-start.3 = ((f32[8,24,144]{2,1,0:T(8,128)}), f32[8,24,144]{2,1,0:T(8,128)S(1)}, u32[]{:S(2)}, u32[]{:S(2)}) async-start(f32[8,24,144]{2,1,0:T(8,128)} %copy.34), calls=%async_computation.3 | async-start | bytes 393216 | tf_op jit(solution)/shard_map/all_to_all | solution.py:147
  298.5 0.2 fusion.122
  298.7 0.0 copy-start.12
  298.7 11.1 %all-to-all-done.3 = f32[8,24,144]{2,1,0:T(8,128)S(1)} async-done(((f32[8,24,144]{2,1,0:T(8,128)}), f32[8,24,144]{2,1,0:T(8,128)S(1)}, u32[]{:S(2)}, u32[]{:S(2)}) %all-to-all-start.3) | async-done | bytes 110624 | tf_op jit(solution)/shard_map/all_to_all | solution.py:147
  309.8 39.9 %all-gather.2 = bf16[8,144,24]{1,2,0:T(8,128)(2,1)S(1)} all-gather(bf16[1,144,24]{1,2,0:T(8,128)(2,1)S(1)} %fusion.126), channel_id=1, replica_groups=mesh['section'=2,'x'=4,'y'=8,'zl'=8,'core'=2] {'zl'}, dimensions={0}, use_global_device_ids=true | all-gather | bytes 62208 | tf_op jit(solution)/shard_map/all_gather | solution.py:149
  349.8 0.2 reshape.160
  349.9 11.4 %all_gather.15 = bf16[24,2304]{1,0:T(8,128)(2,1)S(1)} all-gather(bf16[24,1152]{1,0:T(8,128)(2,1)S(1)} %bitcast.180), channel_id=1, replica_groups=mesh['section'=2,'x'=4,'y'=8,'zl'=8,'core'=2] {'core'}, dimensions={1}, use_global_device_ids=true | all-gather | bytes 165888 | tf_op jit(solution)/shard_map/all_gather | solution.py:150
  361.3 0.6 copy.47
  (50 shorter events, 0.4 us)
Async XLA Ops:
  7.2 24.6 %copy-start.10 = (bf16[2,64,768]{2,1,0:T(8,128)(2,1)S(1)}, bf16[2,64,768]{2,1,0:T(8,128)(2,1)}, u32[]{:S(2)}) copy-start(bf16[2,64,768]{2,1,0:T(8,128)(2,1)} %param.4) | copy-start | bytes 589828
  7.2 90.7 %all-gather.5.cloned.1.call-start = ((), (), s32[]{:S(2)}) async-start(), calls=%async_computation.4 | async-start | bytes 4423680 | tf_op jit(solution)/shard_map/all_gather | solution.py:54
  31.8 1.0 copy-start.9
  33.3 108.6 %copy-start = (f32[2,128,768]{2,1,0:T(8,128)}, f32[2,128,768]{2,1,0:T(8,128)S(1)}, u32[]{:S(2)}) copy-start(f32[2,128,768]{2,1,0:T(8,128)S(1)} %get-tuple-element.6) | copy-start | bytes 2359300
  33.4 124.1 %copy-start.6 = (bf16[1,128,768]{2,1,0:T(8,128)(2,1)}, bf16[1,128,768]{2,1,0:T(8,128)(2,1)S(1)}, u32[]{:S(2)}) copy-start(bf16[1,128,768]{2,1,0:T(8,128)(2,1)S(1)} %get-tuple-element.12) | copy-start | bytes 589828
  33.4 21.7 %collective-permute-start = (bf16[2,16,768]{2,1,0:T(8,128)(2,1)S(1)}, bf16[2,16,768]{2,1,0:T(8,128)(2,1)S(1)}, u32[]{:S(2)}, u32[]{:S(2)}) collective-permute-start(bf16[2,16,768]{2,1,0:T(8,128)(2,1)S(1)} %get-tuple-element.21), channel_id=1, source_target_pairs={{1,0},{2,1},{3,2},{4,3},{5,4},{6,5},{7,6},{8,7},{9,8},{10,9},{11,1... | collective-permute-start | bytes 147464 | tf_op jit(solution)/shard_map/ppermute | solution.py:18
  53.1 3.1 collective-permute-start.1
  101.5 17.1 %collective-permute-start.2 = (bf16[128,768]{1,0:T(8,128)(2,1)S(1)}, bf16[128,768]{1,0:T(8,128)(2,1)S(1)}, u32[]{:S(2)}, u32[]{:S(2)}) collective-permute-start(bf16[128,768]{1,0:T(8,128)(2,1)S(1)} %get-tuple-element.5), channel_id=1, source_target_pairs={{512,0},{513,1},{514,2},{515,3},{516,4},{517,5},{518,6},{519,7},{5... | collective-permute-start | bytes 589832 | tf_op jit(solution)/shard_map/ppermute | solution.py:26
  118.7 18.6 %collective-permute-start.3 = (bf16[2,16,768]{2,1,0:T(8,128)(2,1)S(1)}, bf16[2,16,768]{2,1,0:T(8,128)(2,1)S(1)}, u32[]{:S(2)}, u32[]{:S(2)}) collective-permute-start(bf16[2,16,768]{2,1,0:T(8,128)(2,1)S(1)} %get-tuple-element.17), channel_id=1, source_target_pairs={{1,0},{2,1},{3,2},{4,3},{5,4},{6,5},{7,6},{8,7},{9,8},{10,9},{11,1... | collective-permute-start | bytes 147464 | tf_op jit(solution)/shard_map/ppermute | solution.py:18
  122.3 16.1 %collective-permute-start.4 = (bf16[2,16,768]{2,1,0:T(8,128)(2,1)S(1)}, bf16[2,16,768]{2,1,0:T(8,128)(2,1)S(1)}, u32[]{:S(2)}, u32[]{:S(2)}) collective-permute-start(bf16[2,16,768]{2,1,0:T(8,128)(2,1)S(1)} %get-tuple-element.18), channel_id=1, source_target_pairs={{0,1},{1,2},{2,3},{3,4},{4,5},{5,6},{6,7},{7,8},{8,9},{9,10},{10,1... | collective-permute-start | bytes 147464 | tf_op jit(solution)/shard_map/ppermute | solution.py:17
  142.1 2.4 copy-start.2
  142.1 15.3 %collective-permute-start.5 = (bf16[128,768]{1,0:T(8,128)(2,1)S(1)}, bf16[128,768]{1,0:T(8,128)(2,1)S(1)}, u32[]{:S(2)}, u32[]{:S(2)}) collective-permute-start(bf16[128,768]{1,0:T(8,128)(2,1)S(1)} %get-tuple-element.3), channel_id=1, source_target_pairs={{512,0},{513,1},{514,2},{515,3},{516,4},{517,5},{518,6},{519,7},{5... | collective-permute-start | bytes 589832 | tf_op jit(solution)/shard_map/ppermute | solution.py:26
  157.5 20.6 %copy-start.4 = (bf16[128,768]{1,0:T(8,128)(2,1)}, bf16[128,768]{1,0:T(8,128)(2,1)S(1)}, u32[]{:S(2)}) copy-start(bf16[128,768]{1,0:T(8,128)(2,1)S(1)} %broadcast_select_fusion) | copy-start | bytes 589828
  157.5 20.5 %collective-permute-start.6 = (bf16[2,16,768]{2,1,0:T(8,128)(2,1)S(1)}, bf16[2,16,768]{2,1,0:T(8,128)(2,1)S(1)}, u32[]{:S(2)}, u32[]{:S(2)}) collective-permute-start(bf16[2,16,768]{2,1,0:T(8,128)(2,1)S(1)} %get-tuple-element.10), channel_id=1, source_target_pairs={{1,0},{2,1},{3,2},{4,3},{5,4},{6,5},{7,6},{8,7},{9,8},{10,9},{11,1... | collective-permute-start | bytes 147464 | tf_op jit(solution)/shard_map/ppermute | solution.py:18
  159.4 19.8 %copy-start.7 = (bf16[1,128,768]{2,1,0:T(8,128)(2,1)S(1)}, bf16[1,128,768]{2,1,0:T(8,128)(2,1)}, u32[]{:S(2)}) copy-start(bf16[1,128,768]{2,1,0:T(8,128)(2,1)} %copy-done.6) | copy-start | bytes 589828
  159.4 18.6 %collective-permute-start.7 = (bf16[2,16,768]{2,1,0:T(8,128)(2,1)S(1)}, bf16[2,16,768]{2,1,0:T(8,128)(2,1)S(1)}, u32[]{:S(2)}, u32[]{:S(2)}) collective-permute-start(bf16[2,16,768]{2,1,0:T(8,128)(2,1)S(1)} %get-tuple-element.11), channel_id=1, source_target_pairs={{0,1},{1,2},{2,3},{3,4},{4,5},{5,6},{6,7},{7,8},{8,9},{9,10},{10,1... | collective-permute-start | bytes 147464 | tf_op jit(solution)/shard_map/ppermute | solution.py:17
  178.0 0.6 copy-start.14
  178.6 0.6 copy-start.16
  225.6 6.9 %copy-start.3 = (bf16[2,128,768]{2,1,0:T(8,128)(2,1)S(1)}, bf16[2,128,768]{2,1,0:T(8,128)(2,1)}, u32[]{:S(2)}) copy-start(bf16[2,128,768]{2,1,0:T(8,128)(2,1)} %copy-done.2) | copy-start | bytes 1179652
  225.6 7.7 %copy-start.5 = (bf16[128,768]{1,0:T(8,128)(2,1)S(1)}, bf16[128,768]{1,0:T(8,128)(2,1)}, u32[]{:S(2)}) copy-start(bf16[128,768]{1,0:T(8,128)(2,1)} %copy-done.4) | copy-start | bytes 589828
  225.6 7.7 %copy-start.8 = (bf16[1,128,768]{2,1,0:T(8,128)(2,1)S(1)}, bf16[1,128,768]{2,1,0:T(8,128)(2,1)}, u32[]{:S(2)}) copy-start(bf16[1,128,768]{2,1,0:T(8,128)(2,1)} %copy-done.6) | copy-start | bytes 589828
  225.6 7.7 %copy-start.15 = (bf16[2,16,768]{2,1,0:T(8,128)(2,1)S(1)}, bf16[2,16,768]{2,1,0:T(8,128)(2,1)}, u32[]{:S(2)}) copy-start(bf16[2,16,768]{2,1,0:T(8,128)(2,1)} %copy-done.14) | copy-start | bytes 147460
  225.7 7.7 %copy-start.17 = (bf16[2,16,768]{2,1,0:T(8,128)(2,1)S(1)}, bf16[2,16,768]{2,1,0:T(8,128)(2,1)}, u32[]{:S(2)}) copy-start(bf16[2,16,768]{2,1,0:T(8,128)(2,1)} %copy-done.16) | copy-start | bytes 147460
  225.7 38.4 %all-to-all-start.1 = ((f32[8,24,2304]{2,1,0:T(8,128)}), f32[8,24,2304]{2,1,0:T(8,128)S(1)}, u32[]{:S(2)}, u32[]{:S(2)}) async-start(f32[8,24,2304]{2,1,0:T(8,128)} %bitcast.30), calls=%async_computation.1 | async-start | bytes 3538944 | tf_op jit(solution)/shard_map/all_to_all | solution.py:140
  232.6 1.3 copy-start.1
  264.3 34.2 %copy-start.11 = (bf16[1,2,128,768]{3,2,1,0:T(8,128)(2,1)S(1)}, bf16[1,2,128,768]{3,2,1,0:T(8,128)(2,1)}, u32[]{:S(2)}) copy-start(bf16[1,2,128,768]{3,2,1,0:T(8,128)(2,1)} %copy.45) | copy-start | bytes 1179652
  264.3 34.2 %copy-start.13 = (f32[128,768]{1,0:T(8,128)S(1)}, f32[128,768]{1,0:T(8,128)}, u32[]{:S(2)}) copy-start(f32[128,768]{1,0:T(8,128)} %get-tuple-element.34) | copy-start | bytes 1179652
  268.9 40.9 %all-to-all-start.3 = ((f32[8,24,144]{2,1,0:T(8,128)}), f32[8,24,144]{2,1,0:T(8,128)S(1)}, u32[]{:S(2)}, u32[]{:S(2)}) async-start(f32[8,24,144]{2,1,0:T(8,128)} %copy.34), calls=%async_computation.3 | async-start | bytes 393216 | tf_op jit(solution)/shard_map/all_to_all | solution.py:147
  298.7 63.3 %copy-start.12 = (bf16[1,2,128,768]{3,2,1,0:T(8,128)(2,1)}, bf16[1,2,128,768]{3,2,1,0:T(8,128)(2,1)S(1)}, u32[]{:S(2)}) copy-start(bf16[1,2,128,768]{3,2,1,0:T(8,128)(2,1)S(1)} %fusion.122) | copy-start | bytes 1179652
Sparse Core Ops, SparseCore 0:
  31.9 65.9 all-gather.4

commit v4 on v1

v4 whole, which is shorter than its diff:
```python
import jax
import jax.numpy as jnp
from jax import lax
from jax.sharding import Mesh, PartitionSpec as P

DILATION_STEP = 16
SEQ_AXES = ("zl", "core")


def with_halo(array, sides, width):
    for axis, dim in sides:
        count, length = (lax.axis_size(axis), array.shape[dim])
        up = [(i, (i + 1) % count) for i in range(count - 1)]
        down = [(j, i) for i, j in up]
        last = lax.slice_in_dim(array, length - width, length, axis=dim)
        initial = lax.slice_in_dim(array, 0, width, axis=dim)
        before = lax.ppermute(last, axis, up)
        after = lax.ppermute(initial, axis, down)
        array = jnp.concatenate([before, array, after], axis=dim)
    return array


def from_behind(value, axis, steps):
    count = lax.axis_size(axis)
    initial, last = (max(0, -steps), min(count, count - steps))
    return lax.ppermute(value, axis, [(source, source + steps) for source in range(initial, last)])


def gelu_gate(value):
    inner = 0.7978845608 * (value + 0.044715 * value * value * value)
    return 0.5 * value * (1.0 + jnp.tanh(inner))


def gelu_derivative(value):
    inner = 0.7978845608 * (value + 0.044715 * value * value * value)
    tangent = jnp.tanh(inner)
    return 0.5 * (1.0 + tangent) + 0.5 * value * (1.0 - tangent * tangent) * 0.7978845608 * (
        1.0 + 0.134145 * value * value
    )


def select_position(array, position_index):
    return lax.dynamic_index_in_dim(array, position_index, 0, keepdims=False)


def local(saved_inputs, pooled_adjoint, weights):
    section_id = lax.axis_index("section")
    is_last = section_id == lax.axis_size("section") - 1
    batch_rows = saved_inputs.shape[2]
    channel_width = weights.shape[2] // 3
    dilation_amount = DILATION_STEP
    full_kernel = lax.all_gather(weights[0], "y", axis=0, tiled=True)
    full_kernel = lax.all_gather(full_kernel, "x", axis=0, tiled=True)
    value_rows = saved_inputs[0].astype(jnp.float32)
    norm_scale = lax.rsqrt(jnp.mean(value_rows * value_rows, axis=-1, keepdims=True) + 1e-05)
    normalized_input = value_rows * norm_scale
    layer_activation = gelu_gate(normalized_input).astype(jnp.bfloat16)
    slope = gelu_derivative(normalized_input)
    upsampled = jnp.repeat(pooled_adjoint, 2, axis=1) * 0.5
    activation_widened = with_halo(layer_activation, ((SEQ_AXES, 1),), dilation_amount)

    def block(cotangent_state):
        cotangent_widened = with_halo(cotangent_state, ((SEQ_AXES, 1),), dilation_amount)
        cotangent_kernel_taps = jnp.concatenate(
            [
                cotangent_widened[
                    :,
                    (2 - kernel_offset) * dilation_amount : (2 - kernel_offset) * dilation_amount
                    + batch_rows,
                ]
                for kernel_offset in range(3)
            ],
            axis=-1,
        )
        reverse_propagate = jnp.einsum(
            "npj,cj->npc", cotangent_kernel_taps, full_kernel, preferred_element_type=jnp.float32
        )
        derivative_gradient = reverse_propagate * slope
        centered_average = jnp.mean(derivative_gradient * normalized_input, axis=-1, keepdims=True)
        return (
            cotangent_state.astype(jnp.float32)
            + norm_scale * (derivative_gradient - normalized_input * centered_average)
        ).astype(jnp.bfloat16)

    upper_output = block(upsampled)
    incoming = from_behind(upper_output, "section", -1)
    cotangent_state = jnp.where(is_last, upsampled, incoming)
    results = block(cotangent_state)
    activation_kernel_taps = jnp.stack(
        [
            activation_widened[
                :, kernel_offset * dilation_amount : kernel_offset * dilation_amount + batch_rows
            ]
            for kernel_offset in range(3)
        ],
        axis=0,
    )
    grad_total = jnp.einsum(
        "knpc,npo->cko", activation_kernel_taps, cotangent_state, preferred_element_type=jnp.float32
    ).reshape(channel_width, 3 * channel_width)
    micro_batch = saved_inputs.shape[1]
    n_dp = lax.axis_size(("x", "y"))
    n_seq = lax.axis_size(SEQ_AXES)
    owned_rows = channel_width // n_dp
    pieces = grad_total.astype(jnp.bfloat16).reshape(n_dp, owned_rows, 3 * channel_width)
    received = lax.all_to_all(pieces, ("x", "y"), 0, 0, tiled=True)
    owned = jnp.sum(received.astype(jnp.float32), axis=0)
    column_chunk = 3 * channel_width // n_seq
    owned = owned.reshape(owned_rows, n_seq, column_chunk).transpose(1, 0, 2)
    gathered = lax.all_to_all(owned, SEQ_AXES, 0, 0, tiled=True)
    summed = jnp.sum(gathered, axis=0)
    chunk_grad = (summed / (micro_batch * n_dp)).astype(jnp.bfloat16)
    weight_grad = lax.all_gather(chunk_grad, SEQ_AXES, axis=1, tiled=True)
    return (results[None], weight_grad[None])


def split_mesh(mesh):
    dp_devices = mesh.devices[0, :, 0]
    n_x = len({device.coords[0] for device in dp_devices})
    n_core = len({device.core_on_chip for device in mesh.devices[0, 0, :]})
    n_section, n_dp, n_seq = mesh.devices.shape
    shape = (n_section, n_x, n_dp // n_x, n_seq // n_core, n_core)
    return Mesh(mesh.devices.reshape(shape), ("section", "x", "y", "zl", "core"))


def solution(mesh):
    fine = split_mesh(mesh)
    dp, seq = ("x", "y"), SEQ_AXES
    in_specs = (P("section", dp, seq, None), P(dp, seq, None), P("section", dp, None))
    out_specs = (P("section", dp, seq, None), P("section", dp, None))
    return jax.shard_map(local, mesh=fine, in_specs=in_specs, out_specs=out_specs, check_vma=False)
```

time: 370 us -> 346 us (0.935)
  blocking collectives: 30.4 us -> 143 us
  waiting for transfers between devices: 199 us -> 87.8 us
  starting transfers between devices: 82.5 us -> 70.4 us
  local copies, waits for them, and re-layouts: 22.8 us -> 16.8 us
  matrix products: 14.4 us -> 8.93 us
    all_to_all x0 -> x1, blocking collectives: none -> 88.4 us  [local(): received = lax.all_to_all(pieces, ('x', 'y'), 0, 0, tiled=True)]
    all_to_all x2 -> x1, waiting for transfers between devices: 84 us -> 20.6 us  [local(): gathered = lax.all_to_all(owned, SEQ_AXES, 0, 0, tiled=True)]
    all_gather x1, waiting for transfers between devices: 84.8 us -> 42 us  [local(): full_kernel = lax.all_gather(full_kernel, 'x', axis=0, tiled=True)]
    all_gather x1 -> x2, blocking collectives: 30.4 us -> 54.9 us  [the longest x1 30.4 us: local(): weight_grad = lax.all_gather(chunk_grad, SEQ_AXES, axis=1, tiled=True)]
    all_to_all x2 -> x1, starting transfers between devices: 22.9 us -> 10 us  [local(): gathered = lax.all_to_all(owned, SEQ_AXES, 0, 0, tiled=True)]
    ppermute x2 -> x1, waiting for transfers between devices: 27.3 us -> 20 us  [from_behind(): lax.ppermute(value, axis, [(source, source + steps) for source in range(i...]
    add x1 -> x0, local copies, waits for them, and re-layouts: 5.69 us -> none  [local(): grad_total + jnp.where(is_valid, grad_term.reshape(channel_width, 3 * cha...]
    dot_general x6 -> x3, matrix products: 14.4 us -> 8.93 us  [the longest x2 7.79 us: block(): jnp.einsum('npj,cj->npc', cotangent_kernel_taps, full_kernel, preferred_e...]
  transfers between devices with their start and end apart: 11 -> 9, of which waited for: 7 -> 6; matrix products, arithmetic and copies ran while one was open for 3% -> 1% of each run, Pallas kernels for 0% -> 0%
where the time goes in v4:
time: 346 us; the launch traced here: 345 us
  blocking collectives  143 us (41%)
  waiting for transfers between devices  87.8 us (25%)
  starting transfers between devices  70.4 us (20%)
  local copies, waits for them, and re-layouts  16.8 us (5%)
  between operations  14.3 us (4%)
  matrix products  8.93 us (3%)
    all_to_all x1, blocking collectives, local(): received = lax.all_to_all(pieces, ('x', 'y'), 0, 0, tiled=True)  88.4 us
    all_gather x1, waiting for transfers between devices, local(): full_kernel = lax.all_gather(full_kernel, 'x', axis=0, tiled=True)  42 us
    ppermute x3, starting transfers between devices, with_halo(): before = lax.ppermute(last, axis, up)  33.8 us
    all_gather x1, blocking collectives, local(): weight_grad = lax.all_gather(chunk_grad, SEQ_AXES, axis=1, tiled=True)  30.4 us
    ppermute x3, starting transfers between devices, with_halo(): after = lax.ppermute(initial, axis, down)  25.2 us
    all_gather x1, blocking collectives, local(): full_kernel = lax.all_gather(weights[0], 'y', axis=0, tiled=True)  24.6 us
    all_to_all x1, waiting for transfers between devices, local(): gathered = lax.all_to_all(owned, SEQ_AXES, 0, 0, tiled=True)  20.6 us
    ppermute x1, waiting for transfers between devices, from_behind(): lax.ppermute(value, axis, [(source, source + steps) for source in range(i...  20 us
  transfers between devices with their start and end apart: 9, of which 6 were waited for; matrix products, arithmetic and copies ran while one was open for 1% of the time, Pallas kernels for 0%

profile of v4, /device:TPU:1, one launch (start us, length us, event | category | flops | bytes accessed | tf_op | source)
XLA Modules:
  0.0 345.0 jit_solution(13667543283153535693)
XLA Ops:
  7.2 0.0 copy-start
  7.2 0.0 all-gather.5.cloned.1.call-start
  7.2 24.6 %all-gather = bf16[1,192,2304]{2,1,0:T(8,128)(2,1)} all-gather(bf16[1,24,2304]{2,1,0:T(8,128)(2,1)} %param.5), channel_id=2, replica_groups=mesh['section'=2,'x'=4,'y'=8,'zl'=8,'core'=2] {'y'}, dimensions={1}, use_global_device_ids=true | all-gather | bytes 995328 | tf_op jit(solution)/shard_map/all_gather | solution.py:52
  31.8 0.0 all-gather.5.cloned.1.call-update
  31.8 0.9 broadcast_multiply_fusion
  32.7 0.2 broadcast_in_dim.12
  33.0 0.1 mul.133
  33.1 19.7 %collective-permute-start = (bf16[2,16,768]{2,1,0:T(8,128)(2,1)S(1)}, bf16[2,16,768]{2,1,0:T(8,128)(2,1)S(1)}, u32[]{:S(2)}, u32[]{:S(2)}) collective-permute-start(bf16[2,16,768]{2,1,0:T(8,128)(2,1)S(1)} %get-tuple-element.10), channel_id=1, source_target_pairs={{1,0},{2,1},{3,2},{4,3},{5,4},{6,5},{7,6},{8,7},{9,8},{10,9},{11,1... | collective-permute-start | bytes 147464 | tf_op jit(solution)/shard_map/ppermute | solution.py:18
  52.8 1.9 collective-permute-start.1
  54.7 0.0 copy-done
  54.7 0.2 fusion.56
  54.9 0.0 collective-permute-done
  54.9 1.0 collective-permute-done.1
  55.9 42.0 %all-gather.5.cloned.1.call-done = bf16[1,768,2304]{2,1,0:T(8,128)(2,1)} async-done(((bf16[1,192,2304]{2,1,0:T(8,128)(2,1)}), bf16[1,768,2304]{2,1,0:T(8,128)(2,1)}) %all-gather.5.cloned.1.call-update) | async-done | bytes 3538960 | tf_op jit(solution)/shard_map/all_gather | solution.py:53
  97.9 3.4 fusion.46
  101.3 0.3 fusion.50
  101.6 1.3 collective-permute-start.2
  102.9 20.0 %collective-permute-done.2 = bf16[2,128,768]{2,1,0:T(8,128)(2,1)S(1)} collective-permute-done((bf16[2,128,768]{2,1,0:T(8,128)(2,1)S(1)}, bf16[2,128,768]{2,1,0:T(8,128)(2,1)S(1)}, u32[]{:S(2)}, u32[]{:S(2)}) %collective-permute-start.2) | collective-permute-done | bytes 393248 | tf_op jit(solution)/shard_map/ppermute | solution.py:26
  122.9 0.0 copy-start.2
  123.0 3.6 %collective-permute-start.3 = (bf16[2,16,768]{2,1,0:T(8,128)(2,1)S(1)}, bf16[2,16,768]{2,1,0:T(8,128)(2,1)S(1)}, u32[]{:S(2)}, u32[]{:S(2)}) collective-permute-start(bf16[2,16,768]{2,1,0:T(8,128)(2,1)S(1)} %get-tuple-element.8), channel_id=1, source_target_pairs={{1,0},{2,1},{3,2},{4,3},{5,4},{6,5},{7,6},{8,7},{9,8},{10,9},{11,1... | collective-permute-start | bytes 147464 | tf_op jit(solution)/shard_map/ppermute | solution.py:18
  126.6 27.7 %collective-permute-start.4 = (bf16[2,16,768]{2,1,0:T(8,128)(2,1)S(1)}, bf16[2,16,768]{2,1,0:T(8,128)(2,1)S(1)}, u32[]{:S(2)}, u32[]{:S(2)}) collective-permute-start(bf16[2,16,768]{2,1,0:T(8,128)(2,1)S(1)} %get-tuple-element.9), channel_id=1, source_target_pairs={{0,1},{1,2},{2,3},{3,4},{4,5},{5,6},{6,7},{7,8},{8,9},{9,10},{10,1... | collective-permute-start | bytes 147464 | tf_op jit(solution)/shard_map/ppermute | solution.py:17
  154.3 0.0 collective-permute-done.3
  154.3 1.1 collective-permute-done.4
  155.4 4.3 %fusion.43 = (bf16[2,128,768]{2,1,0:T(8,128)(2,1)S(1)}, f32[2,128]{1,0:T(2,128)S(1)}, f32[2,128,768]{2,1,0:T(8,128)}) fusion(bf16[1,2,128,768]{3,2,1,0:T(8,128)(2,1)S(1)} %copy-done, f32[2,128]{1,0:T(2,128)S(1)} %add_rsqrt_fusion, bf16[1,768,2304]{2,1,0:T(8,128)(2,1)} %all-gather.5.cloned.1.call-done, bf16[2,128,768]{2,1,0:T(8,128)(2,1)S(1)} %broadcast_select_fusion, ...), kind=kOutput, calls=%fused_computation.46 | convolution fusion | flops 916586240 | bytes 5605376 | tf_op jit(solution)/shard_map/npj,cj->npc/dot_general | solution.py:75
  159.8 4.2 %collective-permute-start.5 = (bf16[2,16,768]{2,1,0:T(8,128)(2,1)S(1)}, bf16[2,16,768]{2,1,0:T(8,128)(2,1)S(1)}, u32[]{:S(2)}, u32[]{:S(2)}) collective-permute-start(bf16[2,16,768]{2,1,0:T(8,128)(2,1)S(1)} %get-tuple-element.6), channel_id=1, source_target_pairs={{0,1},{1,2},{2,3},{3,4},{4,5},{5,6},{6,7},{7,8},{8,9},{9,10},{10,1... | collective-permute-start | bytes 147464 | tf_op jit(solution)/shard_map/ppermute | solution.py:17
  164.0 1.9 collective-permute-start.6
  166.0 0.4 fusion.45
  166.3 0.0 collective-permute-done.5
  166.4 3.1 collective-permute-done.6
  169.5 0.1 fusion.65
  169.5 0.0 copy-done.2
  169.5 1.1 fusion
  170.7 5.7 %copy.15 = bf16[768,3,768]{2,1,0:T(4,128)(2,1)} copy(bf16[768,3,768]{0,2,1:T(8,128)(2,1)S(1)} %fusion) | data formatting | bytes 7077888 | tf_op jit(solution)/shard_map/convert_element_type | solution.py:105
  176.4 8.5 %convert_element_type.54 = bf16[32,24,2304]{2,1,0:T(8,128)(2,1)S(1)} reshape(bf16[768,3,768]{2,1,0:T(4,128)(2,1)} %copy.15) | data formatting | bytes 7077888 | tf_op jit(solution)/shard_map/convert_element_type | solution.py:105
  184.9 88.4 %all_to_all.10 = bf16[32,24,2304]{2,1,0:T(8,128)(2,1)S(1)} all-to-all(bf16[32,24,2304]{2,1,0:T(8,128)(2,1)S(1)} %convert_element_type.54), channel_id=1, replica_groups=mesh['section'=2,'x'=4,'y'=8,'zl'=8,'core'=2] {'x','y'}, dimensions={0} | all-to-all | bytes 7077888 | tf_op jit(solution)/shard_map/all_to_all | solution.py:106
  273.3 0.0 copy-start.1
  273.3 0.0 copy-start.3
  273.3 0.0 copy-start.4
  273.3 0.5 convert_reduce_fusion
  273.8 0.3 reshape.32
  274.1 1.0 copy.16
  275.1 10.0 %all-to-all-start.1 = ((f32[16,24,144]{2,1,0:T(8,128)}), f32[16,24,144]{2,1,0:T(8,128)S(1)}, u32[]{:S(2)}, u32[]{:S(2)}) async-start(f32[16,24,144]{2,1,0:T(8,128)} %copy.16), calls=%async_computation.1 | async-start | bytes 786432 | tf_op jit(solution)/shard_map/all_to_all | solution.py:110
  285.1 0.0 copy-done.1
  285.1 0.0 copy-done.3
  285.1 0.0 copy-done.4
  285.1 1.0 fusion.63
  286.1 20.6 %all-to-all-done.1 = f32[16,24,144]{2,1,0:T(8,128)S(1)} async-done(((f32[16,24,144]{2,1,0:T(8,128)}), f32[16,24,144]{2,1,0:T(8,128)S(1)}, u32[]{:S(2)}, u32[]{:S(2)}) %all-to-all-start.1) | async-done | bytes 221216 | tf_op jit(solution)/shard_map/all_to_all | solution.py:110
  306.8 30.4 %all-gather.2 = bf16[16,144,24]{1,2,0:T(8,128)(2,1)S(1)} all-gather(bf16[1,144,24]{1,2,0:T(8,128)(2,1)S(1)} %fusion.67), channel_id=1, replica_groups=mesh['section'=2,'x'=4,'y'=8,'zl'=8,'core'=2] {'zl','core'}, dimensions={0}, use_global_device_ids=true | all-gather | bytes 117504 | tf_op jit(solution)/shard_map/all_gather | solution.py:113
  337.2 0.9 reshape.37
  (10 shorter events, 0.2 us)
Async XLA Ops:
  7.2 47.6 %copy-start = (bf16[1,2,128,768]{3,2,1,0:T(8,128)(2,1)S(1)}, bf16[1,2,128,768]{3,2,1,0:T(8,128)(2,1)}, u32[]{:S(2)}) copy-start(bf16[1,2,128,768]{3,2,1,0:T(8,128)(2,1)} %param.3) | copy-start | bytes 1179652
  7.2 90.7 %all-gather.5.cloned.1.call-start = ((), (), s32[]{:S(2)}) async-start(), calls=%async_computation.2 | async-start | bytes 4423680 | tf_op jit(solution)/shard_map/all_gather | solution.py:53
  33.1 21.8 %collective-permute-start = (bf16[2,16,768]{2,1,0:T(8,128)(2,1)S(1)}, bf16[2,16,768]{2,1,0:T(8,128)(2,1)S(1)}, u32[]{:S(2)}, u32[]{:S(2)}) collective-permute-start(bf16[2,16,768]{2,1,0:T(8,128)(2,1)S(1)} %get-tuple-element.10), channel_id=1, source_target_pairs={{1,0},{2,1},{3,2},{4,3},{5,4},{6,5},{7,6},{8,7},{9,8},{10,9},{11,1... | collective-permute-start | bytes 147464 | tf_op jit(solution)/shard_map/ppermute | solution.py:18
  52.8 3.1 collective-permute-start.1
  101.6 21.3 %collective-permute-start.2 = (bf16[2,128,768]{2,1,0:T(8,128)(2,1)S(1)}, bf16[2,128,768]{2,1,0:T(8,128)(2,1)S(1)}, u32[]{:S(2)}, u32[]{:S(2)}) collective-permute-start(bf16[2,128,768]{2,1,0:T(8,128)(2,1)S(1)} %fusion.50), channel_id=1, source_target_pairs={{512,0},{513,1},{514,2},{515,3},{516,4},{517,5},{518,6},{519,7},{5... | collective-permute-start | bytes 1179656 | tf_op jit(solution)/shard_map/ppermute | solution.py:26
  122.9 46.6 %copy-start.2 = (bf16[2,128,768]{2,1,0:T(8,128)(2,1)}, bf16[2,128,768]{2,1,0:T(8,128)(2,1)S(1)}, u32[]{:S(2)}) copy-start(bf16[2,128,768]{2,1,0:T(8,128)(2,1)S(1)} %broadcast_select_fusion) | copy-start | bytes 1179652
  123.0 31.3 %collective-permute-start.3 = (bf16[2,16,768]{2,1,0:T(8,128)(2,1)S(1)}, bf16[2,16,768]{2,1,0:T(8,128)(2,1)S(1)}, u32[]{:S(2)}, u32[]{:S(2)}) collective-permute-start(bf16[2,16,768]{2,1,0:T(8,128)(2,1)S(1)} %get-tuple-element.8), channel_id=1, source_target_pairs={{1,0},{2,1},{3,2},{4,3},{5,4},{6,5},{7,6},{8,7},{9,8},{10,9},{11,1... | collective-permute-start | bytes 147464 | tf_op jit(solution)/shard_map/ppermute | solution.py:18
  126.6 28.8 %collective-permute-start.4 = (bf16[2,16,768]{2,1,0:T(8,128)(2,1)S(1)}, bf16[2,16,768]{2,1,0:T(8,128)(2,1)S(1)}, u32[]{:S(2)}, u32[]{:S(2)}) collective-permute-start(bf16[2,16,768]{2,1,0:T(8,128)(2,1)S(1)} %get-tuple-element.9), channel_id=1, source_target_pairs={{0,1},{1,2},{2,3},{3,4},{4,5},{5,6},{6,7},{7,8},{8,9},{9,10},{10,1... | collective-permute-start | bytes 147464 | tf_op jit(solution)/shard_map/ppermute | solution.py:17
  159.8 6.5 %collective-permute-start.5 = (bf16[2,16,768]{2,1,0:T(8,128)(2,1)S(1)}, bf16[2,16,768]{2,1,0:T(8,128)(2,1)S(1)}, u32[]{:S(2)}, u32[]{:S(2)}) collective-permute-start(bf16[2,16,768]{2,1,0:T(8,128)(2,1)S(1)} %get-tuple-element.6), channel_id=1, source_target_pairs={{0,1},{1,2},{2,3},{3,4},{4,5},{5,6},{6,7},{7,8},{8,9},{9,10},{10,1... | collective-permute-start | bytes 147464 | tf_op jit(solution)/shard_map/ppermute | solution.py:17
  164.0 5.4 %collective-permute-start.6 = (bf16[2,16,768]{2,1,0:T(8,128)(2,1)S(1)}, bf16[2,16,768]{2,1,0:T(8,128)(2,1)S(1)}, u32[]{:S(2)}, u32[]{:S(2)}) collective-permute-start(bf16[2,16,768]{2,1,0:T(8,128)(2,1)S(1)} %get-tuple-element.7), channel_id=1, source_target_pairs={{1,0},{2,1},{3,2},{4,3},{5,4},{6,5},{7,6},{8,7},{9,8},{10,9},{11,1... | collective-permute-start | bytes 147464 | tf_op jit(solution)/shard_map/ppermute | solution.py:18
  273.3 11.8 %copy-start.1 = (bf16[1,2,128,768]{3,2,1,0:T(8,128)(2,1)S(1)}, bf16[1,2,128,768]{3,2,1,0:T(8,128)(2,1)}, u32[]{:S(2)}) copy-start(bf16[1,2,128,768]{3,2,1,0:T(8,128)(2,1)} %param.3) | copy-start | bytes 1179652
  273.3 11.8 %copy-start.3 = (bf16[2,128,768]{2,1,0:T(8,128)(2,1)S(1)}, bf16[2,128,768]{2,1,0:T(8,128)(2,1)}, u32[]{:S(2)}) copy-start(bf16[2,128,768]{2,1,0:T(8,128)(2,1)} %copy-done.2) | copy-start | bytes 1179652
  273.3 11.8 %copy-start.4 = (f32[2,128,768]{2,1,0:T(8,128)S(1)}, f32[2,128,768]{2,1,0:T(8,128)}, u32[]{:S(2)}) copy-start(f32[2,128,768]{2,1,0:T(8,128)} %get-tuple-element.14) | copy-start | bytes 2359300
  275.1 31.7 %all-to-all-start.1 = ((f32[16,24,144]{2,1,0:T(8,128)}), f32[16,24,144]{2,1,0:T(8,128)S(1)}, u32[]{:S(2)}, u32[]{:S(2)}) async-start(f32[16,24,144]{2,1,0:T(8,128)} %copy.16), calls=%async_computation.1 | async-start | bytes 786432 | tf_op jit(solution)/shard_map/all_to_all | solution.py:110
Sparse Core Ops, SparseCore 0:
  31.9 65.9 all-gather.4

commit v5 on v4

--- a/solution.py
+++ b/solution.py
@@ -100,17 +100,28 @@
     ).reshape(channel_width, 3 * channel_width)
     micro_batch = saved_inputs.shape[1]
     n_dp = lax.axis_size(("x", "y"))
-    n_seq = lax.axis_size(SEQ_AXES)
+    n_zl = lax.axis_size("zl")
+    core_index = lax.axis_index("core")
+    swap = [(0, 1), (1, 0)]
     owned_rows = channel_width // n_dp
-    pieces = grad_total.astype(jnp.bfloat16).reshape(n_dp, owned_rows, 3 * channel_width)
+    half = 3 * channel_width // 2
+    own_half = lax.dynamic_slice_in_dim(grad_total, core_index * half, half, axis=1)
+    other_half = lax.dynamic_slice_in_dim(grad_total, (1 - core_index) * half, half, axis=1)
+    chip_half = own_half + lax.ppermute(other_half, "core", swap)
+    pieces = chip_half.astype(jnp.bfloat16).reshape(n_dp, owned_rows, half)
     received = lax.all_to_all(pieces, ("x", "y"), 0, 0, tiled=True)
     owned = jnp.sum(received.astype(jnp.float32), axis=0)
-    column_chunk = 3 * channel_width // n_seq
-    owned = owned.reshape(owned_rows, n_seq, column_chunk).transpose(1, 0, 2)
-    gathered = lax.all_to_all(owned, SEQ_AXES, 0, 0, tiled=True)
-    summed = jnp.sum(gathered, axis=0)
+    column_chunk = half // n_zl
+    owned = owned.reshape(owned_rows, n_zl, column_chunk).transpose(1, 0, 2)
+    summed = jnp.sum(lax.all_to_all(owned, "zl", 0, 0, tiled=True), axis=0)
     chunk_grad = (summed / (micro_batch * n_dp)).astype(jnp.bfloat16)
-    weight_grad = lax.all_gather(chunk_grad, SEQ_AXES, axis=1, tiled=True)
+    half_grad = lax.all_gather(chunk_grad, "zl", axis=1, tiled=True)
+    partner_grad = lax.ppermute(half_grad, "core", swap)
+    weight_grad = jnp.where(
+        core_index == 0,
+        jnp.concatenate([half_grad, partner_grad], axis=1),
+        jnp.concatenate([partner_grad, half_grad], axis=1),
+    )
     return (results[None], weight_grad[None])
 
 

time: 346 us -> 323 us (0.934)
  blocking collectives: 143 us -> 113 us
  starting transfers between devices: 70.4 us -> 84.4 us
  waiting for transfers between devices: 87.8 us -> 81.7 us
  local copies, waits for them, and re-layouts: 16.8 us -> 11.9 us
  other arithmetic: 3.41 us -> 7.18 us
    all_to_all x1, blocking collectives: 88.4 us -> 48.6 us  [local(): received = lax.all_to_all(pieces, ('x', 'y'), 0, 0, tiled=True)]
    ppermute x0 -> x2, starting transfers between devices: none -> 15.6 us  [the longest x1 13.7 us: local(): partner_grad = lax.ppermute(half_grad, 'core', swap)]
    convert_element_type x2 -> x0, local copies, waits for them, and re-layouts: 14.2 us -> none  [local(): grad_total.astype(jnp.bfloat16).reshape(n_dp, owned_rows, 3 * channel_width)]
    all_to_all x1, waiting for transfers between devices: 20.6 us -> 10.9 us  [local(): summed = jnp.sum(lax.all_to_all(owned, 'zl', 0, 0, tiled=True), axis=0)]
    all_gather x1, blocking collectives: 30.4 us -> 39.8 us  [local(): half_grad = lax.all_gather(chunk_grad, 'zl', axis=1, tiled=True)]
    unnamed x11 -> x13, local copies, waits for them, and re-layouts: 0.93 us -> 8.36 us
    ppermute x0 -> x2, waiting for transfers between devices: none -> 3.52 us  [the longest x1 3.52 us: local(): chip_half = own_half + lax.ppermute(other_half, 'core', swap)]
  transfers between devices with their start and end apart: 9 -> 11, of which waited for: 6 -> 7; matrix products, arithmetic and copies ran while one was open for 1% -> 2% of each run, Pallas kernels for 0% -> 0%
where the time goes in v5:
time: 323 us; the launch traced here: 321 us
  blocking collectives  113 us (35%)
  starting transfers between devices  84.4 us (26%)
  waiting for transfers between devices  81.7 us (25%)
  between operations  14.3 us (4%)
  local copies, waits for them, and re-layouts  11.9 us (4%)
  matrix products  8.89 us (3%)
  other arithmetic  7.18 us (2%)
    all_to_all x1, blocking collectives, local(): received = lax.all_to_all(pieces, ('x', 'y'), 0, 0, tiled=True)  48.6 us
    all_gather x1, waiting for transfers between devices, local(): full_kernel = lax.all_gather(full_kernel, 'x', axis=0, tiled=True)  42 us
    all_gather x1, blocking collectives, local(): half_grad = lax.all_gather(chunk_grad, 'zl', axis=1, tiled=True)  39.8 us
    ppermute x3, starting transfers between devices, with_halo(): before = lax.ppermute(last, axis, up)  33.8 us
    ppermute x3, starting transfers between devices, with_halo(): after = lax.ppermute(initial, axis, down)  25.2 us
    all_gather x1, blocking collectives, local(): full_kernel = lax.all_gather(weights[0], 'y', axis=0, tiled=True)  24.6 us
    ppermute x1, waiting for transfers between devices, from_behind(): lax.ppermute(value, axis, [(source, source + steps) for source in range(i...  20 us
    ppermute x1, starting transfers between devices, local(): partner_grad = lax.ppermute(half_grad, 'core', swap)  13.7 us
  transfers between devices with their start and end apart: 11, of which 7 were waited for; matrix products, arithmetic and copies ran while one was open for 2% of the time, Pallas kernels for 0%

profile of v5, /device:TPU:1, one launch (start us, length us, event | category | flops | bytes accessed | tf_op | source)
XLA Modules:
  0.0 321.4 jit_solution(14996831122677897523)
XLA Ops:
  7.2 0.0 copy-start
  7.2 0.0 all-gather.5.cloned.1.call-start
  7.2 24.6 %all-gather = bf16[1,192,2304]{2,1,0:T(8,128)(2,1)} all-gather(bf16[1,24,2304]{2,1,0:T(8,128)(2,1)} %param.5), channel_id=2, replica_groups=mesh['section'=2,'x'=4,'y'=8,'zl'=8,'core'=2] {'y'}, dimensions={1}, use_global_device_ids=true | all-gather | bytes 995328 | tf_op jit(solution)/shard_map/all_gather | solution.py:52
  31.8 0.0 all-gather.5.cloned.1.call-update
  31.8 0.9 broadcast_multiply_fusion
  32.7 0.2 broadcast_in_dim.4
  33.0 0.1 mul.139
  33.1 19.7 %collective-permute-start = (bf16[2,16,768]{2,1,0:T(8,128)(2,1)S(1)}, bf16[2,16,768]{2,1,0:T(8,128)(2,1)S(1)}, u32[]{:S(2)}, u32[]{:S(2)}) collective-permute-start(bf16[2,16,768]{2,1,0:T(8,128)(2,1)S(1)} %get-tuple-element.12), channel_id=1, source_target_pairs={{1,0},{2,1},{3,2},{4,3},{5,4},{6,5},{7,6},{8,7},{9,8},{10,9},{11,1... | collective-permute-start | bytes 147464 | tf_op jit(solution)/shard_map/ppermute | solution.py:18
  52.8 1.9 collective-permute-start.1
  54.7 0.0 copy-done
  54.7 0.2 fusion.56
  54.9 0.0 collective-permute-done
  54.9 1.0 collective-permute-done.1
  55.9 42.0 %all-gather.5.cloned.1.call-done = bf16[1,768,2304]{2,1,0:T(8,128)(2,1)} async-done(((bf16[1,192,2304]{2,1,0:T(8,128)(2,1)}), bf16[1,768,2304]{2,1,0:T(8,128)(2,1)}) %all-gather.5.cloned.1.call-update) | async-done | bytes 3538960 | tf_op jit(solution)/shard_map/all_gather | solution.py:53
  97.9 3.4 %fusion.46 = (f32[2,128]{1,0:T(2,128)S(1)}, f32[2,128,768]{2,1,0:T(8,128)S(1)}) fusion(bf16[1,2,128,768]{3,2,1,0:T(8,128)(2,1)S(1)} %copy-done, f32[2,128]{1,0:T(2,128)S(1)} %add_rsqrt_fusion, bf16[1,768,2304]{2,1,0:T(8,128)(2,1)} %all-gather.5.cloned.1.call-done, bf16[2,128,768]{2,1,0:T(8,128)(2,1)S(1)} %mul.139, ...), kind=kOutput, calls=%fused_computation.49 | convolution fusion | flops 916193024 | bytes 5212160 | tf_op jit(solution)/shard_map/npj,cj->npc/dot_general | solution.py:75
  101.3 0.3 fusion.50
  101.6 1.3 collective-permute-start.2
  102.9 20.0 %collective-permute-done.2 = bf16[2,128,768]{2,1,0:T(8,128)(2,1)S(1)} collective-permute-done((bf16[2,128,768]{2,1,0:T(8,128)(2,1)S(1)}, bf16[2,128,768]{2,1,0:T(8,128)(2,1)S(1)}, u32[]{:S(2)}, u32[]{:S(2)}) %collective-permute-start.2) | collective-permute-done | bytes 393248 | tf_op jit(solution)/shard_map/ppermute | solution.py:26
  122.9 0.0 copy-start.2
  123.0 3.6 %collective-permute-start.3 = (bf16[2,16,768]{2,1,0:T(8,128)(2,1)S(1)}, bf16[2,16,768]{2,1,0:T(8,128)(2,1)S(1)}, u32[]{:S(2)}, u32[]{:S(2)}) collective-permute-start(bf16[2,16,768]{2,1,0:T(8,128)(2,1)S(1)} %get-tuple-element.10), channel_id=1, source_target_pairs={{1,0},{2,1},{3,2},{4,3},{5,4},{6,5},{7,6},{8,7},{9,8},{10,9},{11,1... | collective-permute-start | bytes 147464 | tf_op jit(solution)/shard_map/ppermute | solution.py:18
  126.6 27.7 %collective-permute-start.4 = (bf16[2,16,768]{2,1,0:T(8,128)(2,1)S(1)}, bf16[2,16,768]{2,1,0:T(8,128)(2,1)S(1)}, u32[]{:S(2)}, u32[]{:S(2)}) collective-permute-start(bf16[2,16,768]{2,1,0:T(8,128)(2,1)S(1)} %get-tuple-element.11), channel_id=1, source_target_pairs={{0,1},{1,2},{2,3},{3,4},{4,5},{5,6},{6,7},{7,8},{8,9},{9,10},{10,1... | collective-permute-start | bytes 147464 | tf_op jit(solution)/shard_map/ppermute | solution.py:17
  154.3 0.0 collective-permute-done.3
  154.3 1.1 collective-permute-done.4
  155.4 4.3 %fusion.43 = (bf16[2,128,768]{2,1,0:T(8,128)(2,1)S(1)}, f32[2,128]{1,0:T(2,128)S(1)}, f32[2,128,768]{2,1,0:T(8,128)}) fusion(bf16[1,2,128,768]{3,2,1,0:T(8,128)(2,1)S(1)} %copy-done, f32[2,128]{1,0:T(2,128)S(1)} %add_rsqrt_fusion, bf16[1,768,2304]{2,1,0:T(8,128)(2,1)} %all-gather.5.cloned.1.call-done, bf16[2,128,768]{2,1,0:T(8,128)(2,1)S(1)} %broadcast_select_fusion, ...), kind=kOutput, calls=%fused_computation.46 | convolution fusion | flops 916586240 | bytes 5605376 | tf_op jit(solution)/shard_map/npj,cj->npc/dot_general | solution.py:75
  159.8 4.2 %collective-permute-start.5 = (bf16[2,16,768]{2,1,0:T(8,128)(2,1)S(1)}, bf16[2,16,768]{2,1,0:T(8,128)(2,1)S(1)}, u32[]{:S(2)}, u32[]{:S(2)}) collective-permute-start(bf16[2,16,768]{2,1,0:T(8,128)(2,1)S(1)} %get-tuple-element.8), channel_id=1, source_target_pairs={{0,1},{1,2},{2,3},{3,4},{4,5},{5,6},{6,7},{7,8},{8,9},{9,10},{10,1... | collective-permute-start | bytes 147464 | tf_op jit(solution)/shard_map/ppermute | solution.py:17
  164.0 1.9 collective-permute-start.6
  165.9 0.4 fusion.45
  166.3 0.0 collective-permute-done.5
  166.3 3.1 collective-permute-done.6
  169.4 0.1 fusion.65
  169.5 0.0 copy-done.2
  169.5 1.1 fusion.24
  170.6 2.3 constant_dynamic-slice_fusion
  172.9 5.2 %copy.26 = f32[768,1152]{1,0:T(8,128)} copy(f32[768,1152]{0,1:T(8,128)} %get-tuple-element.2) | data formatting | bytes 7077888
  178.0 1.9 collective-permute-start.7
  180.0 3.0 copy.25
  183.0 3.5 %collective-permute-done.7 = f32[768,1152]{1,0:T(8,128)} collective-permute-done((f32[768,1152]{1,0:T(8,128)}, f32[768,1152]{1,0:T(8,128)}, u32[]{:S(2)}, u32[]{:S(2)}) %collective-permute-start.7) | collective-permute-done | bytes 3538976 | tf_op jit(solution)/shard_map/ppermute | solution.py:110
  186.5 3.4 %add_convert_fusion = bf16[768,1152]{1,0:T(8,128)(2,1)S(1)} fusion(f32[768,1152]{1,0:T(8,128)} %copy.25, f32[768,1152]{1,0:T(8,128)} %collective-permute-done.7), kind=kLoop, calls=%fused_computation.5 | loop fusion | flops 1769472 | bytes 8847360 | tf_op jit(solution)/shard_map/convert_element_type | solution.py:111
  189.9 48.6 %all_to_all.10 = bf16[32,24,1152]{2,1,0:T(8,128)(2,1)S(1)} all-to-all(bf16[32,24,1152]{2,1,0:T(8,128)(2,1)S(1)} %bitcast.114), channel_id=1, replica_groups=mesh['section'=2,'x'=4,'y'=8,'zl'=8,'core'=2] {'x','y'}, dimensions={0} | all-to-all | bytes 3538944 | tf_op jit(solution)/shard_map/all_to_all | solution.py:112
  238.5 0.0 copy-start.1
  238.5 0.0 copy-start.3
  238.5 0.0 copy-start.4
  238.5 0.2 convert_reduce_fusion
  238.8 0.1 reshape.91
  238.9 0.7 copy.20
  239.7 8.4 %all-to-all-start.1 = ((f32[8,24,144]{2,1,0:T(8,128)}), f32[8,24,144]{2,1,0:T(8,128)S(1)}, u32[]{:S(2)}, u32[]{:S(2)}) async-start(f32[8,24,144]{2,1,0:T(8,128)} %copy.20), calls=%async_computation.1 | async-start | bytes 393216 | tf_op jit(solution)/shard_map/all_to_all | solution.py:116
  248.1 10.9 %all-to-all-done.1 = f32[8,24,144]{2,1,0:T(8,128)S(1)} async-done(((f32[8,24,144]{2,1,0:T(8,128)}), f32[8,24,144]{2,1,0:T(8,128)S(1)}, u32[]{:S(2)}, u32[]{:S(2)}) %all-to-all-start.1) | async-done | bytes 110624 | tf_op jit(solution)/shard_map/all_to_all | solution.py:116
  259.1 39.8 %all-gather.2 = bf16[8,144,24]{1,2,0:T(8,128)(2,1)S(1)} all-gather(bf16[1,144,24]{1,2,0:T(8,128)(2,1)S(1)} %fusion.67), channel_id=1, replica_groups=mesh['section'=2,'x'=4,'y'=8,'zl'=8,'core'=2] {'zl'}, dimensions={0}, use_global_device_ids=true | all-gather | bytes 62208 | tf_op jit(solution)/shard_map/all_gather | solution.py:118
  298.9 0.2 reshape.96
  299.1 13.7 %collective-permute-start.8 = (bf16[24,1152]{1,0:T(8,128)(2,1)S(1)}, bf16[24,1152]{1,0:T(8,128)(2,1)S(1)}, u32[]{:S(2)}, u32[]{:S(2)}) collective-permute-start(bf16[24,1152]{1,0:T(8,128)(2,1)S(1)} %bitcast.116), channel_id=1, source_target_pairs={{0,1},{1,0},{2,3},{3,2},{4,5},{5,4},{6,7},{7,6},{8,9},{9,8},{10,11... | collective-permute-start | bytes 165896 | tf_op jit(solution)/shard_map/ppermute | solution.py:119
  312.8 0.0 copy-done.1
  312.8 0.0 copy-done.3
  312.8 0.0 copy-done.4
  312.8 1.0 fusion.63
  313.8 0.0 collective-permute-done.8
  313.8 0.7 maximum_select_fusion
  (10 shorter events, 0.1 us)
Async XLA Ops:
  7.2 47.6 %copy-start = (bf16[1,2,128,768]{3,2,1,0:T(8,128)(2,1)S(1)}, bf16[1,2,128,768]{3,2,1,0:T(8,128)(2,1)}, u32[]{:S(2)}) copy-start(bf16[1,2,128,768]{3,2,1,0:T(8,128)(2,1)} %param.3) | copy-start | bytes 1179652
  7.2 90.7 %all-gather.5.cloned.1.call-start = ((), (), s32[]{:S(2)}) async-start(), calls=%async_computation.2 | async-start | bytes 4423680 | tf_op jit(solution)/shard_map/all_gather | solution.py:53
  33.1 21.8 %collective-permute-start = (bf16[2,16,768]{2,1,0:T(8,128)(2,1)S(1)}, bf16[2,16,768]{2,1,0:T(8,128)(2,1)S(1)}, u32[]{:S(2)}, u32[]{:S(2)}) collective-permute-start(bf16[2,16,768]{2,1,0:T(8,128)(2,1)S(1)} %get-tuple-element.12), channel_id=1, source_target_pairs={{1,0},{2,1},{3,2},{4,3},{5,4},{6,5},{7,6},{8,7},{9,8},{10,9},{11,1... | collective-permute-start | bytes 147464 | tf_op jit(solution)/shard_map/ppermute | solution.py:18
  52.8 3.1 collective-permute-start.1
  101.6 21.3 %collective-permute-start.2 = (bf16[2,128,768]{2,1,0:T(8,128)(2,1)S(1)}, bf16[2,128,768]{2,1,0:T(8,128)(2,1)S(1)}, u32[]{:S(2)}, u32[]{:S(2)}) collective-permute-start(bf16[2,128,768]{2,1,0:T(8,128)(2,1)S(1)} %fusion.50), channel_id=1, source_target_pairs={{512,0},{513,1},{514,2},{515,3},{516,4},{517,5},{518,6},{519,7},{5... | collective-permute-start | bytes 1179656 | tf_op jit(solution)/shard_map/ppermute | solution.py:26
  122.9 46.5 %copy-start.2 = (bf16[2,128,768]{2,1,0:T(8,128)(2,1)}, bf16[2,128,768]{2,1,0:T(8,128)(2,1)S(1)}, u32[]{:S(2)}) copy-start(bf16[2,128,768]{2,1,0:T(8,128)(2,1)S(1)} %broadcast_select_fusion) | copy-start | bytes 1179652
  123.0 31.3 %collective-permute-start.3 = (bf16[2,16,768]{2,1,0:T(8,128)(2,1)S(1)}, bf16[2,16,768]{2,1,0:T(8,128)(2,1)S(1)}, u32[]{:S(2)}, u32[]{:S(2)}) collective-permute-start(bf16[2,16,768]{2,1,0:T(8,128)(2,1)S(1)} %get-tuple-element.10), channel_id=1, source_target_pairs={{1,0},{2,1},{3,2},{4,3},{5,4},{6,5},{7,6},{8,7},{9,8},{10,9},{11,1... | collective-permute-start | bytes 147464 | tf_op jit(solution)/shard_map/ppermute | solution.py:18
  126.6 28.8 %collective-permute-start.4 = (bf16[2,16,768]{2,1,0:T(8,128)(2,1)S(1)}, bf16[2,16,768]{2,1,0:T(8,128)(2,1)S(1)}, u32[]{:S(2)}, u32[]{:S(2)}) collective-permute-start(bf16[2,16,768]{2,1,0:T(8,128)(2,1)S(1)} %get-tuple-element.11), channel_id=1, source_target_pairs={{0,1},{1,2},{2,3},{3,4},{4,5},{5,6},{6,7},{7,8},{8,9},{9,10},{10,1... | collective-permute-start | bytes 147464 | tf_op jit(solution)/shard_map/ppermute | solution.py:17
  159.8 6.6 %collective-permute-start.5 = (bf16[2,16,768]{2,1,0:T(8,128)(2,1)S(1)}, bf16[2,16,768]{2,1,0:T(8,128)(2,1)S(1)}, u32[]{:S(2)}, u32[]{:S(2)}) collective-permute-start(bf16[2,16,768]{2,1,0:T(8,128)(2,1)S(1)} %get-tuple-element.8), channel_id=1, source_target_pairs={{0,1},{1,2},{2,3},{3,4},{4,5},{5,6},{6,7},{7,8},{8,9},{9,10},{10,1... | collective-permute-start | bytes 147464 | tf_op jit(solution)/shard_map/ppermute | solution.py:17
  164.0 5.4 %collective-permute-start.6 = (bf16[2,16,768]{2,1,0:T(8,128)(2,1)S(1)}, bf16[2,16,768]{2,1,0:T(8,128)(2,1)S(1)}, u32[]{:S(2)}, u32[]{:S(2)}) collective-permute-start(bf16[2,16,768]{2,1,0:T(8,128)(2,1)S(1)} %get-tuple-element.9), channel_id=1, source_target_pairs={{1,0},{2,1},{3,2},{4,3},{5,4},{6,5},{7,6},{8,7},{9,8},{10,9},{11,1... | collective-permute-start | bytes 147464 | tf_op jit(solution)/shard_map/ppermute | solution.py:18
  178.0 8.4 %collective-permute-start.7 = (f32[768,1152]{1,0:T(8,128)}, f32[768,1152]{1,0:T(8,128)}, u32[]{:S(2)}, u32[]{:S(2)}) collective-permute-start(f32[768,1152]{1,0:T(8,128)} %copy.26), channel_id=1, source_target_pairs={{0,1},{1,0},{2,3},{3,2},{4,5},{5,4},{6,7},{7,6},{8,9},{9,8},{10,11... | collective-permute-start | bytes 10616840 | tf_op jit(solution)/shard_map/ppermute | solution.py:110
  238.5 74.3 %copy-start.1 = (bf16[1,2,128,768]{3,2,1,0:T(8,128)(2,1)S(1)}, bf16[1,2,128,768]{3,2,1,0:T(8,128)(2,1)}, u32[]{:S(2)}) copy-start(bf16[1,2,128,768]{3,2,1,0:T(8,128)(2,1)} %param.3) | copy-start | bytes 1179652
  238.5 74.3 %copy-start.3 = (bf16[2,128,768]{2,1,0:T(8,128)(2,1)S(1)}, bf16[2,128,768]{2,1,0:T(8,128)(2,1)}, u32[]{:S(2)}) copy-start(bf16[2,128,768]{2,1,0:T(8,128)(2,1)} %copy-done.2) | copy-start | bytes 1179652
  238.5 74.3 %copy-start.4 = (f32[2,128,768]{2,1,0:T(8,128)S(1)}, f32[2,128,768]{2,1,0:T(8,128)}, u32[]{:S(2)}) copy-start(f32[2,128,768]{2,1,0:T(8,128)} %get-tuple-element.16) | copy-start | bytes 2359300
  239.7 19.4 %all-to-all-start.1 = ((f32[8,24,144]{2,1,0:T(8,128)}), f32[8,24,144]{2,1,0:T(8,128)S(1)}, u32[]{:S(2)}, u32[]{:S(2)}) async-start(f32[8,24,144]{2,1,0:T(8,128)} %copy.20), calls=%async_computation.1 | async-start | bytes 393216 | tf_op jit(solution)/shard_map/all_to_all | solution.py:116
  299.1 14.7 %collective-permute-start.8 = (bf16[24,1152]{1,0:T(8,128)(2,1)S(1)}, bf16[24,1152]{1,0:T(8,128)(2,1)S(1)}, u32[]{:S(2)}, u32[]{:S(2)}) collective-permute-start(bf16[24,1152]{1,0:T(8,128)(2,1)S(1)} %bitcast.116), channel_id=1, source_target_pairs={{0,1},{1,0},{2,3},{3,2},{4,5},{5,4},{6,7},{7,6},{8,9},{9,8},{10,11... | collective-permute-start | bytes 165896 | tf_op jit(solution)/shard_map/ppermute | solution.py:119
Sparse Core Ops, SparseCore 0:
  31.9 65.9 all-gather.4

commit v6 on v5

--- a/solution.py
+++ b/solution.py
@@ -111,11 +111,9 @@
     pieces = chip_half.astype(jnp.bfloat16).reshape(n_dp, owned_rows, half)
     received = lax.all_to_all(pieces, ("x", "y"), 0, 0, tiled=True)
     owned = jnp.sum(received.astype(jnp.float32), axis=0)
-    column_chunk = half // n_zl
-    owned = owned.reshape(owned_rows, n_zl, column_chunk).transpose(1, 0, 2)
-    summed = jnp.sum(lax.all_to_all(owned, "zl", 0, 0, tiled=True), axis=0)
-    chunk_grad = (summed / (micro_batch * n_dp)).astype(jnp.bfloat16)
-    half_grad = lax.all_gather(chunk_grad, "zl", axis=1, tiled=True)
+    copies = jnp.broadcast_to(owned[None], (n_zl, owned_rows, half))
+    summed = jnp.sum(lax.all_to_all(copies, "zl", 0, 0, tiled=True), axis=0)
+    half_grad = (summed / (micro_batch * n_dp)).astype(jnp.bfloat16)
     partner_grad = lax.ppermute(half_grad, "core", swap)
     weight_grad = jnp.where(
         core_index == 0,

time: 323 us -> 307 us (0.950)
  blocking collectives: 113 us -> 73.2 us
  waiting for transfers between devices: 81.7 us -> 101 us
    all_gather x1 -> x0, blocking collectives: 39.8 us -> none  [local(): half_grad = lax.all_gather(chunk_grad, 'zl', axis=1, tiled=True)]
    all_to_all x1, waiting for transfers between devices: 10.9 us -> 29.7 us  [local(): summed = jnp.sum(lax.all_to_all(copies, 'zl', 0, 0, tiled=True), axis=0)]
    unnamed x13 -> x12, local copies, waits for them, and re-layouts: 8.36 us -> 8.2 us
  transfers between devices with their start and end apart: 11 -> 11, of which waited for: 7 -> 8; matrix products, arithmetic and copies ran while one was open for 2% -> 2% of each run, Pallas kernels for 0% -> 0%
where the time goes in v6:
time: 307 us; the launch traced here: 304 us
  waiting for transfers between devices  101 us (33%)
  starting transfers between devices  87.1 us (28%)
  blocking collectives  73.2 us (24%)
  between operations  14.3 us (5%)
  local copies, waits for them, and re-layouts  11.8 us (4%)
  matrix products  8.89 us (3%)
  other arithmetic  7.22 us (2%)
    all_to_all x1, blocking collectives, local(): received = lax.all_to_all(pieces, ('x', 'y'), 0, 0, tiled=True)  48.6 us
    all_gather x1, waiting for transfers between devices, local(): full_kernel = lax.all_gather(full_kernel, 'x', axis=0, tiled=True)  42 us
    ppermute x3, starting transfers between devices, with_halo(): before = lax.ppermute(last, axis, up)  33.8 us
    all_to_all x1, waiting for transfers between devices, local(): summed = jnp.sum(lax.all_to_all(copies, 'zl', 0, 0, tiled=True), axis=0)  29.7 us
    ppermute x3, starting transfers between devices, with_halo(): after = lax.ppermute(initial, axis, down)  25.2 us
    all_gather x1, blocking collectives, local(): full_kernel = lax.all_gather(weights[0], 'y', axis=0, tiled=True)  24.6 us
    ppermute x1, waiting for transfers between devices, from_behind(): lax.ppermute(value, axis, [(source, source + steps) for source in range(i...  20 us
    ppermute x1, starting transfers between devices, local(): partner_grad = lax.ppermute(half_grad, 'core', swap)  16.4 us
  transfers between devices with their start and end apart: 11, of which 8 were waited for; matrix products, arithmetic and copies ran while one was open for 2% of the time, Pallas kernels for 0%

profile of v6, /device:TPU:1, one launch (start us, length us, event | category | flops | bytes accessed | tf_op | source)
XLA Modules:
  0.0 303.7 jit_solution(8245059223037793888)
XLA Ops:
  7.2 0.0 copy-start
  7.2 0.0 all-gather.4.cloned.1.call-start
  7.2 24.6 %all-gather = bf16[1,192,2304]{2,1,0:T(8,128)(2,1)} all-gather(bf16[1,24,2304]{2,1,0:T(8,128)(2,1)} %param.5), channel_id=2, replica_groups=mesh['section'=2,'x'=4,'y'=8,'zl'=8,'core'=2] {'y'}, dimensions={1}, use_global_device_ids=true | all-gather | bytes 995328 | tf_op jit(solution)/shard_map/all_gather | solution.py:52
  31.8 0.0 all-gather.4.cloned.1.call-update
  31.8 0.9 broadcast_multiply_fusion
  32.7 0.2 broadcast_in_dim.6
  33.0 0.1 mul.139
  33.1 19.7 %collective-permute-start = (bf16[2,16,768]{2,1,0:T(8,128)(2,1)S(1)}, bf16[2,16,768]{2,1,0:T(8,128)(2,1)S(1)}, u32[]{:S(2)}, u32[]{:S(2)}) collective-permute-start(bf16[2,16,768]{2,1,0:T(8,128)(2,1)S(1)} %get-tuple-element.12), channel_id=1, source_target_pairs={{1,0},{2,1},{3,2},{4,3},{5,4},{6,5},{7,6},{8,7},{9,8},{10,9},{11,1... | collective-permute-start | bytes 147464 | tf_op jit(solution)/shard_map/ppermute | solution.py:18
  52.8 1.9 collective-permute-start.1
  54.7 0.0 copy-done
  54.7 0.2 fusion.56
  54.9 0.0 collective-permute-done
  54.9 1.0 collective-permute-done.1
  55.9 42.0 %all-gather.4.cloned.1.call-done = bf16[1,768,2304]{2,1,0:T(8,128)(2,1)} async-done(((bf16[1,192,2304]{2,1,0:T(8,128)(2,1)}), bf16[1,768,2304]{2,1,0:T(8,128)(2,1)}) %all-gather.4.cloned.1.call-update) | async-done | bytes 3538960 | tf_op jit(solution)/shard_map/all_gather | solution.py:53
  97.9 3.4 %fusion.46 = (f32[2,128]{1,0:T(2,128)S(1)}, f32[2,128,768]{2,1,0:T(8,128)S(1)}) fusion(bf16[1,2,128,768]{3,2,1,0:T(8,128)(2,1)S(1)} %copy-done, f32[2,128]{1,0:T(2,128)S(1)} %add_rsqrt_fusion, bf16[1,768,2304]{2,1,0:T(8,128)(2,1)} %all-gather.4.cloned.1.call-done, bf16[2,128,768]{2,1,0:T(8,128)(2,1)S(1)} %mul.139, ...), kind=kOutput, calls=%fused_computation.49 | convolution fusion | flops 916193024 | bytes 5212160 | tf_op jit(solution)/shard_map/npj,cj->npc/dot_general | solution.py:75
  101.3 0.3 fusion.50
  101.6 1.3 collective-permute-start.2
  102.9 20.0 %collective-permute-done.2 = bf16[2,128,768]{2,1,0:T(8,128)(2,1)S(1)} collective-permute-done((bf16[2,128,768]{2,1,0:T(8,128)(2,1)S(1)}, bf16[2,128,768]{2,1,0:T(8,128)(2,1)S(1)}, u32[]{:S(2)}, u32[]{:S(2)}) %collective-permute-start.2) | collective-permute-done | bytes 393248 | tf_op jit(solution)/shard_map/ppermute | solution.py:26
  122.9 0.0 copy-start.2
  123.0 3.6 %collective-permute-start.3 = (bf16[2,16,768]{2,1,0:T(8,128)(2,1)S(1)}, bf16[2,16,768]{2,1,0:T(8,128)(2,1)S(1)}, u32[]{:S(2)}, u32[]{:S(2)}) collective-permute-start(bf16[2,16,768]{2,1,0:T(8,128)(2,1)S(1)} %get-tuple-element.10), channel_id=1, source_target_pairs={{1,0},{2,1},{3,2},{4,3},{5,4},{6,5},{7,6},{8,7},{9,8},{10,9},{11,1... | collective-permute-start | bytes 147464 | tf_op jit(solution)/shard_map/ppermute | solution.py:18
  126.6 27.7 %collective-permute-start.4 = (bf16[2,16,768]{2,1,0:T(8,128)(2,1)S(1)}, bf16[2,16,768]{2,1,0:T(8,128)(2,1)S(1)}, u32[]{:S(2)}, u32[]{:S(2)}) collective-permute-start(bf16[2,16,768]{2,1,0:T(8,128)(2,1)S(1)} %get-tuple-element.11), channel_id=1, source_target_pairs={{0,1},{1,2},{2,3},{3,4},{4,5},{5,6},{6,7},{7,8},{8,9},{9,10},{10,1... | collective-permute-start | bytes 147464 | tf_op jit(solution)/shard_map/ppermute | solution.py:17
  154.3 0.0 collective-permute-done.3
  154.3 1.1 collective-permute-done.4
  155.4 4.3 %fusion.43 = (bf16[2,128,768]{2,1,0:T(8,128)(2,1)S(1)}, f32[2,128]{1,0:T(2,128)S(1)}, f32[2,128,768]{2,1,0:T(8,128)}) fusion(bf16[1,2,128,768]{3,2,1,0:T(8,128)(2,1)S(1)} %copy-done, f32[2,128]{1,0:T(2,128)S(1)} %add_rsqrt_fusion, bf16[1,768,2304]{2,1,0:T(8,128)(2,1)} %all-gather.4.cloned.1.call-done, bf16[2,128,768]{2,1,0:T(8,128)(2,1)S(1)} %broadcast_select_fusion, ...), kind=kOutput, calls=%fused_computation.46 | convolution fusion | flops 916586240 | bytes 5605376 | tf_op jit(solution)/shard_map/npj,cj->npc/dot_general | solution.py:75
  159.8 4.2 %collective-permute-start.5 = (bf16[2,16,768]{2,1,0:T(8,128)(2,1)S(1)}, bf16[2,16,768]{2,1,0:T(8,128)(2,1)S(1)}, u32[]{:S(2)}, u32[]{:S(2)}) collective-permute-start(bf16[2,16,768]{2,1,0:T(8,128)(2,1)S(1)} %get-tuple-element.8), channel_id=1, source_target_pairs={{0,1},{1,2},{2,3},{3,4},{4,5},{5,6},{6,7},{7,8},{8,9},{9,10},{10,1... | collective-permute-start | bytes 147464 | tf_op jit(solution)/shard_map/ppermute | solution.py:17
  164.0 1.9 collective-permute-start.6
  165.9 0.4 fusion.45
  166.3 0.0 collective-permute-done.5
  166.3 3.1 %collective-permute-done.6 = bf16[2,16,768]{2,1,0:T(8,128)(2,1)S(1)} collective-permute-done((bf16[2,16,768]{2,1,0:T(8,128)(2,1)S(1)}, bf16[2,16,768]{2,1,0:T(8,128)(2,1)S(1)}, u32[]{:S(2)}, u32[]{:S(2)}) %collective-permute-start.6) | collective-permute-done | bytes 49184 | tf_op jit(solution)/shard_map/ppermute | solution.py:18
  169.4 0.1 fusion.65
  169.5 0.0 copy-done.2
  169.5 1.1 fusion.24
  170.6 2.3 constant_dynamic-slice_fusion
  172.9 5.2 %copy.16 = f32[768,1152]{1,0:T(8,128)} copy(f32[768,1152]{0,1:T(8,128)} %get-tuple-element.2) | data formatting | bytes 7077888
  178.0 1.9 collective-permute-start.7
  180.0 3.0 copy.15
  183.0 3.5 %collective-permute-done.7 = f32[768,1152]{1,0:T(8,128)} collective-permute-done((f32[768,1152]{1,0:T(8,128)}, f32[768,1152]{1,0:T(8,128)}, u32[]{:S(2)}, u32[]{:S(2)}) %collective-permute-start.7) | collective-permute-done | bytes 3538976 | tf_op jit(solution)/shard_map/ppermute | solution.py:110
  186.5 3.4 %add_convert_fusion = bf16[768,1152]{1,0:T(8,128)(2,1)S(1)} fusion(f32[768,1152]{1,0:T(8,128)} %copy.15, f32[768,1152]{1,0:T(8,128)} %collective-permute-done.7), kind=kLoop, calls=%fused_computation.5 | loop fusion | flops 1769472 | bytes 8847360 | tf_op jit(solution)/shard_map/convert_element_type | solution.py:111
  189.9 48.6 %all_to_all.10 = bf16[32,24,1152]{2,1,0:T(8,128)(2,1)S(1)} all-to-all(bf16[32,24,1152]{2,1,0:T(8,128)(2,1)S(1)} %bitcast.106), channel_id=1, replica_groups=mesh['section'=2,'x'=4,'y'=8,'zl'=8,'core'=2] {'x','y'}, dimensions={0} | all-to-all | bytes 3538944 | tf_op jit(solution)/shard_map/all_to_all | solution.py:112
  238.5 0.0 copy-start.1
  238.5 0.0 copy-start.3
  238.5 0.0 copy-start.4
  238.5 0.2 convert_reduce_fusion
  238.8 1.0 broadcast_in_dim.8
  239.8 8.4 %all-to-all-start.1 = ((f32[8,24,1152]{2,1,0:T(8,128)}), f32[8,24,1152]{2,1,0:T(8,128)S(1)}, u32[]{:S(2)}, u32[]{:S(2)}) async-start(f32[8,24,1152]{2,1,0:T(8,128)} %broadcast_in_dim.8), calls=%async_computation.1 | async-start | bytes 1769472 | tf_op jit(solution)/shard_map/all_to_all | solution.py:115
  248.2 0.0 copy-done.1
  248.2 0.0 copy-done.3
  248.2 0.0 copy-done.4
  248.2 1.0 fusion.63
  249.2 29.7 %all-to-all-done.1 = f32[8,24,1152]{2,1,0:T(8,128)S(1)} async-done(((f32[8,24,1152]{2,1,0:T(8,128)}), f32[8,24,1152]{2,1,0:T(8,128)S(1)}, u32[]{:S(2)}, u32[]{:S(2)}) %all-to-all-start.1) | async-done | bytes 884768 | tf_op jit(solution)/shard_map/all_to_all | solution.py:115
  279.0 16.4 %collective-permute-start.8 = (bf16[24,1152]{1,0:T(8,128)(2,1)S(1)}, bf16[24,1152]{1,0:T(8,128)(2,1)S(1)}, u32[]{:S(2)}, u32[]{:S(2)}) collective-permute-start(bf16[24,1152]{1,0:T(8,128)(2,1)S(1)} %multiply_convert_fusion), channel_id=1, source_target_pairs={{0,1},{1,0},{2,3},{3,2},{4,5},{5,4},{6,7},{7,6},{8,9},{9,8},{10,11... | collective-permute-start | bytes 165896 | tf_op jit(solution)/shard_map/ppermute | solution.py:117
  295.4 0.8 collective-permute-done.8
  296.2 0.7 maximum_select_fusion
  (10 shorter events, 0.2 us)
Async XLA Ops:
  7.2 47.6 %copy-start = (bf16[1,2,128,768]{3,2,1,0:T(8,128)(2,1)S(1)}, bf16[1,2,128,768]{3,2,1,0:T(8,128)(2,1)}, u32[]{:S(2)}) copy-start(bf16[1,2,128,768]{3,2,1,0:T(8,128)(2,1)} %param.3) | copy-start | bytes 1179652
  7.2 90.7 %all-gather.4.cloned.1.call-start = ((), (), s32[]{:S(2)}) async-start(), calls=%async_computation.2 | async-start | bytes 4423680 | tf_op jit(solution)/shard_map/all_gather | solution.py:53
  33.1 21.8 %collective-permute-start = (bf16[2,16,768]{2,1,0:T(8,128)(2,1)S(1)}, bf16[2,16,768]{2,1,0:T(8,128)(2,1)S(1)}, u32[]{:S(2)}, u32[]{:S(2)}) collective-permute-start(bf16[2,16,768]{2,1,0:T(8,128)(2,1)S(1)} %get-tuple-element.12), channel_id=1, source_target_pairs={{1,0},{2,1},{3,2},{4,3},{5,4},{6,5},{7,6},{8,7},{9,8},{10,9},{11,1... | collective-permute-start | bytes 147464 | tf_op jit(solution)/shard_map/ppermute | solution.py:18
  52.8 3.1 %collective-permute-start.1 = (bf16[2,16,768]{2,1,0:T(8,128)(2,1)S(1)}, bf16[2,16,768]{2,1,0:T(8,128)(2,1)S(1)}, u32[]{:S(2)}, u32[]{:S(2)}) collective-permute-start(bf16[2,16,768]{2,1,0:T(8,128)(2,1)S(1)} %get-tuple-element.13), channel_id=1, source_target_pairs={{0,1},{1,2},{2,3},{3,4},{4,5},{5,6},{6,7},{7,8},{8,9},{9,10},{10,1... | collective-permute-start | bytes 147464 | tf_op jit(solution)/shard_map/ppermute | solution.py:17
  101.6 21.3 %collective-permute-start.2 = (bf16[2,128,768]{2,1,0:T(8,128)(2,1)S(1)}, bf16[2,128,768]{2,1,0:T(8,128)(2,1)S(1)}, u32[]{:S(2)}, u32[]{:S(2)}) collective-permute-start(bf16[2,128,768]{2,1,0:T(8,128)(2,1)S(1)} %fusion.50), channel_id=1, source_target_pairs={{512,0},{513,1},{514,2},{515,3},{516,4},{517,5},{518,6},{519,7},{5... | collective-permute-start | bytes 1179656 | tf_op jit(solution)/shard_map/ppermute | solution.py:26
  122.9 46.5 %copy-start.2 = (bf16[2,128,768]{2,1,0:T(8,128)(2,1)}, bf16[2,128,768]{2,1,0:T(8,128)(2,1)S(1)}, u32[]{:S(2)}) copy-start(bf16[2,128,768]{2,1,0:T(8,128)(2,1)S(1)} %broadcast_select_fusion) | copy-start | bytes 1179652
  123.0 31.3 %collective-permute-start.3 = (bf16[2,16,768]{2,1,0:T(8,128)(2,1)S(1)}, bf16[2,16,768]{2,1,0:T(8,128)(2,1)S(1)}, u32[]{:S(2)}, u32[]{:S(2)}) collective-permute-start(bf16[2,16,768]{2,1,0:T(8,128)(2,1)S(1)} %get-tuple-element.10), channel_id=1, source_target_pairs={{1,0},{2,1},{3,2},{4,3},{5,4},{6,5},{7,6},{8,7},{9,8},{10,9},{11,1... | collective-permute-start | bytes 147464 | tf_op jit(solution)/shard_map/ppermute | solution.py:18
  126.6 28.8 %collective-permute-start.4 = (bf16[2,16,768]{2,1,0:T(8,128)(2,1)S(1)}, bf16[2,16,768]{2,1,0:T(8,128)(2,1)S(1)}, u32[]{:S(2)}, u32[]{:S(2)}) collective-permute-start(bf16[2,16,768]{2,1,0:T(8,128)(2,1)S(1)} %get-tuple-element.11), channel_id=1, source_target_pairs={{0,1},{1,2},{2,3},{3,4},{4,5},{5,6},{6,7},{7,8},{8,9},{9,10},{10,1... | collective-permute-start | bytes 147464 | tf_op jit(solution)/shard_map/ppermute | solution.py:17
  159.8 6.6 %collective-permute-start.5 = (bf16[2,16,768]{2,1,0:T(8,128)(2,1)S(1)}, bf16[2,16,768]{2,1,0:T(8,128)(2,1)S(1)}, u32[]{:S(2)}, u32[]{:S(2)}) collective-permute-start(bf16[2,16,768]{2,1,0:T(8,128)(2,1)S(1)} %get-tuple-element.8), channel_id=1, source_target_pairs={{0,1},{1,2},{2,3},{3,4},{4,5},{5,6},{6,7},{7,8},{8,9},{9,10},{10,1... | collective-permute-start | bytes 147464 | tf_op jit(solution)/shard_map/ppermute | solution.py:17
  164.0 5.4 %collective-permute-start.6 = (bf16[2,16,768]{2,1,0:T(8,128)(2,1)S(1)}, bf16[2,16,768]{2,1,0:T(8,128)(2,1)S(1)}, u32[]{:S(2)}, u32[]{:S(2)}) collective-permute-start(bf16[2,16,768]{2,1,0:T(8,128)(2,1)S(1)} %get-tuple-element.9), channel_id=1, source_target_pairs={{1,0},{2,1},{3,2},{4,3},{5,4},{6,5},{7,6},{8,7},{9,8},{10,9},{11,1... | collective-permute-start | bytes 147464 | tf_op jit(solution)/shard_map/ppermute | solution.py:18
  178.0 8.4 %collective-permute-start.7 = (f32[768,1152]{1,0:T(8,128)}, f32[768,1152]{1,0:T(8,128)}, u32[]{:S(2)}, u32[]{:S(2)}) collective-permute-start(f32[768,1152]{1,0:T(8,128)} %copy.16), channel_id=1, source_target_pairs={{0,1},{1,0},{2,3},{3,2},{4,5},{5,4},{6,7},{7,6},{8,9},{9,8},{10,11... | collective-permute-start | bytes 10616840 | tf_op jit(solution)/shard_map/ppermute | solution.py:110
  238.5 9.7 %copy-start.1 = (bf16[1,2,128,768]{3,2,1,0:T(8,128)(2,1)S(1)}, bf16[1,2,128,768]{3,2,1,0:T(8,128)(2,1)}, u32[]{:S(2)}) copy-start(bf16[1,2,128,768]{3,2,1,0:T(8,128)(2,1)} %param.3) | copy-start | bytes 1179652
  238.5 9.7 %copy-start.3 = (bf16[2,128,768]{2,1,0:T(8,128)(2,1)S(1)}, bf16[2,128,768]{2,1,0:T(8,128)(2,1)}, u32[]{:S(2)}) copy-start(bf16[2,128,768]{2,1,0:T(8,128)(2,1)} %copy-done.2) | copy-start | bytes 1179652
  238.5 9.7 %copy-start.4 = (f32[2,128,768]{2,1,0:T(8,128)S(1)}, f32[2,128,768]{2,1,0:T(8,128)}, u32[]{:S(2)}) copy-start(f32[2,128,768]{2,1,0:T(8,128)} %get-tuple-element.16) | copy-start | bytes 2359300
  239.8 39.1 %all-to-all-start.1 = ((f32[8,24,1152]{2,1,0:T(8,128)}), f32[8,24,1152]{2,1,0:T(8,128)S(1)}, u32[]{:S(2)}, u32[]{:S(2)}) async-start(f32[8,24,1152]{2,1,0:T(8,128)} %broadcast_in_dim.8), calls=%async_computation.1 | async-start | bytes 1769472 | tf_op jit(solution)/shard_map/all_to_all | solution.py:115
  279.0 17.3 %collective-permute-start.8 = (bf16[24,1152]{1,0:T(8,128)(2,1)S(1)}, bf16[24,1152]{1,0:T(8,128)(2,1)S(1)}, u32[]{:S(2)}, u32[]{:S(2)}) collective-permute-start(bf16[24,1152]{1,0:T(8,128)(2,1)S(1)} %multiply_convert_fusion), channel_id=1, source_target_pairs={{0,1},{1,0},{2,3},{3,2},{4,5},{5,4},{6,7},{7,6},{8,9},{9,8},{10,11... | collective-permute-start | bytes 165896 | tf_op jit(solution)/shard_map/ppermute | solution.py:117
Sparse Core Ops, SparseCore 0:
  31.9 65.9 all-gather.3

commit v7 on v6

--- a/solution.py
+++ b/solution.py
@@ -49,8 +49,17 @@
     batch_rows = saved_inputs.shape[2]
     channel_width = weights.shape[2] // 3
     dilation_amount = DILATION_STEP
-    full_kernel = lax.all_gather(weights[0], "y", axis=0, tiled=True)
-    full_kernel = lax.all_gather(full_kernel, "x", axis=0, tiled=True)
+    kernel_core = lax.axis_index("core")
+    kernel_half = weights.shape[2] // 2
+    own_columns = lax.dynamic_slice_in_dim(weights[0], kernel_core * kernel_half, kernel_half, axis=1)
+    own_columns = lax.all_gather(own_columns, "y", axis=0, tiled=True)
+    own_columns = lax.all_gather(own_columns, "x", axis=0, tiled=True)
+    partner_columns = lax.ppermute(own_columns, "core", [(0, 1), (1, 0)])
+    full_kernel = jnp.where(
+        kernel_core == 0,
+        jnp.concatenate([own_columns, partner_columns], axis=1),
+        jnp.concatenate([partner_columns, own_columns], axis=1),
+    )
     value_rows = saved_inputs[0].astype(jnp.float32)
     norm_scale = lax.rsqrt(jnp.mean(value_rows * value_rows, axis=-1, keepdims=True) + 1e-05)
     normalized_input = value_rows * norm_scale

time: 307 us -> 304 us (level)
  starting transfers between devices: 87.1 us -> 73 us
  waiting for transfers between devices: 101 us -> 108 us
  local copies, waits for them, and re-layouts: 11.8 us -> 15.8 us
    ppermute x3, starting transfers between devices: 25.2 us -> 5.76 us  [with_halo(): after = lax.ppermute(initial, axis, down)]
    all_gather x1, waiting for transfers between devices: 42 us -> 51.3 us  [local(): own_columns = lax.all_gather(own_columns, 'x', axis=0, tiled=True)]
    ppermute x3, starting transfers between devices: 33.8 us -> 37.6 us  [with_halo(): before = lax.ppermute(last, axis, up)]
    unnamed x12 -> x6, local copies, waits for them, and re-layouts: 8.2 us -> 11.2 us
  transfers between devices with their start and end apart: 11 -> 12, of which waited for: 8 -> 8; matrix products, arithmetic and copies ran while one was open for 2% -> 3% of each run, Pallas kernels for 0% -> 0%
where the time goes in v7:
time: 304 us; the launch traced here: 301 us
  waiting for transfers between devices  108 us (36%)
  starting transfers between devices  73 us (24%)
  blocking collectives  71.5 us (24%)
  local copies, waits for them, and re-layouts  15.8 us (5%)
  between operations  14.3 us (5%)
  matrix products  11.3 us (4%)
  other arithmetic  7.22 us (2%)
    all_gather x1, waiting for transfers between devices, local(): own_columns = lax.all_gather(own_columns, 'x', axis=0, tiled=True)  51.3 us
    all_to_all x1, blocking collectives, local(): received = lax.all_to_all(pieces, ('x', 'y'), 0, 0, tiled=True)  48.4 us
    ppermute x3, starting transfers between devices, with_halo(): before = lax.ppermute(last, axis, up)  37.6 us
    all_to_all x1, waiting for transfers between devices, local(): summed = jnp.sum(lax.all_to_all(copies, 'zl', 0, 0, tiled=True), axis=0)  29.7 us
    all_gather x1, blocking collectives, local(): own_columns = lax.all_gather(own_columns, 'y', axis=0, tiled=True)  23.1 us
    ppermute x1, waiting for transfers between devices, from_behind(): lax.ppermute(value, axis, [(source, source + steps) for source in range(i...  19.7 us
    ppermute x1, starting transfers between devices, local(): partner_grad = lax.ppermute(half_grad, 'core', swap)  16.4 us
    unnamed x6, local copies, waits for them, and re-layouts  11.2 us
  transfers between devices with their start and end apart: 12, of which 8 were waited for; matrix products, arithmetic and copies ran while one was open for 3% of the time, Pallas kernels for 0%

profile of v7, /device:TPU:1, one launch (start us, length us, event | category | flops | bytes accessed | tf_op | source)
XLA Modules:
  0.0 301.2 jit_solution(7955589879225986507)
XLA Ops:
  7.2 0.0 copy-start
  7.2 0.0 copy-start.1
  7.2 0.0 all-gather.4.cloned.1.call-start
  7.2 0.8 copy-done
  8.1 23.1 %all-gather = bf16[1,192,1152]{2,1,0:T(8,128)(2,1)} all-gather(bf16[1,24,1152]{2,1,0:T(8,128)(2,1)S(1)} %constant_dynamic-slice_fusion.2), channel_id=2, replica_groups=mesh['section'=2,'x'=4,'y'=8,'zl'=8,'core'=2] {'y'}, dimensions={1}, use_global_device_ids=true | all-gather | bytes 497664 | tf_op jit(solution)/shard_map/all_gather | solution.py:55
  31.2 0.0 all-gather.4.cloned.1.call-update
  31.2 51.3 %all-gather.4.cloned.1.call-done = bf16[1,768,1152]{2,1,0:T(8,128)(2,1)} async-done(((bf16[1,192,1152]{2,1,0:T(8,128)(2,1)}), bf16[1,768,1152]{2,1,0:T(8,128)(2,1)}) %all-gather.4.cloned.1.call-update) | async-done | bytes 1769488 | tf_op jit(solution)/shard_map/all_gather | solution.py:56
  82.5 2.7 collective-permute-start.2
  85.3 0.9 broadcast_multiply_fusion
  86.2 0.2 broadcast_in_dim.6
  86.4 0.1 mul.140
  86.6 1.9 collective-permute-start
  88.5 3.6 %collective-permute-start.1 = (bf16[2,16,768]{2,1,0:T(8,128)(2,1)S(1)}, bf16[2,16,768]{2,1,0:T(8,128)(2,1)S(1)}, u32[]{:S(2)}, u32[]{:S(2)}) collective-permute-start(bf16[2,16,768]{2,1,0:T(8,128)(2,1)S(1)} %get-tuple-element.13), channel_id=1, source_target_pairs={{0,1},{1,2},{2,3},{3,4},{4,5},{5,6},{6,7},{7,8},{8,9},{9,10},{10,1... | collective-permute-start | bytes 147464 | tf_op jit(solution)/shard_map/ppermute | solution.py:17
  92.2 0.0 copy-done.1
  92.2 0.2 fusion.57
  92.4 0.0 collective-permute-done
  92.4 1.0 collective-permute-done.1
  93.4 0.0 collective-permute-done.2
  93.4 5.0 %fusion.47 = (f32[2,128]{1,0:T(2,128)S(1)}, f32[2,128,768]{2,1,0:T(8,128)S(1)}) fusion(bf16[1,2,128,768]{3,2,1,0:T(8,128)(2,1)S(1)} %copy-done.1, f32[2,128]{1,0:T(2,128)S(1)} %add_rsqrt_fusion, bf16[768,1152]{1,0:T(8,128)(2,1)} %collective-permute-done.2, bf16[768,1152]{1,0:T(8,128)(2,1)} %bitcast.108, pred[]{:T(512)S(6)} %eq.8, ...), kind=kOutput, calls=%fused_computation.49 | convolution fusion | flops 932118272 | bytes 5212161 | tf_op jit(solution)/shard_map/npj,cj->npc/dot_general | solution.py:84
  98.4 0.3 fusion.51
  98.7 1.3 collective-permute-start.3
  100.0 19.7 %collective-permute-done.3 = bf16[2,128,768]{2,1,0:T(8,128)(2,1)S(1)} collective-permute-done((bf16[2,128,768]{2,1,0:T(8,128)(2,1)S(1)}, bf16[2,128,768]{2,1,0:T(8,128)(2,1)S(1)}, u32[]{:S(2)}, u32[]{:S(2)}) %collective-permute-start.3) | collective-permute-done | bytes 393248 | tf_op jit(solution)/shard_map/ppermute | solution.py:26
  119.7 1.9 collective-permute-start.4
  121.6 29.7 %collective-permute-start.5 = (bf16[2,16,768]{2,1,0:T(8,128)(2,1)S(1)}, bf16[2,16,768]{2,1,0:T(8,128)(2,1)S(1)}, u32[]{:S(2)}, u32[]{:S(2)}) collective-permute-start(bf16[2,16,768]{2,1,0:T(8,128)(2,1)S(1)} %get-tuple-element.11), channel_id=1, source_target_pairs={{0,1},{1,2},{2,3},{3,4},{4,5},{5,6},{6,7},{7,8},{8,9},{9,10},{10,1... | collective-permute-start | bytes 147464 | tf_op jit(solution)/shard_map/ppermute | solution.py:17
  151.4 0.0 collective-permute-done.4
  151.4 1.1 collective-permute-done.5
  152.5 5.1 %fusion.44 = (bf16[2,128,768]{2,1,0:T(8,128)(2,1)S(1)}, f32[2,128]{1,0:T(2,128)S(1)}, f32[2,128,768]{2,1,0:T(8,128)S(1)}) fusion(bf16[1,2,128,768]{3,2,1,0:T(8,128)(2,1)S(1)} %copy-done.1, f32[2,128]{1,0:T(2,128)S(1)} %add_rsqrt_fusion, bf16[768,1152]{1,0:T(8,128)(2,1)} %collective-permute-done.2, bf16[768,1152]{1,0:T(8,128)(2,1)} %bitcast.109, ...), kind=kOutput, calls=%fused_computation.46 | convolution fusion | flops 932511488 | bytes 5605377 | tf_op jit(solution)/shard_map/npj,cj->npc/dot_general | solution.py:84
  157.6 4.2 %collective-permute-start.6 = (bf16[2,16,768]{2,1,0:T(8,128)(2,1)S(1)}, bf16[2,16,768]{2,1,0:T(8,128)(2,1)S(1)}, u32[]{:S(2)}, u32[]{:S(2)}) collective-permute-start(bf16[2,16,768]{2,1,0:T(8,128)(2,1)S(1)} %get-tuple-element.8), channel_id=1, source_target_pairs={{0,1},{1,2},{2,3},{3,4},{4,5},{5,6},{6,7},{7,8},{8,9},{9,10},{10,1... | collective-permute-start | bytes 147464 | tf_op jit(solution)/shard_map/ppermute | solution.py:17
  161.9 1.9 collective-permute-start.7
  163.8 0.4 fusion.46
  164.2 0.0 collective-permute-done.6
  164.2 3.1 %collective-permute-done.7 = bf16[2,16,768]{2,1,0:T(8,128)(2,1)S(1)} collective-permute-done((bf16[2,16,768]{2,1,0:T(8,128)(2,1)S(1)}, bf16[2,16,768]{2,1,0:T(8,128)(2,1)S(1)}, u32[]{:S(2)}, u32[]{:S(2)}) %collective-permute-start.7) | collective-permute-done | bytes 49184 | tf_op jit(solution)/shard_map/ppermute | solution.py:18
  167.3 0.1 fusion.66
  167.4 1.1 fusion.25
  168.5 3.3 %constant_dynamic-slice_fusion = (f32[768,1152]{0,1:T(8,128)}, f32[768,1152]{0,1:T(8,128)}) fusion(f32[768,2304]{0,1:T(8,128)S(1)} %bitcast.104, s32[]{:T(128)S(6)} %select_n.44, s32[]{:T(128)S(6)} %select_n.40), kind=kLoop, calls=%fused_computation.77 | loop fusion | bytes 14155784 | tf_op jit(solution)/shard_map/dynamic_slice | solution.py:118
  171.8 5.2 %copy.16 = f32[768,1152]{1,0:T(8,128)} copy(f32[768,1152]{0,1:T(8,128)} %get-tuple-element.2) | data formatting | bytes 7077888
  177.0 1.9 collective-permute-start.8
  178.9 5.2 %copy.15 = f32[768,1152]{1,0:T(8,128)} copy(f32[768,1152]{0,1:T(8,128)} %get-tuple-element.3) | data formatting | bytes 7077888
  184.0 1.4 collective-permute-done.8
  185.4 3.4 %add_convert_fusion = bf16[768,1152]{1,0:T(8,128)(2,1)S(1)} fusion(f32[768,1152]{1,0:T(8,128)} %copy.15, f32[768,1152]{1,0:T(8,128)} %collective-permute-done.8), kind=kLoop, calls=%fused_computation.3 | loop fusion | flops 1769472 | bytes 8847360 | tf_op jit(solution)/shard_map/convert_element_type | solution.py:120
  188.8 48.4 %all_to_all.10 = bf16[32,24,1152]{2,1,0:T(8,128)(2,1)S(1)} all-to-all(bf16[32,24,1152]{2,1,0:T(8,128)(2,1)S(1)} %bitcast.105), channel_id=1, replica_groups=mesh['section'=2,'x'=4,'y'=8,'zl'=8,'core'=2] {'x','y'}, dimensions={0} | all-to-all | bytes 3538944 | tf_op jit(solution)/shard_map/all_to_all | solution.py:121
  237.2 0.2 convert_reduce_fusion
  237.4 1.0 broadcast_in_dim.8
  238.4 7.3 %all-to-all-start.1 = ((f32[8,24,1152]{2,1,0:T(8,128)}), f32[8,24,1152]{2,1,0:T(8,128)S(1)}, u32[]{:S(2)}, u32[]{:S(2)}) async-start(f32[8,24,1152]{2,1,0:T(8,128)} %broadcast_in_dim.8), calls=%async_computation.1 | async-start | bytes 1769472 | tf_op jit(solution)/shard_map/all_to_all | solution.py:124
  245.7 1.0 fusion.64
  246.7 29.7 %all-to-all-done.1 = f32[8,24,1152]{2,1,0:T(8,128)S(1)} async-done(((f32[8,24,1152]{2,1,0:T(8,128)}), f32[8,24,1152]{2,1,0:T(8,128)S(1)}, u32[]{:S(2)}, u32[]{:S(2)}) %all-to-all-start.1) | async-done | bytes 884768 | tf_op jit(solution)/shard_map/all_to_all | solution.py:124
  276.5 16.4 %collective-permute-start.9 = (bf16[24,1152]{1,0:T(8,128)(2,1)S(1)}, bf16[24,1152]{1,0:T(8,128)(2,1)S(1)}, u32[]{:S(2)}, u32[]{:S(2)}) collective-permute-start(bf16[24,1152]{1,0:T(8,128)(2,1)S(1)} %multiply_convert_fusion), channel_id=1, source_target_pairs={{0,1},{1,0},{2,3},{3,2},{4,5},{5,4},{6,7},{7,6},{8,9},{9,8},{10,11... | collective-permute-start | bytes 165896 | tf_op jit(solution)/shard_map/ppermute | solution.py:126
  292.9 0.8 collective-permute-done.9
  293.7 0.7 maximum_select_fusion.1
  (11 shorter events, 0.2 us)
Async XLA Ops:
  7.2 0.9 copy-start
  7.2 85.0 %copy-start.1 = (bf16[1,2,128,768]{3,2,1,0:T(8,128)(2,1)S(1)}, bf16[1,2,128,768]{3,2,1,0:T(8,128)(2,1)}, u32[]{:S(2)}) copy-start(bf16[1,2,128,768]{3,2,1,0:T(8,128)(2,1)} %param.3) | copy-start | bytes 1179652
  7.2 75.3 %all-gather.4.cloned.1.call-start = ((), (), s32[]{:S(2)}) async-start(), calls=%async_computation.2 | async-start | bytes 2211840 | tf_op jit(solution)/shard_map/all_gather | solution.py:56
  82.5 10.8 %collective-permute-start.2 = (bf16[768,1152]{1,0:T(8,128)(2,1)}, bf16[768,1152]{1,0:T(8,128)(2,1)}, u32[]{:S(2)}, u32[]{:S(2)}) collective-permute-start(bf16[768,1152]{1,0:T(8,128)(2,1)} %bitcast.107), channel_id=1, source_target_pairs={{0,1},{1,0},{2,3},{3,2},{4,5},{5,4},{6,7},{7,6},{8,9},{9,8},{10,11... | collective-permute-start | bytes 5308424 | tf_op jit(solution)/shard_map/ppermute | solution.py:57
  86.6 5.8 %collective-permute-start = (bf16[2,16,768]{2,1,0:T(8,128)(2,1)S(1)}, bf16[2,16,768]{2,1,0:T(8,128)(2,1)S(1)}, u32[]{:S(2)}, u32[]{:S(2)}) collective-permute-start(bf16[2,16,768]{2,1,0:T(8,128)(2,1)S(1)} %get-tuple-element.12), channel_id=1, source_target_pairs={{1,0},{2,1},{3,2},{4,3},{5,4},{6,5},{7,6},{8,7},{9,8},{10,9},{11,1... | collective-permute-start | bytes 147464 | tf_op jit(solution)/shard_map/ppermute | solution.py:18
  88.5 4.8 %collective-permute-start.1 = (bf16[2,16,768]{2,1,0:T(8,128)(2,1)S(1)}, bf16[2,16,768]{2,1,0:T(8,128)(2,1)S(1)}, u32[]{:S(2)}, u32[]{:S(2)}) collective-permute-start(bf16[2,16,768]{2,1,0:T(8,128)(2,1)S(1)} %get-tuple-element.13), channel_id=1, source_target_pairs={{0,1},{1,2},{2,3},{3,4},{4,5},{5,6},{6,7},{7,8},{8,9},{9,10},{10,1... | collective-permute-start | bytes 147464 | tf_op jit(solution)/shard_map/ppermute | solution.py:17
  98.7 21.0 %collective-permute-start.3 = (bf16[2,128,768]{2,1,0:T(8,128)(2,1)S(1)}, bf16[2,128,768]{2,1,0:T(8,128)(2,1)S(1)}, u32[]{:S(2)}, u32[]{:S(2)}) collective-permute-start(bf16[2,128,768]{2,1,0:T(8,128)(2,1)S(1)} %fusion.51), channel_id=1, source_target_pairs={{512,0},{513,1},{514,2},{515,3},{516,4},{517,5},{518,6},{519,7},{5... | collective-permute-start | bytes 1179656 | tf_op jit(solution)/shard_map/ppermute | solution.py:26
  119.7 31.6 %collective-permute-start.4 = (bf16[2,16,768]{2,1,0:T(8,128)(2,1)S(1)}, bf16[2,16,768]{2,1,0:T(8,128)(2,1)S(1)}, u32[]{:S(2)}, u32[]{:S(2)}) collective-permute-start(bf16[2,16,768]{2,1,0:T(8,128)(2,1)S(1)} %get-tuple-element.10), channel_id=1, source_target_pairs={{1,0},{2,1},{3,2},{4,3},{5,4},{6,5},{7,6},{8,7},{9,8},{10,9},{11,1... | collective-permute-start | bytes 147464 | tf_op jit(solution)/shard_map/ppermute | solution.py:18
  121.6 30.9 %collective-permute-start.5 = (bf16[2,16,768]{2,1,0:T(8,128)(2,1)S(1)}, bf16[2,16,768]{2,1,0:T(8,128)(2,1)S(1)}, u32[]{:S(2)}, u32[]{:S(2)}) collective-permute-start(bf16[2,16,768]{2,1,0:T(8,128)(2,1)S(1)} %get-tuple-element.11), channel_id=1, source_target_pairs={{0,1},{1,2},{2,3},{3,4},{4,5},{5,6},{6,7},{7,8},{8,9},{9,10},{10,1... | collective-permute-start | bytes 147464 | tf_op jit(solution)/shard_map/ppermute | solution.py:17
  157.6 6.6 %collective-permute-start.6 = (bf16[2,16,768]{2,1,0:T(8,128)(2,1)S(1)}, bf16[2,16,768]{2,1,0:T(8,128)(2,1)S(1)}, u32[]{:S(2)}, u32[]{:S(2)}) collective-permute-start(bf16[2,16,768]{2,1,0:T(8,128)(2,1)S(1)} %get-tuple-element.8), channel_id=1, source_target_pairs={{0,1},{1,2},{2,3},{3,4},{4,5},{5,6},{6,7},{7,8},{8,9},{9,10},{10,1... | collective-permute-start | bytes 147464 | tf_op jit(solution)/shard_map/ppermute | solution.py:17
  161.9 5.4 %collective-permute-start.7 = (bf16[2,16,768]{2,1,0:T(8,128)(2,1)S(1)}, bf16[2,16,768]{2,1,0:T(8,128)(2,1)S(1)}, u32[]{:S(2)}, u32[]{:S(2)}) collective-permute-start(bf16[2,16,768]{2,1,0:T(8,128)(2,1)S(1)} %get-tuple-element.9), channel_id=1, source_target_pairs={{1,0},{2,1},{3,2},{4,3},{5,4},{6,5},{7,6},{8,7},{9,8},{10,9},{11,1... | collective-permute-start | bytes 147464 | tf_op jit(solution)/shard_map/ppermute | solution.py:18
  177.0 8.4 %collective-permute-start.8 = (f32[768,1152]{1,0:T(8,128)}, f32[768,1152]{1,0:T(8,128)}, u32[]{:S(2)}, u32[]{:S(2)}) collective-permute-start(f32[768,1152]{1,0:T(8,128)} %copy.16), channel_id=1, source_target_pairs={{0,1},{1,0},{2,3},{3,2},{4,5},{5,4},{6,7},{7,6},{8,9},{9,8},{10,11... | collective-permute-start | bytes 10616840 | tf_op jit(solution)/shard_map/ppermute | solution.py:119
  238.4 38.0 %all-to-all-start.1 = ((f32[8,24,1152]{2,1,0:T(8,128)}), f32[8,24,1152]{2,1,0:T(8,128)S(1)}, u32[]{:S(2)}, u32[]{:S(2)}) async-start(f32[8,24,1152]{2,1,0:T(8,128)} %broadcast_in_dim.8), calls=%async_computation.1 | async-start | bytes 1769472 | tf_op jit(solution)/shard_map/all_to_all | solution.py:124
  276.5 17.3 %collective-permute-start.9 = (bf16[24,1152]{1,0:T(8,128)(2,1)S(1)}, bf16[24,1152]{1,0:T(8,128)(2,1)S(1)}, u32[]{:S(2)}, u32[]{:S(2)}) collective-permute-start(bf16[24,1152]{1,0:T(8,128)(2,1)S(1)} %multiply_convert_fusion), channel_id=1, source_target_pairs={{0,1},{1,0},{2,3},{3,2},{4,5},{5,4},{6,7},{7,6},{8,9},{9,8},{10,11... | collective-permute-start | bytes 165896 | tf_op jit(solution)/shard_map/ppermute | solution.py:126
Sparse Core Ops, SparseCore 0:
  31.3 51.1 all-gather.3

commit v8 on v7

--- a/solution.py
+++ b/solution.py
@@ -60,22 +60,25 @@
         jnp.concatenate([own_columns, partner_columns], axis=1),
         jnp.concatenate([partner_columns, own_columns], axis=1),
     )
-    value_rows = saved_inputs[0].astype(jnp.float32)
+    seq_index = lax.axis_index(SEQ_AXES)
+    sequence_length = lax.axis_size(SEQ_AXES) * batch_rows
+    inputs_widened = with_halo(saved_inputs[0], ((SEQ_AXES, 1),), dilation_amount)
+    upsampled = jnp.repeat(pooled_adjoint, 2, axis=1) * 0.5
+    upsampled_widened = with_halo(upsampled, ((SEQ_AXES, 1),), 2 * dilation_amount)
+    value_rows = inputs_widened.astype(jnp.float32)
     norm_scale = lax.rsqrt(jnp.mean(value_rows * value_rows, axis=-1, keepdims=True) + 1e-05)
     normalized_input = value_rows * norm_scale
-    layer_activation = gelu_gate(normalized_input).astype(jnp.bfloat16)
+    activation_widened = gelu_gate(normalized_input).astype(jnp.bfloat16)
     slope = gelu_derivative(normalized_input)
-    upsampled = jnp.repeat(pooled_adjoint, 2, axis=1) * 0.5
-    activation_widened = with_halo(layer_activation, ((SEQ_AXES, 1),), dilation_amount)
+    wide_rows = batch_rows + 2 * dilation_amount
 
-    def block(cotangent_state):
-        cotangent_widened = with_halo(cotangent_state, ((SEQ_AXES, 1),), dilation_amount)
+    def block(cotangent_widened, cotangent_state, scale, normalized, derivative, rows):
         cotangent_kernel_taps = jnp.concatenate(
             [
                 cotangent_widened[
                     :,
                     (2 - kernel_offset) * dilation_amount : (2 - kernel_offset) * dilation_amount
-                    + batch_rows,
+                    + rows,
                 ]
                 for kernel_offset in range(3)
             ],
@@ -84,17 +87,32 @@
         reverse_propagate = jnp.einsum(
             "npj,cj->npc", cotangent_kernel_taps, full_kernel, preferred_element_type=jnp.float32
         )
-        derivative_gradient = reverse_propagate * slope
-        centered_average = jnp.mean(derivative_gradient * normalized_input, axis=-1, keepdims=True)
+        derivative_gradient = reverse_propagate * derivative
+        centered_average = jnp.mean(derivative_gradient * normalized, axis=-1, keepdims=True)
         return (
             cotangent_state.astype(jnp.float32)
-            + norm_scale * (derivative_gradient - normalized_input * centered_average)
+            + scale * (derivative_gradient - normalized * centered_average)
         ).astype(jnp.bfloat16)
 
-    upper_output = block(upsampled)
+    upsampled_halo = upsampled_widened[:, dilation_amount : dilation_amount + wide_rows]
+    upper_output = block(
+        upsampled_widened, upsampled_halo, norm_scale, normalized_input, slope, wide_rows
+    )
+    position = seq_index * batch_rows - dilation_amount + jnp.arange(wide_rows)
+    inside = (position >= 0) & (position < sequence_length)
+    upper_output = jnp.where(inside[None, :, None], upper_output, jnp.zeros_like(upper_output))
     incoming = from_behind(upper_output, "section", -1)
-    cotangent_state = jnp.where(is_last, upsampled, incoming)
-    results = block(cotangent_state)
+    cotangent_widened = jnp.where(is_last, upsampled_halo, incoming)
+    centre = slice(dilation_amount, dilation_amount + batch_rows)
+    cotangent_state = cotangent_widened[:, centre]
+    results = block(
+        cotangent_widened,
+        cotangent_state,
+        norm_scale[:, centre],
+        normalized_input[:, centre],
+        slope[:, centre],
+        batch_rows,
+    )
     activation_kernel_taps = jnp.stack(
         [
             activation_widened[

time: 304 us -> 299 us (0.984)
  waiting for transfers between devices: 108 us -> 102 us
    all_to_all x1, starting transfers between devices: 7.3 us -> 39.2 us  [local(): summed = jnp.sum(lax.all_to_all(copies, 'zl', 0, 0, tiled=True), axis=0)]
    ppermute x3 -> x2, starting transfers between devices: 37.6 us -> 6.8 us  [with_halo(): before = lax.ppermute(last, axis, up)]
    all_to_all x1, waiting for transfers between devices: 29.7 us -> 24.9 us  [local(): summed = jnp.sum(lax.all_to_all(copies, 'zl', 0, 0, tiled=True), axis=0)]
  transfers between devices with their start and end apart: 12 -> 10, of which waited for: 8 -> 6; matrix products, arithmetic and copies ran while one was open for 3% -> 5% of each run, Pallas kernels for 0% -> 0%
where the time goes in v8:
time: 299 us; the launch traced here: 296 us
  waiting for transfers between devices  102 us (34%)
  starting transfers between devices  72.2 us (24%)
  blocking collectives  71.5 us (24%)
  local copies, waits for them, and re-layouts  16.9 us (6%)
  between operations  14.3 us (5%)
  matrix products  11.9 us (4%)
  other arithmetic  6.97 us (2%)
    all_gather x1, waiting for transfers between devices, local(): own_columns = lax.all_gather(own_columns, 'x', axis=0, tiled=True)  51.3 us
    all_to_all x1, blocking collectives, local(): received = lax.all_to_all(pieces, ('x', 'y'), 0, 0, tiled=True)  48.4 us
    all_to_all x1, starting transfers between devices, local(): summed = jnp.sum(lax.all_to_all(copies, 'zl', 0, 0, tiled=True), axis=0)  39.2 us
    all_to_all x1, waiting for transfers between devices, local(): summed = jnp.sum(lax.all_to_all(copies, 'zl', 0, 0, tiled=True), axis=0)  24.9 us
    all_gather x1, blocking collectives, local(): own_columns = lax.all_gather(own_columns, 'y', axis=0, tiled=True)  23.1 us
    ppermute x1, waiting for transfers between devices, from_behind(): lax.ppermute(value, axis, [(source, source + steps) for source in range(i...  20.2 us
    ppermute x1, starting transfers between devices, local(): partner_grad = lax.ppermute(half_grad, 'core', swap)  16.3 us
    unnamed x6, local copies, waits for them, and re-layouts  11.2 us
  transfers between devices with their start and end apart: 10, of which 6 were waited for; matrix products, arithmetic and copies ran while one was open for 5% of the time, Pallas kernels for 0%

profile of v8, /device:TPU:1, one launch (start us, length us, event | category | flops | bytes accessed | tf_op | source)
XLA Modules:
  0.0 296.1 jit_solution(1961318982322184690)
XLA Ops:
  7.2 0.0 copy-start
  7.2 0.0 copy-start.1
  7.2 0.0 all-gather.4.cloned.1.call-start
  7.2 0.8 copy-done
  8.1 23.1 %all-gather = bf16[1,192,1152]{2,1,0:T(8,128)(2,1)} all-gather(bf16[1,24,1152]{2,1,0:T(8,128)(2,1)S(1)} %constant_dynamic-slice_fusion.2), channel_id=2, replica_groups=mesh['section'=2,'x'=4,'y'=8,'zl'=8,'core'=2] {'y'}, dimensions={1}, use_global_device_ids=true | all-gather | bytes 497664 | tf_op jit(solution)/shard_map/all_gather | solution.py:55
  31.2 0.0 all-gather.4.cloned.1.call-update
  31.2 51.3 %all-gather.4.cloned.1.call-done = bf16[1,768,1152]{2,1,0:T(8,128)(2,1)} async-done(((bf16[1,192,1152]{2,1,0:T(8,128)(2,1)}), bf16[1,768,1152]{2,1,0:T(8,128)(2,1)}) %all-gather.4.cloned.1.call-update) | async-done | bytes 1769488 | tf_op jit(solution)/shard_map/all_gather | solution.py:56
  82.5 2.7 collective-permute-start.4
  85.3 0.8 fusion.50
  86.1 3.2 %collective-permute-start.2 = (bf16[2,16,768]{2,1,0:T(8,128)(2,1)S(1)}, bf16[2,16,768]{2,1,0:T(8,128)(2,1)S(1)}, u32[]{:S(2)}, u32[]{:S(2)}) collective-permute-start(bf16[2,16,768]{2,1,0:T(8,128)(2,1)S(1)} %get-tuple-element.14), channel_id=1, source_target_pairs={{0,1},{1,2},{2,3},{3,4},{4,5},{5,6},{6,7},{7,8},{8,9},{9,10},{10,1... | collective-permute-start | bytes 147464 | tf_op jit(solution)/shard_map/ppermute | solution.py:17
  89.3 1.9 collective-permute-start.3
  91.2 0.9 broadcast_multiply_fusion
  92.2 0.2 broadcast_in_dim.16
  92.4 0.1 mul.127
  92.6 3.6 %collective-permute-start = (bf16[2,32,768]{2,1,0:T(8,128)(2,1)S(1)}, bf16[2,32,768]{2,1,0:T(8,128)(2,1)S(1)}, u32[]{:S(2)}, u32[]{:S(2)}) collective-permute-start(bf16[2,32,768]{2,1,0:T(8,128)(2,1)S(1)} %get-tuple-element.16), channel_id=1, source_target_pairs={{0,1},{1,2},{2,3},{3,4},{4,5},{5,6},{6,7},{7,8},{8,9},{9,10},{10,1... | collective-permute-start | bytes 294920 | tf_op jit(solution)/shard_map/ppermute | solution.py:17
  96.2 1.9 collective-permute-start.1
  98.2 0.0 collective-permute-done.2
  98.2 0.0 collective-permute-done.3
  98.2 0.0 copy-done.1
  98.2 0.2 fusion.28
  98.4 0.0 collective-permute-done
  98.4 3.8 %collective-permute-done.1 = bf16[2,32,768]{2,1,0:T(8,128)(2,1)S(1)} collective-permute-done((bf16[2,32,768]{2,1,0:T(8,128)(2,1)S(1)}, bf16[2,32,768]{2,1,0:T(8,128)(2,1)S(1)}, u32[]{:S(2)}, u32[]{:S(2)}) %collective-permute-start.1) | collective-permute-done | bytes 98336 | tf_op jit(solution)/shard_map/ppermute | solution.py:18
  102.2 0.0 collective-permute-done.4
  102.2 6.1 %multiply_convert_fusion = (bf16[2,160,768]{2,1,0:T(8,128)(2,1)S(1)}, f32[2,160,768]{2,1,0:T(8,128)}, f32[2,160]{1,0:T(2,128)S(1)}, f32[2,160,768]{2,1,0:T(8,128)S(1)}, f32[2,160,768]{2,1,0:T(8,128)S(1)}) fusion(f32[2,160]{1,0:T(2,128)S(1)} %get-tuple-element.19, bf16[2,16,768]{2,1,0:T(8,128)(2,1)S(1)} %collective-permute-done.3, ...), kind=kOutput, calls=%fused_computation.37 | convolution fusion | flops 1162886912 | bytes 8555009 | tf_op jit(solution)/shard_map/npj,cj->npc/dot_general | solution.py:87
  108.3 0.3 fusion.41
  108.7 1.3 collective-permute-start.5
  110.0 0.1 slice_bitcast_fusion.2
  110.1 20.2 %collective-permute-done.5 = bf16[2,160,768]{2,1,0:T(8,128)(2,1)S(1)} collective-permute-done((bf16[2,160,768]{2,1,0:T(8,128)(2,1)S(1)}, bf16[2,160,768]{2,1,0:T(8,128)(2,1)S(1)}, u32[]{:S(2)}, u32[]{:S(2)}) %collective-permute-start.5) | collective-permute-done | bytes 491552 | tf_op jit(solution)/shard_map/ppermute | solution.py:26
  130.3 0.1 broadcast_select_fusion
  130.3 1.1 fusion.22
  131.4 3.3 %constant_dynamic-slice_fusion = (f32[768,1152]{0,1:T(8,128)}, f32[768,1152]{0,1:T(8,128)}) fusion(f32[768,2304]{0,1:T(8,128)S(1)} %bitcast.39, s32[]{:T(128)S(6)} %select_n.49, s32[]{:T(128)S(6)} %select_n.44), kind=kLoop, calls=%fused_computation.62 | loop fusion | bytes 14155784 | tf_op jit(solution)/shard_map/dynamic_slice | solution.py:136
  134.7 5.2 %copy.16 = f32[768,1152]{1,0:T(8,128)} copy(f32[768,1152]{0,1:T(8,128)} %get-tuple-element.2) | data formatting | bytes 7077888
  139.9 1.9 collective-permute-start.6
  141.8 5.2 %copy.15 = f32[768,1152]{1,0:T(8,128)} copy(f32[768,1152]{0,1:T(8,128)} %get-tuple-element.3) | data formatting | bytes 7077888
  147.0 1.4 collective-permute-done.6
  148.3 3.4 %add_convert_fusion = bf16[768,1152]{1,0:T(8,128)(2,1)S(1)} fusion(f32[768,1152]{1,0:T(8,128)} %copy.15, f32[768,1152]{1,0:T(8,128)} %collective-permute-done.6), kind=kLoop, calls=%fused_computation.3 | loop fusion | flops 1769472 | bytes 8847360 | tf_op jit(solution)/shard_map/convert_element_type | solution.py:138
  151.7 48.4 %all_to_all.10 = bf16[32,24,1152]{2,1,0:T(8,128)(2,1)S(1)} all-to-all(bf16[32,24,1152]{2,1,0:T(8,128)(2,1)S(1)} %bitcast.40), channel_id=1, replica_groups=mesh['section'=2,'x'=4,'y'=8,'zl'=8,'core'=2] {'x','y'}, dimensions={0} | all-to-all | bytes 3538944 | tf_op jit(solution)/shard_map/all_to_all | solution.py:139
  200.1 0.2 convert_reduce_fusion
  200.3 1.0 broadcast_in_dim.32
  201.3 39.2 %all-to-all-start.1 = ((f32[8,24,1152]{2,1,0:T(8,128)}), f32[8,24,1152]{2,1,0:T(8,128)S(1)}, u32[]{:S(2)}, u32[]{:S(2)}) async-start(f32[8,24,1152]{2,1,0:T(8,128)} %broadcast_in_dim.32), calls=%async_computation.1 | async-start | bytes 1769472 | tf_op jit(solution)/shard_map/all_to_all | solution.py:142
  240.6 0.1 slice_bitcast_fusion.3
  240.6 0.1 fusion.49
  240.7 4.7 %multiply_reduce_fusion.1 = (f32[2,128]{1,0:T(2,128)S(1)}, f32[2,128,768]{2,1,0:T(8,128)S(1)}) fusion(f32[2,160,768]{2,1,0:T(8,128)S(1)} %get-tuple-element.7, f32[2,160,768]{2,1,0:T(8,128)} %get-tuple-element.5, bf16[768,1152]{1,0:T(8,128)(2,1)} %collective-permute-done.4, bf16[768,1152]{1,0:T(8,128)(2,1)} %bitcast.48, pred[]{:T(512)S(6)} %eq.8, ...), kind=kOutput, calls=%fused_computation.43 | convolution fusion | flops 926023424 | bytes 7078913 | tf_op jit(solution)/shard_map/npj,cj->npc/dot_general | solution.py:87
  245.4 1.0 fusion.42
  246.4 24.9 %all-to-all-done.1 = f32[8,24,1152]{2,1,0:T(8,128)S(1)} async-done(((f32[8,24,1152]{2,1,0:T(8,128)}), f32[8,24,1152]{2,1,0:T(8,128)S(1)}, u32[]{:S(2)}, u32[]{:S(2)}) %all-to-all-start.1) | async-done | bytes 884768 | tf_op jit(solution)/shard_map/all_to_all | solution.py:142
  271.4 16.3 %collective-permute-start.7 = (bf16[24,1152]{1,0:T(8,128)(2,1)S(1)}, bf16[24,1152]{1,0:T(8,128)(2,1)S(1)}, u32[]{:S(2)}, u32[]{:S(2)}) collective-permute-start(bf16[24,1152]{1,0:T(8,128)(2,1)S(1)} %multiply_convert_fusion.1), channel_id=1, source_target_pairs={{0,1},{1,0},{2,3},{3,2},{4,5},{5,4},{6,7},{7,6},{8,9},{9,8},{10,11... | collective-permute-start | bytes 165896 | tf_op jit(solution)/shard_map/ppermute | solution.py:144
  287.8 0.8 collective-permute-done.7
  288.6 0.7 maximum_select_fusion.1
  (10 shorter events, 0.1 us)
Async XLA Ops:
  7.2 0.9 copy-start
  7.2 91.0 %copy-start.1 = (bf16[1,2,128,768]{3,2,1,0:T(8,128)(2,1)S(1)}, bf16[1,2,128,768]{3,2,1,0:T(8,128)(2,1)}, u32[]{:S(2)}) copy-start(bf16[1,2,128,768]{3,2,1,0:T(8,128)(2,1)} %param.3) | copy-start | bytes 1179652
  7.2 75.3 %all-gather.4.cloned.1.call-start = ((), (), s32[]{:S(2)}) async-start(), calls=%async_computation.2 | async-start | bytes 2211840 | tf_op jit(solution)/shard_map/all_gather | solution.py:56
  82.5 19.7 %collective-permute-start.4 = (bf16[768,1152]{1,0:T(8,128)(2,1)}, bf16[768,1152]{1,0:T(8,128)(2,1)}, u32[]{:S(2)}, u32[]{:S(2)}) collective-permute-start(bf16[768,1152]{1,0:T(8,128)(2,1)} %bitcast.46), channel_id=1, source_target_pairs={{0,1},{1,0},{2,3},{3,2},{4,5},{5,4},{6,7},{7,6},{8,9},{9,8},{10,11... | collective-permute-start | bytes 5308424 | tf_op jit(solution)/shard_map/ppermute | solution.py:57
  86.1 12.1 %collective-permute-start.2 = (bf16[2,16,768]{2,1,0:T(8,128)(2,1)S(1)}, bf16[2,16,768]{2,1,0:T(8,128)(2,1)S(1)}, u32[]{:S(2)}, u32[]{:S(2)}) collective-permute-start(bf16[2,16,768]{2,1,0:T(8,128)(2,1)S(1)} %get-tuple-element.14), channel_id=1, source_target_pairs={{0,1},{1,2},{2,3},{3,4},{4,5},{5,6},{6,7},{7,8},{8,9},{9,10},{10,1... | collective-permute-start | bytes 147464 | tf_op jit(solution)/shard_map/ppermute | solution.py:17
  89.3 8.9 %collective-permute-start.3 = (bf16[2,16,768]{2,1,0:T(8,128)(2,1)S(1)}, bf16[2,16,768]{2,1,0:T(8,128)(2,1)S(1)}, u32[]{:S(2)}, u32[]{:S(2)}) collective-permute-start(bf16[2,16,768]{2,1,0:T(8,128)(2,1)S(1)} %get-tuple-element.15), channel_id=1, source_target_pairs={{1,0},{2,1},{3,2},{4,3},{5,4},{6,5},{7,6},{8,7},{9,8},{10,9},{11,1... | collective-permute-start | bytes 147464 | tf_op jit(solution)/shard_map/ppermute | solution.py:18
  92.6 5.8 %collective-permute-start = (bf16[2,32,768]{2,1,0:T(8,128)(2,1)S(1)}, bf16[2,32,768]{2,1,0:T(8,128)(2,1)S(1)}, u32[]{:S(2)}, u32[]{:S(2)}) collective-permute-start(bf16[2,32,768]{2,1,0:T(8,128)(2,1)S(1)} %get-tuple-element.16), channel_id=1, source_target_pairs={{0,1},{1,2},{2,3},{3,4},{4,5},{5,6},{6,7},{7,8},{8,9},{9,10},{10,1... | collective-permute-start | bytes 294920 | tf_op jit(solution)/shard_map/ppermute | solution.py:17
  96.2 5.9 %collective-permute-start.1 = (bf16[2,32,768]{2,1,0:T(8,128)(2,1)S(1)}, bf16[2,32,768]{2,1,0:T(8,128)(2,1)S(1)}, u32[]{:S(2)}, u32[]{:S(2)}) collective-permute-start(bf16[2,32,768]{2,1,0:T(8,128)(2,1)S(1)} %get-tuple-element.17), channel_id=1, source_target_pairs={{1,0},{2,1},{3,2},{4,3},{5,4},{6,5},{7,6},{8,7},{9,8},{10,9},{11,1... | collective-permute-start | bytes 294920 | tf_op jit(solution)/shard_map/ppermute | solution.py:18
  108.7 21.6 %collective-permute-start.5 = (bf16[2,160,768]{2,1,0:T(8,128)(2,1)S(1)}, bf16[2,160,768]{2,1,0:T(8,128)(2,1)S(1)}, u32[]{:S(2)}, u32[]{:S(2)}) collective-permute-start(bf16[2,160,768]{2,1,0:T(8,128)(2,1)S(1)} %fusion.41), channel_id=1, source_target_pairs={{512,0},{513,1},{514,2},{515,3},{516,4},{517,5},{518,6},{519,7},{5... | collective-permute-start | bytes 1474568 | tf_op jit(solution)/shard_map/ppermute | solution.py:26
  139.9 8.4 %collective-permute-start.6 = (f32[768,1152]{1,0:T(8,128)}, f32[768,1152]{1,0:T(8,128)}, u32[]{:S(2)}, u32[]{:S(2)}) collective-permute-start(f32[768,1152]{1,0:T(8,128)} %copy.16), channel_id=1, source_target_pairs={{0,1},{1,0},{2,3},{3,2},{4,5},{5,4},{6,7},{7,6},{8,9},{9,8},{10,11... | collective-permute-start | bytes 10616840 | tf_op jit(solution)/shard_map/ppermute | solution.py:137
  201.3 70.0 %all-to-all-start.1 = ((f32[8,24,1152]{2,1,0:T(8,128)}), f32[8,24,1152]{2,1,0:T(8,128)S(1)}, u32[]{:S(2)}, u32[]{:S(2)}) async-start(f32[8,24,1152]{2,1,0:T(8,128)} %broadcast_in_dim.32), calls=%async_computation.1 | async-start | bytes 1769472 | tf_op jit(solution)/shard_map/all_to_all | solution.py:142
  271.4 17.2 %collective-permute-start.7 = (bf16[24,1152]{1,0:T(8,128)(2,1)S(1)}, bf16[24,1152]{1,0:T(8,128)(2,1)S(1)}, u32[]{:S(2)}, u32[]{:S(2)}) collective-permute-start(bf16[24,1152]{1,0:T(8,128)(2,1)S(1)} %multiply_convert_fusion.1), channel_id=1, source_target_pairs={{0,1},{1,0},{2,3},{3,2},{4,5},{5,4},{6,7},{7,6},{8,9},{9,8},{10,11... | collective-permute-start | bytes 165896 | tf_op jit(solution)/shard_map/ppermute | solution.py:144
Sparse Core Ops, SparseCore 0:
  31.3 51.1 all-gather.3

commit v9 on v8

--- a/solution.py
+++ b/solution.py
@@ -131,21 +131,22 @@
     core_index = lax.axis_index("core")
     swap = [(0, 1), (1, 0)]
     owned_rows = channel_width // n_dp
-    half = 3 * channel_width // 2
-    own_half = lax.dynamic_slice_in_dim(grad_total, core_index * half, half, axis=1)
-    other_half = lax.dynamic_slice_in_dim(grad_total, (1 - core_index) * half, half, axis=1)
-    chip_half = own_half + lax.ppermute(other_half, "core", swap)
-    pieces = chip_half.astype(jnp.bfloat16).reshape(n_dp, owned_rows, half)
-    received = lax.all_to_all(pieces, ("x", "y"), 0, 0, tiled=True)
+    n_core = lax.axis_size("core")
+    rows_per_core = owned_rows // n_core
+    grouped = grad_total.reshape(n_dp, n_core, rows_per_core, 3 * channel_width)
+    own_rows = lax.dynamic_index_in_dim(grouped, core_index, axis=1, keepdims=False)
+    other_rows = lax.dynamic_index_in_dim(grouped, 1 - core_index, axis=1, keepdims=False)
+    chip_rows = own_rows + lax.ppermute(other_rows, "core", swap)
+    received = lax.all_to_all(chip_rows.astype(jnp.bfloat16), ("x", "y"), 0, 0, tiled=True)
     owned = jnp.sum(received.astype(jnp.float32), axis=0)
-    copies = jnp.broadcast_to(owned[None], (n_zl, owned_rows, half))
+    copies = jnp.broadcast_to(owned[None], (n_zl, rows_per_core, 3 * channel_width))
     summed = jnp.sum(lax.all_to_all(copies, "zl", 0, 0, tiled=True), axis=0)
-    half_grad = (summed / (micro_batch * n_dp)).astype(jnp.bfloat16)
-    partner_grad = lax.ppermute(half_grad, "core", swap)
+    part_grad = (summed / (micro_batch * n_dp)).astype(jnp.bfloat16)
+    partner_grad = lax.ppermute(part_grad, "core", swap)
     weight_grad = jnp.where(
         core_index == 0,
-        jnp.concatenate([half_grad, partner_grad], axis=1),
-        jnp.concatenate([partner_grad, half_grad], axis=1),
+        jnp.concatenate([part_grad, partner_grad], axis=0),
+        jnp.concatenate([partner_grad, part_grad], axis=0),
     )
     return (results[None], weight_grad[None])
 

time: 299 us -> 351 us (1.17)
  local copies, waits for them, and re-layouts: 16.9 us -> 35.2 us
  blocking collectives: 71.5 us -> 86.5 us
  waiting for transfers between devices: 102 us -> 115 us
  starting transfers between devices: 72.2 us -> 76.9 us
    all_to_all x1, blocking collectives: 48.4 us -> 63.4 us  [local(): lax.all_to_all(chip_rows.astype(jnp.bfloat16), ('x', 'y'), 0, 0, tiled=True)]
    another operation x0 -> x1, local copies, waits for them, and re-layouts: none -> 13.4 us  [local(): grouped = grad_total.reshape(n_dp, n_core, rows_per_core, 3 * channel_width)]
    transpose x0 -> x1, local copies, waits for them, and re-layouts: none -> 11 us  [local(): jnp.einsum('knpc,npo->cko', activation_kernel_taps, cotangent_state, pref...]
    unnamed x6, local copies, waits for them, and re-layouts: 11.2 us -> 0.85 us
    all_to_all x1, waiting for transfers between devices: 24.9 us -> 33 us  [local(): summed = jnp.sum(lax.all_to_all(copies, 'zl', 0, 0, tiled=True), axis=0)]
    ppermute x2, waiting for transfers between devices: 2.22 us -> 6.88 us  [the longest x1 6.01 us: local(): chip_rows = own_rows + lax.ppermute(other_rows, 'core', swap)]
    ppermute x2, starting transfers between devices: 18.2 us -> 22.8 us  [the longest x1 20.7 us: local(): partner_grad = lax.ppermute(part_grad, 'core', swap)]
  transfers between devices with their start and end apart: 10 -> 10, of which waited for: 6 -> 6; matrix products, arithmetic and copies ran while one was open for 5% -> 2% of each run, Pallas kernels for 0% -> 0%
where the time goes in v9:
time: 351 us; the launch traced here: 349 us
  waiting for transfers between devices  115 us (33%)
  blocking collectives  86.5 us (25%)
  starting transfers between devices  76.9 us (22%)
  local copies, waits for them, and re-layouts  35.2 us (10%)
  matrix products  15.1 us (4%)
  between operations  14.3 us (4%)
  other arithmetic  5.93 us (2%)
    all_to_all x1, blocking collectives, local(): lax.all_to_all(chip_rows.astype(jnp.bfloat16), ('x', 'y'), 0, 0, tiled=True)  63.4 us
    all_gather x1, waiting for transfers between devices, local(): own_columns = lax.all_gather(own_columns, 'x', axis=0, tiled=True)  51.3 us
    all_to_all x1, starting transfers between devices, local(): summed = jnp.sum(lax.all_to_all(copies, 'zl', 0, 0, tiled=True), axis=0)  39.4 us
    all_to_all x1, waiting for transfers between devices, local(): summed = jnp.sum(lax.all_to_all(copies, 'zl', 0, 0, tiled=True), axis=0)  33 us
    all_gather x1, blocking collectives, local(): own_columns = lax.all_gather(own_columns, 'y', axis=0, tiled=True)  23.1 us
    ppermute x1, starting transfers between devices, local(): partner_grad = lax.ppermute(part_grad, 'core', swap)  20.7 us
    ppermute x1, waiting for transfers between devices, from_behind(): lax.ppermute(value, axis, [(source, source + steps) for source in range(i...  20.2 us
    another operation x1, local copies, waits for them, and re-layouts, local(): grouped = grad_total.reshape(n_dp, n_core, rows_per_core, 3 * channel_width)  13.4 us
  transfers between devices with their start and end apart: 10, of which 6 were waited for; matrix products, arithmetic and copies ran while one was open for 2% of the time, Pallas kernels for 0%

profile of v9, /device:TPU:1, one launch (start us, length us, event | category | flops | bytes accessed | tf_op | source)
XLA Modules:
  0.0 348.9 jit_solution(16639561578706261695)
XLA Ops:
  7.2 0.0 copy-start
  7.2 0.0 copy-start.2
  7.2 0.0 all-gather.4.cloned.1.call-start
  7.2 0.8 copy-done
  8.1 23.1 %all-gather = bf16[1,192,1152]{2,1,0:T(8,128)(2,1)} all-gather(bf16[1,24,1152]{2,1,0:T(8,128)(2,1)S(1)} %constant_dynamic-slice_fusion.2), channel_id=2, replica_groups=mesh['section'=2,'x'=4,'y'=8,'zl'=8,'core'=2] {'y'}, dimensions={1}, use_global_device_ids=true | all-gather | bytes 497664 | tf_op jit(solution)/shard_map/all_gather | solution.py:55
  31.2 0.0 all-gather.4.cloned.1.call-update
  31.2 51.3 %all-gather.4.cloned.1.call-done = bf16[1,768,1152]{2,1,0:T(8,128)(2,1)} async-done(((bf16[1,192,1152]{2,1,0:T(8,128)(2,1)}), bf16[1,768,1152]{2,1,0:T(8,128)(2,1)}) %all-gather.4.cloned.1.call-update) | async-done | bytes 1769488 | tf_op jit(solution)/shard_map/all_gather | solution.py:56
  82.5 2.7 collective-permute-start.4
  85.3 0.8 fusion.50
  86.1 3.2 collective-permute-start.2
  89.3 1.9 collective-permute-start.3
  91.2 0.9 broadcast_multiply_fusion
  92.2 0.2 broadcast_in_dim.16
  92.4 0.1 mul.123
  92.6 3.6 %collective-permute-start = (bf16[2,32,768]{2,1,0:T(8,128)(2,1)S(1)}, bf16[2,32,768]{2,1,0:T(8,128)(2,1)S(1)}, u32[]{:S(2)}, u32[]{:S(2)}) collective-permute-start(bf16[2,32,768]{2,1,0:T(8,128)(2,1)S(1)} %get-tuple-element.16), channel_id=1, source_target_pairs={{0,1},{1,2},{2,3},{3,4},{4,5},{5,6},{6,7},{7,8},{8,9},{9,10},{10,1... | collective-permute-start | bytes 294920 | tf_op jit(solution)/shard_map/ppermute | solution.py:17
  96.2 1.9 collective-permute-start.1
  98.2 0.0 collective-permute-done.2
  98.2 0.0 collective-permute-done.3
  98.2 0.0 copy-done.2
  98.2 0.2 fusion.28
  98.4 0.0 collective-permute-done
  98.4 3.8 %collective-permute-done.1 = bf16[2,32,768]{2,1,0:T(8,128)(2,1)S(1)} collective-permute-done((bf16[2,32,768]{2,1,0:T(8,128)(2,1)S(1)}, bf16[2,32,768]{2,1,0:T(8,128)(2,1)S(1)}, u32[]{:S(2)}, u32[]{:S(2)}) %collective-permute-start.1) | collective-permute-done | bytes 98336 | tf_op jit(solution)/shard_map/ppermute | solution.py:18
  102.2 0.0 collective-permute-done.4
  102.2 6.2 %multiply_convert_fusion = (bf16[2,160,768]{2,1,0:T(8,128)(2,1)S(1)}, f32[2,160,768]{2,1,0:T(8,128)}, f32[2,160]{1,0:T(2,128)S(1)}, f32[2,160,768]{2,1,0:T(8,128)S(1)}, f32[2,160,768]{2,1,0:T(8,128)S(1)}) fusion(f32[2,160]{1,0:T(2,128)S(1)} %get-tuple-element.19, bf16[2,16,768]{2,1,0:T(8,128)(2,1)S(1)} %collective-permute-done.3, ...), kind=kOutput, calls=%fused_computation.39 | convolution fusion | flops 1162886912 | bytes 8555009 | tf_op jit(solution)/shard_map/npj,cj->npc/dot_general | solution.py:87
  108.4 0.3 fusion.41
  108.8 1.3 collective-permute-start.5
  110.1 0.1 slice_bitcast_fusion.2
  110.2 20.2 %collective-permute-done.5 = bf16[2,160,768]{2,1,0:T(8,128)(2,1)S(1)} collective-permute-done((bf16[2,160,768]{2,1,0:T(8,128)(2,1)S(1)}, bf16[2,160,768]{2,1,0:T(8,128)(2,1)S(1)}, u32[]{:S(2)}, u32[]{:S(2)}) %collective-permute-start.5) | collective-permute-done | bytes 491552 | tf_op jit(solution)/shard_map/ppermute | solution.py:26
  130.4 0.1 broadcast_select_fusion
  130.4 4.0 %convolution_bitcast_fusion = f32[768,3,768]{0,2,1:T(8,128)} fusion(bf16[1,2,128,768]{3,2,1,0:T(8,128)(2,1)S(1)} %get-tuple-element.9, bf16[1,2,128,768]{3,2,1,0:T(8,128)(2,1)S(1)} %get-tuple-element.10, bf16[1,2,128,768]{3,2,1,0:T(8,128)(2,1)S(1)} %get-tuple-element.8, bf16[2,160,768]{2,1,0:T(8,128)(2,1)S(1)} %broadcast_select_fusion), kind=kOutput, calls=%fused_computation.6 | convolution fusion | flops 909508608 | bytes 8650752 | tf_op jit(solution)/shard_map/knpc,npo->cko/dot_general | solution.py:125
  134.4 11.0 %copy.25 = f32[768,3,768]{2,1,0:T(4,128)} copy(f32[768,3,768]{0,2,1:T(8,128)} %convolution_bitcast_fusion) | data formatting | bytes 14155776 | tf_op jit(solution)/shard_map/knpc,npo->cko/transpose | solution.py:125
  145.4 13.4 %reshape_reshape.3 = f32[32,2,12,2304]{3,2,1,0:T(8,128)} reshape(f32[768,3,768]{2,1,0:T(4,128)} %copy.25) | data formatting | bytes 14155776 | tf_op jit(solution)/shard_map/reshape;reshape | solution.py:136
  158.7 4.4 %constant_dynamic-slice_fusion.1 = (f32[32,1,12,2304]{3,2,1,0:T(8,128)S(1)}, f32[32,1,12,2304]{3,2,1,0:T(8,128)S(1)}) fusion(f32[32,2,12,2304]{3,2,1,0:T(8,128)} %reshape_reshape.3, s32[]{:T(128)S(6)} %select_n.52, s32[]{:T(128)S(6)} %select_n.53), kind=kLoop, calls=%fused_computation.65 | loop fusion | bytes 14155784 | tf_op jit(solution)/shard_map/jit(dynamic_index_in_dim)/dynamic_slice | solution.py:137
  163.1 2.1 copy.36
  165.2 2.1 collective-permute-start.6
  167.3 6.0 %collective-permute-done.6 = f32[32,12,2304]{2,0,1:T(8,128)S(1)} collective-permute-done((f32[32,12,2304]{2,0,1:T(8,128)S(1)}, f32[32,12,2304]{2,0,1:T(8,128)S(1)}, u32[]{:S(2)}, u32[]{:S(2)}) %collective-permute-start.6) | collective-permute-done | bytes 3538976 | tf_op jit(solution)/shard_map/ppermute | solution.py:139
  173.3 2.1 fusion.1
  175.5 1.0 copy.28
  176.5 63.4 %all_to_all.10 = bf16[32,12,2304]{2,1,0:T(8,128)(2,1)S(1)} all-to-all(bf16[32,12,2304]{2,1,0:T(8,128)(2,1)S(1)} %copy.28), channel_id=1, replica_groups=mesh['section'=2,'x'=4,'y'=8,'zl'=8,'core'=2] {'x','y'}, dimensions={0} | all-to-all | bytes 3538944 | tf_op jit(solution)/shard_map/all_to_all | solution.py:140
  239.8 0.4 convert_reduce_fusion
  240.2 1.1 broadcast_in_dim.32
  241.3 39.4 %all-to-all-start.1 = ((f32[8,12,2304]{2,1,0:T(8,128)}), f32[8,12,2304]{2,1,0:T(8,128)S(1)}, u32[]{:S(2)}, u32[]{:S(2)}) async-start(f32[8,12,2304]{2,1,0:T(8,128)} %broadcast_in_dim.32), calls=%async_computation.1 | async-start | bytes 2359296 | tf_op jit(solution)/shard_map/all_to_all | solution.py:143
  280.7 0.1 slice_bitcast_fusion.3
  280.8 0.1 fusion.49
  280.8 0.0 copy-start.1
  280.9 4.9 %multiply_reduce_fusion.1 = (f32[2,128]{1,0:T(2,128)S(1)}, f32[2,128,768]{2,1,0:T(8,128)S(1)}) fusion(f32[2,160,768]{2,1,0:T(8,128)S(1)} %get-tuple-element.7, f32[2,160,768]{2,1,0:T(8,128)} %get-tuple-element.5, bf16[768,1152]{1,0:T(8,128)(2,1)} %collective-permute-done.4, bf16[768,1152]{1,0:T(8,128)(2,1)} %bitcast.52, pred[]{:T(512)S(6)} %eq.8, ...), kind=kOutput, calls=%fused_computation.45 | convolution fusion | flops 926023424 | bytes 7078913 | tf_op jit(solution)/shard_map/npj,cj->npc/dot_general | solution.py:87
  285.7 1.0 fusion.42
  286.7 33.0 %all-to-all-done.1 = f32[8,12,2304]{2,1,0:T(8,128)S(1)} async-done(((f32[8,12,2304]{2,1,0:T(8,128)}), f32[8,12,2304]{2,1,0:T(8,128)S(1)}, u32[]{:S(2)}, u32[]{:S(2)}) %all-to-all-start.1) | async-done | bytes 884768 | tf_op jit(solution)/shard_map/all_to_all | solution.py:143
  319.7 0.1 reduce_sum.49
  319.8 20.7 %collective-permute-start.7 = (bf16[12,2304]{1,0:T(8,128)(2,1)S(1)}, bf16[12,2304]{1,0:T(8,128)(2,1)S(1)}, u32[]{:S(2)}, u32[]{:S(2)}) collective-permute-start(bf16[12,2304]{1,0:T(8,128)(2,1)S(1)} %multiply_convert_fusion.1), channel_id=1, source_target_pairs={{0,1},{1,0},{2,3},{3,2},{4,5},{5,4},{6,7},{7,6},{8,9},{9,8},{10,11... | collective-permute-start | bytes 165896 | tf_op jit(solution)/shard_map/ppermute | solution.py:145
  340.5 0.9 collective-permute-done.7
  341.4 0.7 maximum_select_fusion.1
  342.1 0.0 copy-done.1
  (9 shorter events, 0.1 us)
Async XLA Ops:
  7.2 0.9 copy-start
  7.2 91.0 %copy-start.2 = (bf16[1,2,128,768]{3,2,1,0:T(8,128)(2,1)S(1)}, bf16[1,2,128,768]{3,2,1,0:T(8,128)(2,1)}, u32[]{:S(2)}) copy-start(bf16[1,2,128,768]{3,2,1,0:T(8,128)(2,1)} %param.3) | copy-start | bytes 1179652
  7.2 75.3 %all-gather.4.cloned.1.call-start = ((), (), s32[]{:S(2)}) async-start(), calls=%async_computation.2 | async-start | bytes 2211840 | tf_op jit(solution)/shard_map/all_gather | solution.py:56
  82.5 19.7 %collective-permute-start.4 = (bf16[768,1152]{1,0:T(8,128)(2,1)}, bf16[768,1152]{1,0:T(8,128)(2,1)}, u32[]{:S(2)}, u32[]{:S(2)}) collective-permute-start(bf16[768,1152]{1,0:T(8,128)(2,1)} %bitcast.50), channel_id=1, source_target_pairs={{0,1},{1,0},{2,3},{3,2},{4,5},{5,4},{6,7},{7,6},{8,9},{9,8},{10,11... | collective-permute-start | bytes 5308424 | tf_op jit(solution)/shard_map/ppermute | solution.py:57
  86.1 12.1 %collective-permute-start.2 = (bf16[2,16,768]{2,1,0:T(8,128)(2,1)S(1)}, bf16[2,16,768]{2,1,0:T(8,128)(2,1)S(1)}, u32[]{:S(2)}, u32[]{:S(2)}) collective-permute-start(bf16[2,16,768]{2,1,0:T(8,128)(2,1)S(1)} %get-tuple-element.14), channel_id=1, source_target_pairs={{0,1},{1,2},{2,3},{3,4},{4,5},{5,6},{6,7},{7,8},{8,9},{9,10},{10,1... | collective-permute-start | bytes 147464 | tf_op jit(solution)/shard_map/ppermute | solution.py:17
  89.3 8.9 %collective-permute-start.3 = (bf16[2,16,768]{2,1,0:T(8,128)(2,1)S(1)}, bf16[2,16,768]{2,1,0:T(8,128)(2,1)S(1)}, u32[]{:S(2)}, u32[]{:S(2)}) collective-permute-start(bf16[2,16,768]{2,1,0:T(8,128)(2,1)S(1)} %get-tuple-element.15), channel_id=1, source_target_pairs={{1,0},{2,1},{3,2},{4,3},{5,4},{6,5},{7,6},{8,7},{9,8},{10,9},{11,1... | collective-permute-start | bytes 147464 | tf_op jit(solution)/shard_map/ppermute | solution.py:18
  92.6 5.8 %collective-permute-start = (bf16[2,32,768]{2,1,0:T(8,128)(2,1)S(1)}, bf16[2,32,768]{2,1,0:T(8,128)(2,1)S(1)}, u32[]{:S(2)}, u32[]{:S(2)}) collective-permute-start(bf16[2,32,768]{2,1,0:T(8,128)(2,1)S(1)} %get-tuple-element.16), channel_id=1, source_target_pairs={{0,1},{1,2},{2,3},{3,4},{4,5},{5,6},{6,7},{7,8},{8,9},{9,10},{10,1... | collective-permute-start | bytes 294920 | tf_op jit(solution)/shard_map/ppermute | solution.py:17
  96.2 5.9 %collective-permute-start.1 = (bf16[2,32,768]{2,1,0:T(8,128)(2,1)S(1)}, bf16[2,32,768]{2,1,0:T(8,128)(2,1)S(1)}, u32[]{:S(2)}, u32[]{:S(2)}) collective-permute-start(bf16[2,32,768]{2,1,0:T(8,128)(2,1)S(1)} %get-tuple-element.17), channel_id=1, source_target_pairs={{1,0},{2,1},{3,2},{4,3},{5,4},{6,5},{7,6},{8,7},{9,8},{10,9},{11,1... | collective-permute-start | bytes 294920 | tf_op jit(solution)/shard_map/ppermute | solution.py:18
  108.8 21.6 %collective-permute-start.5 = (bf16[2,160,768]{2,1,0:T(8,128)(2,1)S(1)}, bf16[2,160,768]{2,1,0:T(8,128)(2,1)S(1)}, u32[]{:S(2)}, u32[]{:S(2)}) collective-permute-start(bf16[2,160,768]{2,1,0:T(8,128)(2,1)S(1)} %fusion.41), channel_id=1, source_target_pairs={{512,0},{513,1},{514,2},{515,3},{516,4},{517,5},{518,6},{519,7},{5... | collective-permute-start | bytes 1474568 | tf_op jit(solution)/shard_map/ppermute | solution.py:26
  165.2 8.1 %collective-permute-start.6 = (f32[32,12,2304]{2,0,1:T(8,128)S(1)}, f32[32,12,2304]{2,0,1:T(8,128)S(1)}, u32[]{:S(2)}, u32[]{:S(2)}) collective-permute-start(f32[32,12,2304]{2,0,1:T(8,128)S(1)} %bitcast.44), channel_id=1, source_target_pairs={{0,1},{1,0},{2,3},{3,2},{4,5},{5,4},{6,7},{7,6},{8,9},{9,8},{10,11... | collective-permute-start | bytes 10616840 | tf_op jit(solution)/shard_map/ppermute | solution.py:139
  241.3 78.4 %all-to-all-start.1 = ((f32[8,12,2304]{2,1,0:T(8,128)}), f32[8,12,2304]{2,1,0:T(8,128)S(1)}, u32[]{:S(2)}, u32[]{:S(2)}) async-start(f32[8,12,2304]{2,1,0:T(8,128)} %broadcast_in_dim.32), calls=%async_computation.1 | async-start | bytes 2359296 | tf_op jit(solution)/shard_map/all_to_all | solution.py:143
  280.8 61.3 %copy-start.1 = (bf16[1,24,2304]{2,1,0:T(8,128)(2,1)S(1)}, bf16[1,24,2304]{2,1,0:T(8,128)(2,1)}, u32[]{:S(2)}) copy-start(bf16[1,24,2304]{2,1,0:T(8,128)(2,1)} %param.5) | copy-start | bytes 331780
  319.8 21.6 %collective-permute-start.7 = (bf16[12,2304]{1,0:T(8,128)(2,1)S(1)}, bf16[12,2304]{1,0:T(8,128)(2,1)S(1)}, u32[]{:S(2)}, u32[]{:S(2)}) collective-permute-start(bf16[12,2304]{1,0:T(8,128)(2,1)S(1)} %multiply_convert_fusion.1), channel_id=1, source_target_pairs={{0,1},{1,0},{2,3},{3,2},{4,5},{5,4},{6,7},{7,6},{8,9},{9,8},{10,11... | collective-permute-start | bytes 165896 | tf_op jit(solution)/shard_map/ppermute | solution.py:145
Sparse Core Ops, SparseCore 0:
  31.3 51.1 all-gather.3

commit v10 on v8

--- a/solution.py
+++ b/solution.py
@@ -138,8 +138,8 @@
     pieces = chip_half.astype(jnp.bfloat16).reshape(n_dp, owned_rows, half)
     received = lax.all_to_all(pieces, ("x", "y"), 0, 0, tiled=True)
     owned = jnp.sum(received.astype(jnp.float32), axis=0)
-    copies = jnp.broadcast_to(owned[None], (n_zl, owned_rows, half))
-    summed = jnp.sum(lax.all_to_all(copies, "zl", 0, 0, tiled=True), axis=0)
+    copies = jnp.broadcast_to(owned.astype(jnp.bfloat16)[None], (n_zl, owned_rows, half))
+    summed = jnp.sum(lax.all_to_all(copies, "zl", 0, 0, tiled=True).astype(jnp.float32), axis=0)
     half_grad = (summed / (micro_batch * n_dp)).astype(jnp.bfloat16)
     partner_grad = lax.ppermute(half_grad, "core", swap)
     weight_grad = jnp.where(

time: 299 us -> 280 us (0.936)
  waiting for transfers between devices: 102 us -> 86.6 us
  starting transfers between devices: 72.2 us -> 68.9 us
    all_to_all x1, waiting for transfers between devices: 24.9 us -> 9.14 us  [local(): lax.all_to_all(copies, 'zl', 0, 0, tiled=True).astype(jnp.float32)]
    ppermute x1, starting transfers between devices: 16.3 us -> 13.1 us  [local(): partner_grad = lax.ppermute(half_grad, 'core', swap)]
where the time goes in v10:
time: 280 us; the launch traced here: 277 us
  waiting for transfers between devices  86.6 us (31%)
  blocking collectives  71.5 us (26%)
  starting transfers between devices  68.9 us (25%)
  local copies, waits for them, and re-layouts  16.7 us (6%)
  between operations  14.3 us (5%)
  matrix products  11.9 us (4%)
  other arithmetic  6.99 us (2%)
    all_gather x1, waiting for transfers between devices, local(): own_columns = lax.all_gather(own_columns, 'x', axis=0, tiled=True)  51.3 us
    all_to_all x1, blocking collectives, local(): received = lax.all_to_all(pieces, ('x', 'y'), 0, 0, tiled=True)  48.4 us
    all_to_all x1, starting transfers between devices, local(): lax.all_to_all(copies, 'zl', 0, 0, tiled=True).astype(jnp.float32)  39.2 us
    all_gather x1, blocking collectives, local(): own_columns = lax.all_gather(own_columns, 'y', axis=0, tiled=True)  23.1 us
    ppermute x1, waiting for transfers between devices, from_behind(): lax.ppermute(value, axis, [(source, source + steps) for source in range(i...  20.2 us
    ppermute x1, starting transfers between devices, local(): partner_grad = lax.ppermute(half_grad, 'core', swap)  13.1 us
    unnamed x6, local copies, waits for them, and re-layouts  11.2 us
    dot_general x2, matrix products, block(): jnp.einsum('npj,cj->npc', cotangent_kernel_taps, full_kernel, preferred_e...  10.8 us
  transfers between devices with their start and end apart: 10, of which 6 were waited for; matrix products, arithmetic and copies ran while one was open for 5% of the time, Pallas kernels for 0%

profile of v10, /device:TPU:1, one launch (start us, length us, event | category | flops | bytes accessed | tf_op | source)
XLA Modules:
  0.0 276.9 jit_solution(7346691688057407059)
XLA Ops:
  7.2 0.0 copy-start
  7.2 0.0 copy-start.1
  7.2 0.0 all-gather.4.cloned.1.call-start
  7.2 0.8 copy-done
  8.1 23.1 %all-gather = bf16[1,192,1152]{2,1,0:T(8,128)(2,1)} all-gather(bf16[1,24,1152]{2,1,0:T(8,128)(2,1)S(1)} %constant_dynamic-slice_fusion.2), channel_id=2, replica_groups=mesh['section'=2,'x'=4,'y'=8,'zl'=8,'core'=2] {'y'}, dimensions={1}, use_global_device_ids=true | all-gather | bytes 497664 | tf_op jit(solution)/shard_map/all_gather | solution.py:55
  31.2 0.0 all-gather.4.cloned.1.call-update
  31.2 51.3 %all-gather.4.cloned.1.call-done = bf16[1,768,1152]{2,1,0:T(8,128)(2,1)} async-done(((bf16[1,192,1152]{2,1,0:T(8,128)(2,1)}), bf16[1,768,1152]{2,1,0:T(8,128)(2,1)}) %all-gather.4.cloned.1.call-update) | async-done | bytes 1769488 | tf_op jit(solution)/shard_map/all_gather | solution.py:56
  82.5 2.7 collective-permute-start.4
  85.3 0.8 fusion.50
  86.1 3.2 %collective-permute-start.2 = (bf16[2,16,768]{2,1,0:T(8,128)(2,1)S(1)}, bf16[2,16,768]{2,1,0:T(8,128)(2,1)S(1)}, u32[]{:S(2)}, u32[]{:S(2)}) collective-permute-start(bf16[2,16,768]{2,1,0:T(8,128)(2,1)S(1)} %get-tuple-element.14), channel_id=1, source_target_pairs={{0,1},{1,2},{2,3},{3,4},{4,5},{5,6},{6,7},{7,8},{8,9},{9,10},{10,1... | collective-permute-start | bytes 147464 | tf_op jit(solution)/shard_map/ppermute | solution.py:17
  89.3 1.9 collective-permute-start.3
  91.2 0.9 broadcast_multiply_fusion
  92.2 0.2 broadcast_in_dim.16
  92.4 0.1 mul.127
  92.6 3.6 %collective-permute-start = (bf16[2,32,768]{2,1,0:T(8,128)(2,1)S(1)}, bf16[2,32,768]{2,1,0:T(8,128)(2,1)S(1)}, u32[]{:S(2)}, u32[]{:S(2)}) collective-permute-start(bf16[2,32,768]{2,1,0:T(8,128)(2,1)S(1)} %get-tuple-element.16), channel_id=1, source_target_pairs={{0,1},{1,2},{2,3},{3,4},{4,5},{5,6},{6,7},{7,8},{8,9},{9,10},{10,1... | collective-permute-start | bytes 294920 | tf_op jit(solution)/shard_map/ppermute | solution.py:17
  96.2 1.9 collective-permute-start.1
  98.2 0.0 collective-permute-done.2
  98.2 0.0 collective-permute-done.3
  98.2 0.0 copy-done.1
  98.2 0.2 fusion.28
  98.4 0.0 collective-permute-done
  98.4 3.8 %collective-permute-done.1 = bf16[2,32,768]{2,1,0:T(8,128)(2,1)S(1)} collective-permute-done((bf16[2,32,768]{2,1,0:T(8,128)(2,1)S(1)}, bf16[2,32,768]{2,1,0:T(8,128)(2,1)S(1)}, u32[]{:S(2)}, u32[]{:S(2)}) %collective-permute-start.1) | collective-permute-done | bytes 98336 | tf_op jit(solution)/shard_map/ppermute | solution.py:18
  102.2 0.0 collective-permute-done.4
  102.2 6.1 %multiply_convert_fusion = (bf16[2,160,768]{2,1,0:T(8,128)(2,1)S(1)}, f32[2,160,768]{2,1,0:T(8,128)}, f32[2,160]{1,0:T(2,128)S(1)}, f32[2,160,768]{2,1,0:T(8,128)S(1)}, f32[2,160,768]{2,1,0:T(8,128)S(1)}) fusion(f32[2,160]{1,0:T(2,128)S(1)} %get-tuple-element.19, bf16[2,16,768]{2,1,0:T(8,128)(2,1)S(1)} %collective-permute-done.3, ...), kind=kOutput, calls=%fused_computation.36 | convolution fusion | flops 1162886912 | bytes 8555009 | tf_op jit(solution)/shard_map/npj,cj->npc/dot_general | solution.py:87
  108.3 0.3 fusion.41
  108.7 1.3 collective-permute-start.5
  110.0 0.1 slice_bitcast_fusion.2
  110.1 20.2 %collective-permute-done.5 = bf16[2,160,768]{2,1,0:T(8,128)(2,1)S(1)} collective-permute-done((bf16[2,160,768]{2,1,0:T(8,128)(2,1)S(1)}, bf16[2,160,768]{2,1,0:T(8,128)(2,1)S(1)}, u32[]{:S(2)}, u32[]{:S(2)}) %collective-permute-start.5) | collective-permute-done | bytes 491552 | tf_op jit(solution)/shard_map/ppermute | solution.py:26
  130.3 0.1 broadcast_select_fusion
  130.3 1.1 fusion.22
  131.4 3.3 %constant_dynamic-slice_fusion = (f32[768,1152]{0,1:T(8,128)}, f32[768,1152]{0,1:T(8,128)}) fusion(f32[768,2304]{0,1:T(8,128)S(1)} %bitcast.39, s32[]{:T(128)S(6)} %select_n.49, s32[]{:T(128)S(6)} %select_n.44), kind=kLoop, calls=%fused_computation.62 | loop fusion | bytes 14155784 | tf_op jit(solution)/shard_map/dynamic_slice | solution.py:136
  134.7 5.2 %copy.16 = f32[768,1152]{1,0:T(8,128)} copy(f32[768,1152]{0,1:T(8,128)} %get-tuple-element.2) | data formatting | bytes 7077888
  139.9 1.9 collective-permute-start.6
  141.8 5.2 %copy.15 = f32[768,1152]{1,0:T(8,128)} copy(f32[768,1152]{0,1:T(8,128)} %get-tuple-element.3) | data formatting | bytes 7077888
  147.0 1.4 collective-permute-done.6
  148.3 3.4 %add_convert_fusion = bf16[768,1152]{1,0:T(8,128)(2,1)S(1)} fusion(f32[768,1152]{1,0:T(8,128)} %copy.15, f32[768,1152]{1,0:T(8,128)} %collective-permute-done.6), kind=kLoop, calls=%fused_computation.2 | loop fusion | flops 1769472 | bytes 8847360 | tf_op jit(solution)/shard_map/convert_element_type | solution.py:138
  151.7 48.4 %all_to_all.10 = bf16[32,24,1152]{2,1,0:T(8,128)(2,1)S(1)} all-to-all(bf16[32,24,1152]{2,1,0:T(8,128)(2,1)S(1)} %bitcast.40), channel_id=1, replica_groups=mesh['section'=2,'x'=4,'y'=8,'zl'=8,'core'=2] {'x','y'}, dimensions={0} | all-to-all | bytes 3538944 | tf_op jit(solution)/shard_map/all_to_all | solution.py:139
  200.1 0.3 reduce_sum.51
  200.3 0.8 broadcast_in_dim.32
  201.1 39.2 %all-to-all-start.1 = ((bf16[8,24,1152]{2,1,0:T(8,128)(2,1)}), bf16[8,24,1152]{2,1,0:T(8,128)(2,1)S(1)}, u32[]{:S(2)}, u32[]{:S(2)}) async-start(bf16[8,24,1152]{2,1,0:T(8,128)(2,1)} %broadcast_in_dim.32), calls=%async_computation.1 | async-start | bytes 884736 | tf_op jit(solution)/shard_map/all_to_all | solution.py:142
  240.4 0.1 slice_bitcast_fusion.3
  240.4 0.1 fusion.49
  240.5 4.7 %multiply_reduce_fusion.1 = (f32[2,128]{1,0:T(2,128)S(1)}, f32[2,128,768]{2,1,0:T(8,128)S(1)}) fusion(f32[2,160,768]{2,1,0:T(8,128)S(1)} %get-tuple-element.7, f32[2,160,768]{2,1,0:T(8,128)} %get-tuple-element.5, bf16[768,1152]{1,0:T(8,128)(2,1)} %collective-permute-done.4, bf16[768,1152]{1,0:T(8,128)(2,1)} %bitcast.48, pred[]{:T(512)S(6)} %eq.8, ...), kind=kOutput, calls=%fused_computation.43 | convolution fusion | flops 926023424 | bytes 7078913 | tf_op jit(solution)/shard_map/npj,cj->npc/dot_general | solution.py:87
  245.2 1.0 fusion.42
  246.2 9.1 %all-to-all-done.1 = bf16[8,24,1152]{2,1,0:T(8,128)(2,1)S(1)} async-done(((bf16[8,24,1152]{2,1,0:T(8,128)(2,1)}), bf16[8,24,1152]{2,1,0:T(8,128)(2,1)S(1)}, u32[]{:S(2)}, u32[]{:S(2)}) %all-to-all-start.1) | async-done | bytes 442400 | tf_op jit(solution)/shard_map/all_to_all | solution.py:142
  255.4 0.1 convert_reduce_fusion
  255.5 13.1 %collective-permute-start.7 = (bf16[24,1152]{1,0:T(8,128)(2,1)S(1)}, bf16[24,1152]{1,0:T(8,128)(2,1)S(1)}, u32[]{:S(2)}, u32[]{:S(2)}) collective-permute-start(bf16[24,1152]{1,0:T(8,128)(2,1)S(1)} %multiply_convert_fusion.1), channel_id=1, source_target_pairs={{0,1},{1,0},{2,3},{3,2},{4,5},{5,4},{6,7},{7,6},{8,9},{9,8},{10,11... | collective-permute-start | bytes 165896 | tf_op jit(solution)/shard_map/ppermute | solution.py:144
  268.6 0.8 collective-permute-done.7
  269.4 0.7 maximum_select_fusion.1
  (9 shorter events, 0.1 us)
Async XLA Ops:
  7.2 0.9 copy-start
  7.2 91.0 %copy-start.1 = (bf16[1,2,128,768]{3,2,1,0:T(8,128)(2,1)S(1)}, bf16[1,2,128,768]{3,2,1,0:T(8,128)(2,1)}, u32[]{:S(2)}) copy-start(bf16[1,2,128,768]{3,2,1,0:T(8,128)(2,1)} %param.3) | copy-start | bytes 1179652
  7.2 75.3 %all-gather.4.cloned.1.call-start = ((), (), s32[]{:S(2)}) async-start(), calls=%async_computation.2 | async-start | bytes 2211840 | tf_op jit(solution)/shard_map/all_gather | solution.py:56
  82.5 19.7 %collective-permute-start.4 = (bf16[768,1152]{1,0:T(8,128)(2,1)}, bf16[768,1152]{1,0:T(8,128)(2,1)}, u32[]{:S(2)}, u32[]{:S(2)}) collective-permute-start(bf16[768,1152]{1,0:T(8,128)(2,1)} %bitcast.46), channel_id=1, source_target_pairs={{0,1},{1,0},{2,3},{3,2},{4,5},{5,4},{6,7},{7,6},{8,9},{9,8},{10,11... | collective-permute-start | bytes 5308424 | tf_op jit(solution)/shard_map/ppermute | solution.py:57
  86.1 12.1 %collective-permute-start.2 = (bf16[2,16,768]{2,1,0:T(8,128)(2,1)S(1)}, bf16[2,16,768]{2,1,0:T(8,128)(2,1)S(1)}, u32[]{:S(2)}, u32[]{:S(2)}) collective-permute-start(bf16[2,16,768]{2,1,0:T(8,128)(2,1)S(1)} %get-tuple-element.14), channel_id=1, source_target_pairs={{0,1},{1,2},{2,3},{3,4},{4,5},{5,6},{6,7},{7,8},{8,9},{9,10},{10,1... | collective-permute-start | bytes 147464 | tf_op jit(solution)/shard_map/ppermute | solution.py:17
  89.3 8.9 %collective-permute-start.3 = (bf16[2,16,768]{2,1,0:T(8,128)(2,1)S(1)}, bf16[2,16,768]{2,1,0:T(8,128)(2,1)S(1)}, u32[]{:S(2)}, u32[]{:S(2)}) collective-permute-start(bf16[2,16,768]{2,1,0:T(8,128)(2,1)S(1)} %get-tuple-element.15), channel_id=1, source_target_pairs={{1,0},{2,1},{3,2},{4,3},{5,4},{6,5},{7,6},{8,7},{9,8},{10,9},{11,1... | collective-permute-start | bytes 147464 | tf_op jit(solution)/shard_map/ppermute | solution.py:18
  92.6 5.8 %collective-permute-start = (bf16[2,32,768]{2,1,0:T(8,128)(2,1)S(1)}, bf16[2,32,768]{2,1,0:T(8,128)(2,1)S(1)}, u32[]{:S(2)}, u32[]{:S(2)}) collective-permute-start(bf16[2,32,768]{2,1,0:T(8,128)(2,1)S(1)} %get-tuple-element.16), channel_id=1, source_target_pairs={{0,1},{1,2},{2,3},{3,4},{4,5},{5,6},{6,7},{7,8},{8,9},{9,10},{10,1... | collective-permute-start | bytes 294920 | tf_op jit(solution)/shard_map/ppermute | solution.py:17
  96.2 5.9 %collective-permute-start.1 = (bf16[2,32,768]{2,1,0:T(8,128)(2,1)S(1)}, bf16[2,32,768]{2,1,0:T(8,128)(2,1)S(1)}, u32[]{:S(2)}, u32[]{:S(2)}) collective-permute-start(bf16[2,32,768]{2,1,0:T(8,128)(2,1)S(1)} %get-tuple-element.17), channel_id=1, source_target_pairs={{1,0},{2,1},{3,2},{4,3},{5,4},{6,5},{7,6},{8,7},{9,8},{10,9},{11,1... | collective-permute-start | bytes 294920 | tf_op jit(solution)/shard_map/ppermute | solution.py:18
  108.7 21.6 %collective-permute-start.5 = (bf16[2,160,768]{2,1,0:T(8,128)(2,1)S(1)}, bf16[2,160,768]{2,1,0:T(8,128)(2,1)S(1)}, u32[]{:S(2)}, u32[]{:S(2)}) collective-permute-start(bf16[2,160,768]{2,1,0:T(8,128)(2,1)S(1)} %fusion.41), channel_id=1, source_target_pairs={{512,0},{513,1},{514,2},{515,3},{516,4},{517,5},{518,6},{519,7},{5... | collective-permute-start | bytes 1474568 | tf_op jit(solution)/shard_map/ppermute | solution.py:26
  139.9 8.4 %collective-permute-start.6 = (f32[768,1152]{1,0:T(8,128)}, f32[768,1152]{1,0:T(8,128)}, u32[]{:S(2)}, u32[]{:S(2)}) collective-permute-start(f32[768,1152]{1,0:T(8,128)} %copy.16), channel_id=1, source_target_pairs={{0,1},{1,0},{2,3},{3,2},{4,5},{5,4},{6,7},{7,6},{8,9},{9,8},{10,11... | collective-permute-start | bytes 10616840 | tf_op jit(solution)/shard_map/ppermute | solution.py:137
  201.1 54.2 %all-to-all-start.1 = ((bf16[8,24,1152]{2,1,0:T(8,128)(2,1)}), bf16[8,24,1152]{2,1,0:T(8,128)(2,1)S(1)}, u32[]{:S(2)}, u32[]{:S(2)}) async-start(bf16[8,24,1152]{2,1,0:T(8,128)(2,1)} %broadcast_in_dim.32), calls=%async_computation.1 | async-start | bytes 884736 | tf_op jit(solution)/shard_map/all_to_all | solution.py:142
  255.5 14.0 %collective-permute-start.7 = (bf16[24,1152]{1,0:T(8,128)(2,1)S(1)}, bf16[24,1152]{1,0:T(8,128)(2,1)S(1)}, u32[]{:S(2)}, u32[]{:S(2)}) collective-permute-start(bf16[24,1152]{1,0:T(8,128)(2,1)S(1)} %multiply_convert_fusion.1), channel_id=1, source_target_pairs={{0,1},{1,0},{2,3},{3,2},{4,5},{5,4},{6,7},{7,6},{8,9},{9,8},{10,11... | collective-permute-start | bytes 165896 | tf_op jit(solution)/shard_map/ppermute | solution.py:144
Sparse Core Ops, SparseCore 0:
  31.3 51.1 all-gather.3

commit v11 on v10

--- a/solution.py
+++ b/solution.py
@@ -52,8 +52,10 @@
     kernel_core = lax.axis_index("core")
     kernel_half = weights.shape[2] // 2
     own_columns = lax.dynamic_slice_in_dim(weights[0], kernel_core * kernel_half, kernel_half, axis=1)
-    own_columns = lax.all_gather(own_columns, "y", axis=0, tiled=True)
-    own_columns = lax.all_gather(own_columns, "x", axis=0, tiled=True)
+    n_gx, n_gy = lax.axis_size("x"), lax.axis_size("y")
+    own_columns = lax.all_gather(own_columns, "x", axis=0, tiled=False)
+    own_columns = lax.all_gather(own_columns, "y", axis=1, tiled=False)
+    own_columns = own_columns.reshape(n_gx * n_gy * own_columns.shape[2], kernel_half)
     partner_columns = lax.ppermute(own_columns, "core", [(0, 1), (1, 0)])
     full_kernel = jnp.where(
         kernel_core == 0,

time: 280 us -> 274 us (0.979)
  blocking collectives: 71.5 us -> 58.3 us
  starting transfers between devices: 68.9 us -> 72.9 us
  waiting for transfers between devices: 86.6 us -> 89.6 us
    all_gather x1, blocking collectives: 23.1 us -> 11.2 us  [local(): own_columns = lax.all_gather(own_columns, 'x', axis=0, tiled=False)]
    ppermute x1, starting transfers between devices: 2.74 us -> 6.72 us  [local(): partner_columns = lax.ppermute(own_columns, 'core', [(0, 1), (1, 0)])]
    all_gather x1, waiting for transfers between devices: 51.3 us -> 54.3 us  [local(): own_columns = lax.all_gather(own_columns, 'y', axis=1, tiled=False)]
where the time goes in v11:
time: 274 us; the launch traced here: 271 us
  waiting for transfers between devices  89.6 us (33%)
  starting transfers between devices  72.9 us (27%)
  blocking collectives  58.3 us (21%)
  local copies, waits for them, and re-layouts  16.7 us (6%)
  between operations  14.3 us (5%)
  matrix products  11.9 us (4%)
  other arithmetic  6.99 us (3%)
    all_gather x1, waiting for transfers between devices, local(): own_columns = lax.all_gather(own_columns, 'y', axis=1, tiled=False)  54.3 us
    all_to_all x1, blocking collectives, local(): received = lax.all_to_all(pieces, ('x', 'y'), 0, 0, tiled=True)  47.2 us
    all_to_all x1, starting transfers between devices, local(): lax.all_to_all(copies, 'zl', 0, 0, tiled=True).astype(jnp.float32)  39.2 us
    ppermute x1, waiting for transfers between devices, from_behind(): lax.ppermute(value, axis, [(source, source + steps) for source in range(i...  20.2 us
    ppermute x1, starting transfers between devices, local(): partner_grad = lax.ppermute(half_grad, 'core', swap)  13.1 us
    all_gather x1, blocking collectives, local(): own_columns = lax.all_gather(own_columns, 'x', axis=0, tiled=False)  11.2 us
    unnamed x6, local copies, waits for them, and re-layouts  11.2 us
    dot_general x2, matrix products, block(): jnp.einsum('npj,cj->npc', cotangent_kernel_taps, full_kernel, preferred_e...  10.8 us
  transfers between devices with their start and end apart: 10, of which 6 were waited for; matrix products, arithmetic and copies ran while one was open for 5% of the time, Pallas kernels for 0%

profile of v11, /device:TPU:1, one launch (start us, length us, event | category | flops | bytes accessed | tf_op | source)
XLA Modules:
  0.0 270.8 jit_solution(3406364317866667200)
XLA Ops:
  7.2 0.0 copy-start
  7.2 0.0 copy-start.1
  7.2 0.0 all-gather.3.cloned.1.call-start
  7.2 0.8 copy-done
  8.1 11.2 %all_gather.10 = bf16[4,24,1152]{2,1,0:T(8,128)(2,1)} all-gather(bf16[1,24,1152]{2,1,0:T(8,128)(2,1)S(1)} %constant_dynamic-slice_fusion.2), channel_id=1, replica_groups=mesh['section'=2,'x'=4,'y'=8,'zl'=8,'core'=2] {'x'}, dimensions={0}, use_global_device_ids=true | all-gather | bytes 276480 | tf_op jit(solution)/shard_map/all_gather | solution.py:56
  19.3 0.0 all-gather.3.cloned.1.call-update
  19.3 54.3 %all-gather.3.cloned.1.call-done = bf16[4,192,1152]{2,1,0:T(8,128)(2,1)} async-done(((bf16[4,24,1152]{2,1,0:T(8,128)(2,1)}), bf16[4,192,1152]{2,1,0:T(8,128)(2,1)}) %all-gather.3.cloned.1.call-update) | async-done | bytes 1769488 | tf_op jit(solution)/shard_map/all_gather | solution.py:57
  73.6 6.7 %collective-permute-start.4 = (bf16[768,1152]{1,0:T(8,128)(2,1)}, bf16[768,1152]{1,0:T(8,128)(2,1)}, u32[]{:S(2)}, u32[]{:S(2)}) collective-permute-start(bf16[768,1152]{1,0:T(8,128)(2,1)} %bitcast.46), channel_id=1, source_target_pairs={{0,1},{1,0},{2,3},{3,2},{4,5},{5,4},{6,7},{7,6},{8,9},{9,8},{10,11... | collective-permute-start | bytes 5308424 | tf_op jit(solution)/shard_map/ppermute | solution.py:59
  80.3 0.8 fusion.50
  81.1 3.2 %collective-permute-start.2 = (bf16[2,16,768]{2,1,0:T(8,128)(2,1)S(1)}, bf16[2,16,768]{2,1,0:T(8,128)(2,1)S(1)}, u32[]{:S(2)}, u32[]{:S(2)}) collective-permute-start(bf16[2,16,768]{2,1,0:T(8,128)(2,1)S(1)} %get-tuple-element.14), channel_id=1, source_target_pairs={{0,1},{1,2},{2,3},{3,4},{4,5},{5,6},{6,7},{7,8},{8,9},{9,10},{10,1... | collective-permute-start | bytes 147464 | tf_op jit(solution)/shard_map/ppermute | solution.py:17
  84.3 1.9 collective-permute-start.3
  86.2 0.9 broadcast_multiply_fusion
  87.2 0.2 broadcast_in_dim.16
  87.4 0.1 mul.127
  87.6 3.6 %collective-permute-start = (bf16[2,32,768]{2,1,0:T(8,128)(2,1)S(1)}, bf16[2,32,768]{2,1,0:T(8,128)(2,1)S(1)}, u32[]{:S(2)}, u32[]{:S(2)}) collective-permute-start(bf16[2,32,768]{2,1,0:T(8,128)(2,1)S(1)} %get-tuple-element.16), channel_id=1, source_target_pairs={{0,1},{1,2},{2,3},{3,4},{4,5},{5,6},{6,7},{7,8},{8,9},{9,10},{10,1... | collective-permute-start | bytes 294920 | tf_op jit(solution)/shard_map/ppermute | solution.py:17
  91.2 1.9 collective-permute-start.1
  93.2 0.0 collective-permute-done.2
  93.2 0.0 collective-permute-done.3
  93.2 0.0 copy-done.1
  93.2 0.2 fusion.28
  93.4 0.0 collective-permute-done
  93.4 3.8 %collective-permute-done.1 = bf16[2,32,768]{2,1,0:T(8,128)(2,1)S(1)} collective-permute-done((bf16[2,32,768]{2,1,0:T(8,128)(2,1)S(1)}, bf16[2,32,768]{2,1,0:T(8,128)(2,1)S(1)}, u32[]{:S(2)}, u32[]{:S(2)}) %collective-permute-start.1) | collective-permute-done | bytes 98336 | tf_op jit(solution)/shard_map/ppermute | solution.py:18
  97.2 0.0 collective-permute-done.4
  97.2 6.1 %multiply_convert_fusion = (bf16[2,160,768]{2,1,0:T(8,128)(2,1)S(1)}, f32[2,160,768]{2,1,0:T(8,128)}, f32[2,160]{1,0:T(2,128)S(1)}, f32[2,160,768]{2,1,0:T(8,128)S(1)}, f32[2,160,768]{2,1,0:T(8,128)S(1)}) fusion(f32[2,160]{1,0:T(2,128)S(1)} %get-tuple-element.19, bf16[2,16,768]{2,1,0:T(8,128)(2,1)S(1)} %collective-permute-done.3, ...), kind=kOutput, calls=%fused_computation.36 | convolution fusion | flops 1162886912 | bytes 8555009 | tf_op jit(solution)/shard_map/npj,cj->npc/dot_general | solution.py:89
  103.3 0.3 fusion.41
  103.7 1.3 collective-permute-start.5
  105.0 0.1 slice_bitcast_fusion.2
  105.1 20.2 %collective-permute-done.5 = bf16[2,160,768]{2,1,0:T(8,128)(2,1)S(1)} collective-permute-done((bf16[2,160,768]{2,1,0:T(8,128)(2,1)S(1)}, bf16[2,160,768]{2,1,0:T(8,128)(2,1)S(1)}, u32[]{:S(2)}, u32[]{:S(2)}) %collective-permute-start.5) | collective-permute-done | bytes 491552 | tf_op jit(solution)/shard_map/ppermute | solution.py:26
  125.3 0.1 broadcast_select_fusion
  125.3 1.1 fusion.22
  126.5 3.3 %constant_dynamic-slice_fusion = (f32[768,1152]{0,1:T(8,128)}, f32[768,1152]{0,1:T(8,128)}) fusion(f32[768,2304]{0,1:T(8,128)S(1)} %bitcast.39, s32[]{:T(128)S(6)} %select_n.49, s32[]{:T(128)S(6)} %select_n.44), kind=kLoop, calls=%fused_computation.62 | loop fusion | bytes 14155784 | tf_op jit(solution)/shard_map/dynamic_slice | solution.py:138
  129.7 5.2 %copy.19 = f32[768,1152]{1,0:T(8,128)} copy(f32[768,1152]{0,1:T(8,128)} %get-tuple-element.2) | data formatting | bytes 7077888
  134.9 1.9 collective-permute-start.6
  136.8 5.2 %copy.18 = f32[768,1152]{1,0:T(8,128)} copy(f32[768,1152]{0,1:T(8,128)} %get-tuple-element.3) | data formatting | bytes 7077888
  142.0 1.4 collective-permute-done.6
  143.4 3.4 %add_convert_fusion = bf16[768,1152]{1,0:T(8,128)(2,1)S(1)} fusion(f32[768,1152]{1,0:T(8,128)} %copy.18, f32[768,1152]{1,0:T(8,128)} %collective-permute-done.6), kind=kLoop, calls=%fused_computation.2 | loop fusion | flops 1769472 | bytes 8847360 | tf_op jit(solution)/shard_map/convert_element_type | solution.py:140
  146.8 47.2 %all_to_all.10 = bf16[32,24,1152]{2,1,0:T(8,128)(2,1)S(1)} all-to-all(bf16[32,24,1152]{2,1,0:T(8,128)(2,1)S(1)} %bitcast.40), channel_id=1, replica_groups=mesh['section'=2,'x'=4,'y'=8,'zl'=8,'core'=2] {'x','y'}, dimensions={0} | all-to-all | bytes 3538944 | tf_op jit(solution)/shard_map/all_to_all | solution.py:141
  193.9 0.3 reduce_sum.51
  194.2 0.8 broadcast_in_dim.32
  195.0 39.2 %all-to-all-start.1 = ((bf16[8,24,1152]{2,1,0:T(8,128)(2,1)}), bf16[8,24,1152]{2,1,0:T(8,128)(2,1)S(1)}, u32[]{:S(2)}, u32[]{:S(2)}) async-start(bf16[8,24,1152]{2,1,0:T(8,128)(2,1)} %broadcast_in_dim.32), calls=%async_computation.1 | async-start | bytes 884736 | tf_op jit(solution)/shard_map/all_to_all | solution.py:144
  234.2 0.1 slice_bitcast_fusion.3
  234.3 0.1 fusion.49
  234.4 4.7 %multiply_reduce_fusion.1 = (f32[2,128]{1,0:T(2,128)S(1)}, f32[2,128,768]{2,1,0:T(8,128)S(1)}) fusion(f32[2,160,768]{2,1,0:T(8,128)S(1)} %get-tuple-element.7, f32[2,160,768]{2,1,0:T(8,128)} %get-tuple-element.5, bf16[768,1152]{1,0:T(8,128)(2,1)} %collective-permute-done.4, bf16[768,1152]{1,0:T(8,128)(2,1)} %bitcast.48, pred[]{:T(512)S(6)} %eq.8, ...), kind=kOutput, calls=%fused_computation.43 | convolution fusion | flops 926023424 | bytes 7078913 | tf_op jit(solution)/shard_map/npj,cj->npc/dot_general | solution.py:89
  239.0 1.0 fusion.42
  240.1 9.1 %all-to-all-done.1 = bf16[8,24,1152]{2,1,0:T(8,128)(2,1)S(1)} async-done(((bf16[8,24,1152]{2,1,0:T(8,128)(2,1)}), bf16[8,24,1152]{2,1,0:T(8,128)(2,1)S(1)}, u32[]{:S(2)}, u32[]{:S(2)}) %all-to-all-start.1) | async-done | bytes 442400 | tf_op jit(solution)/shard_map/all_to_all | solution.py:144
  249.2 0.1 convert_reduce_fusion
  249.3 13.1 %collective-permute-start.7 = (bf16[24,1152]{1,0:T(8,128)(2,1)S(1)}, bf16[24,1152]{1,0:T(8,128)(2,1)S(1)}, u32[]{:S(2)}, u32[]{:S(2)}) collective-permute-start(bf16[24,1152]{1,0:T(8,128)(2,1)S(1)} %multiply_convert_fusion.1), channel_id=1, source_target_pairs={{0,1},{1,0},{2,3},{3,2},{4,5},{5,4},{6,7},{7,6},{8,9},{9,8},{10,11... | collective-permute-start | bytes 165896 | tf_op jit(solution)/shard_map/ppermute | solution.py:146
  262.4 0.8 collective-permute-done.7
  263.2 0.7 maximum_select_fusion.1
  (9 shorter events, 0.1 us)
Async XLA Ops:
  7.2 0.9 copy-start
  7.2 86.0 %copy-start.1 = (bf16[1,2,128,768]{3,2,1,0:T(8,128)(2,1)S(1)}, bf16[1,2,128,768]{3,2,1,0:T(8,128)(2,1)}, u32[]{:S(2)}) copy-start(bf16[1,2,128,768]{3,2,1,0:T(8,128)(2,1)} %param.3) | copy-start | bytes 1179652
  7.2 66.4 %all-gather.3.cloned.1.call-start = ((), (), s32[]{:S(2)}) async-start(), calls=%async_computation.2 | async-start | bytes 1990656 | tf_op jit(solution)/shard_map/all_gather | solution.py:57
  73.6 23.6 %collective-permute-start.4 = (bf16[768,1152]{1,0:T(8,128)(2,1)}, bf16[768,1152]{1,0:T(8,128)(2,1)}, u32[]{:S(2)}, u32[]{:S(2)}) collective-permute-start(bf16[768,1152]{1,0:T(8,128)(2,1)} %bitcast.46), channel_id=1, source_target_pairs={{0,1},{1,0},{2,3},{3,2},{4,5},{5,4},{6,7},{7,6},{8,9},{9,8},{10,11... | collective-permute-start | bytes 5308424 | tf_op jit(solution)/shard_map/ppermute | solution.py:59
  81.1 12.0 %collective-permute-start.2 = (bf16[2,16,768]{2,1,0:T(8,128)(2,1)S(1)}, bf16[2,16,768]{2,1,0:T(8,128)(2,1)S(1)}, u32[]{:S(2)}, u32[]{:S(2)}) collective-permute-start(bf16[2,16,768]{2,1,0:T(8,128)(2,1)S(1)} %get-tuple-element.14), channel_id=1, source_target_pairs={{0,1},{1,2},{2,3},{3,4},{4,5},{5,6},{6,7},{7,8},{8,9},{9,10},{10,1... | collective-permute-start | bytes 147464 | tf_op jit(solution)/shard_map/ppermute | solution.py:17
  84.3 8.9 %collective-permute-start.3 = (bf16[2,16,768]{2,1,0:T(8,128)(2,1)S(1)}, bf16[2,16,768]{2,1,0:T(8,128)(2,1)S(1)}, u32[]{:S(2)}, u32[]{:S(2)}) collective-permute-start(bf16[2,16,768]{2,1,0:T(8,128)(2,1)S(1)} %get-tuple-element.15), channel_id=1, source_target_pairs={{1,0},{2,1},{3,2},{4,3},{5,4},{6,5},{7,6},{8,7},{9,8},{10,9},{11,1... | collective-permute-start | bytes 147464 | tf_op jit(solution)/shard_map/ppermute | solution.py:18
  87.6 5.8 %collective-permute-start = (bf16[2,32,768]{2,1,0:T(8,128)(2,1)S(1)}, bf16[2,32,768]{2,1,0:T(8,128)(2,1)S(1)}, u32[]{:S(2)}, u32[]{:S(2)}) collective-permute-start(bf16[2,32,768]{2,1,0:T(8,128)(2,1)S(1)} %get-tuple-element.16), channel_id=1, source_target_pairs={{0,1},{1,2},{2,3},{3,4},{4,5},{5,6},{6,7},{7,8},{8,9},{9,10},{10,1... | collective-permute-start | bytes 294920 | tf_op jit(solution)/shard_map/ppermute | solution.py:17
  91.2 5.9 %collective-permute-start.1 = (bf16[2,32,768]{2,1,0:T(8,128)(2,1)S(1)}, bf16[2,32,768]{2,1,0:T(8,128)(2,1)S(1)}, u32[]{:S(2)}, u32[]{:S(2)}) collective-permute-start(bf16[2,32,768]{2,1,0:T(8,128)(2,1)S(1)} %get-tuple-element.17), channel_id=1, source_target_pairs={{1,0},{2,1},{3,2},{4,3},{5,4},{6,5},{7,6},{8,7},{9,8},{10,9},{11,1... | collective-permute-start | bytes 294920 | tf_op jit(solution)/shard_map/ppermute | solution.py:18
  103.7 21.6 %collective-permute-start.5 = (bf16[2,160,768]{2,1,0:T(8,128)(2,1)S(1)}, bf16[2,160,768]{2,1,0:T(8,128)(2,1)S(1)}, u32[]{:S(2)}, u32[]{:S(2)}) collective-permute-start(bf16[2,160,768]{2,1,0:T(8,128)(2,1)S(1)} %fusion.41), channel_id=1, source_target_pairs={{512,0},{513,1},{514,2},{515,3},{516,4},{517,5},{518,6},{519,7},{5... | collective-permute-start | bytes 1474568 | tf_op jit(solution)/shard_map/ppermute | solution.py:26
  134.9 8.4 %collective-permute-start.6 = (f32[768,1152]{1,0:T(8,128)}, f32[768,1152]{1,0:T(8,128)}, u32[]{:S(2)}, u32[]{:S(2)}) collective-permute-start(f32[768,1152]{1,0:T(8,128)} %copy.19), channel_id=1, source_target_pairs={{0,1},{1,0},{2,3},{3,2},{4,5},{5,4},{6,7},{7,6},{8,9},{9,8},{10,11... | collective-permute-start | bytes 10616840 | tf_op jit(solution)/shard_map/ppermute | solution.py:139
  195.0 54.2 %all-to-all-start.1 = ((bf16[8,24,1152]{2,1,0:T(8,128)(2,1)}), bf16[8,24,1152]{2,1,0:T(8,128)(2,1)S(1)}, u32[]{:S(2)}, u32[]{:S(2)}) async-start(bf16[8,24,1152]{2,1,0:T(8,128)(2,1)} %broadcast_in_dim.32), calls=%async_computation.1 | async-start | bytes 884736 | tf_op jit(solution)/shard_map/all_to_all | solution.py:144
  249.3 14.0 %collective-permute-start.7 = (bf16[24,1152]{1,0:T(8,128)(2,1)S(1)}, bf16[24,1152]{1,0:T(8,128)(2,1)S(1)}, u32[]{:S(2)}, u32[]{:S(2)}) collective-permute-start(bf16[24,1152]{1,0:T(8,128)(2,1)S(1)} %multiply_convert_fusion.1), channel_id=1, source_target_pairs={{0,1},{1,0},{2,3},{3,2},{4,5},{5,4},{6,7},{7,6},{8,9},{9,8},{10,11... | collective-permute-start | bytes 165896 | tf_op jit(solution)/shard_map/ppermute | solution.py:146
Sparse Core Ops, SparseCore 0:
  19.4 54.1 all-gather.2

commit v12 on v11

--- a/solution.py
+++ b/solution.py
@@ -134,9 +134,12 @@
     swap = [(0, 1), (1, 0)]
     owned_rows = channel_width // n_dp
     half = 3 * channel_width // 2
-    own_half = lax.dynamic_slice_in_dim(grad_total, core_index * half, half, axis=1)
-    other_half = lax.dynamic_slice_in_dim(grad_total, (1 - core_index) * half, half, axis=1)
-    chip_half = own_half + lax.ppermute(other_half, "core", swap)
+    rounded_total = grad_total.astype(jnp.bfloat16)
+    own_half = lax.dynamic_slice_in_dim(rounded_total, core_index * half, half, axis=1)
+    other_half = lax.dynamic_slice_in_dim(rounded_total, (1 - core_index) * half, half, axis=1)
+    chip_half = own_half.astype(jnp.float32) + lax.ppermute(other_half, "core", swap).astype(
+        jnp.float32
+    )
     pieces = chip_half.astype(jnp.bfloat16).reshape(n_dp, owned_rows, half)
     received = lax.all_to_all(pieces, ("x", "y"), 0, 0, tiled=True)
     owned = jnp.sum(received.astype(jnp.float32), axis=0)

time: 274 us -> 268 us (0.978)
  local copies, waits for them, and re-layouts: 16.7 us -> 12 us
    unnamed x6 -> x8, local copies, waits for them, and re-layouts: 11.2 us -> 8.27 us
  transfers between devices with their start and end apart: 10 -> 10, of which waited for: 6 -> 6; matrix products, arithmetic and copies ran while one was open for 5% -> 4% of each run, Pallas kernels for 0% -> 0%
where the time goes in v12:
time: 268 us; the launch traced here: 265 us
  waiting for transfers between devices  90 us (34%)
  starting transfers between devices  72.2 us (27%)
  blocking collectives  58.4 us (22%)
  between operations  14.3 us (5%)
  local copies, waits for them, and re-layouts  12 us (4%)
  matrix products  11 us (4%)
  other arithmetic  7.09 us (3%)
    all_gather x1, waiting for transfers between devices, local(): own_columns = lax.all_gather(own_columns, 'y', axis=1, tiled=False)  54.3 us
    all_to_all x1, blocking collectives, local(): received = lax.all_to_all(pieces, ('x', 'y'), 0, 0, tiled=True)  47.2 us
    all_to_all x1, starting transfers between devices, local(): lax.all_to_all(copies, 'zl', 0, 0, tiled=True).astype(jnp.float32)  39.2 us
    ppermute x1, waiting for transfers between devices, from_behind(): lax.ppermute(value, axis, [(source, source + steps) for source in range(i...  21 us
    ppermute x1, starting transfers between devices, local(): partner_grad = lax.ppermute(half_grad, 'core', swap)  13.1 us
    all_gather x1, blocking collectives, local(): own_columns = lax.all_gather(own_columns, 'x', axis=0, tiled=False)  11.2 us
    dot_general x2, matrix products, block(): jnp.einsum('npj,cj->npc', cotangent_kernel_taps, full_kernel, preferred_e...  9.83 us
    all_to_all x1, waiting for transfers between devices, local(): lax.all_to_all(copies, 'zl', 0, 0, tiled=True).astype(jnp.float32)  8.81 us
  transfers between devices with their start and end apart: 10, of which 6 were waited for; matrix products, arithmetic and copies ran while one was open for 4% of the time, Pallas kernels for 0%

profile of v12, /device:TPU:1, one launch (start us, length us, event | category | flops | bytes accessed | tf_op | source)
XLA Modules:
  0.0 264.9 jit_solution(886409400594719542)
XLA Ops:
  7.2 0.0 copy-start
  7.2 0.0 copy-start.1
  7.2 0.0 all-gather.3.cloned.1.call-start
  7.2 0.8 copy-done
  8.1 11.2 %all_gather.10 = bf16[4,24,1152]{2,1,0:T(8,128)(2,1)} all-gather(bf16[1,24,1152]{2,1,0:T(8,128)(2,1)S(1)} %constant_dynamic-slice_fusion.2), channel_id=1, replica_groups=mesh['section'=2,'x'=4,'y'=8,'zl'=8,'core'=2] {'x'}, dimensions={0}, use_global_device_ids=true | all-gather | bytes 276480 | tf_op jit(solution)/shard_map/all_gather | solution.py:56
  19.3 0.0 all-gather.3.cloned.1.call-update
  19.3 54.3 %all-gather.3.cloned.1.call-done = bf16[4,192,1152]{2,1,0:T(8,128)(2,1)} async-done(((bf16[4,24,1152]{2,1,0:T(8,128)(2,1)}), bf16[4,192,1152]{2,1,0:T(8,128)(2,1)}) %all-gather.3.cloned.1.call-update) | async-done | bytes 1769488 | tf_op jit(solution)/shard_map/all_gather | solution.py:57
  73.6 6.7 %collective-permute-start.4 = (bf16[768,1152]{1,0:T(8,128)(2,1)}, bf16[768,1152]{1,0:T(8,128)(2,1)}, u32[]{:S(2)}, u32[]{:S(2)}) collective-permute-start(bf16[768,1152]{1,0:T(8,128)(2,1)} %bitcast.46), channel_id=1, source_target_pairs={{0,1},{1,0},{2,3},{3,2},{4,5},{5,4},{6,7},{7,6},{8,9},{9,8},{10,11... | collective-permute-start | bytes 5308424 | tf_op jit(solution)/shard_map/ppermute | solution.py:59
  80.3 0.8 fusion.49
  81.1 1.9 collective-permute-start.3
  83.1 3.6 %collective-permute-start.2 = (bf16[2,16,768]{2,1,0:T(8,128)(2,1)S(1)}, bf16[2,16,768]{2,1,0:T(8,128)(2,1)S(1)}, u32[]{:S(2)}, u32[]{:S(2)}) collective-permute-start(bf16[2,16,768]{2,1,0:T(8,128)(2,1)S(1)} %get-tuple-element.14), channel_id=1, source_target_pairs={{0,1},{1,2},{2,3},{3,4},{4,5},{5,6},{6,7},{7,8},{8,9},{9,10},{10,1... | collective-permute-start | bytes 147464 | tf_op jit(solution)/shard_map/ppermute | solution.py:17
  86.7 0.9 broadcast_multiply_fusion
  87.7 0.2 broadcast_in_dim.16
  87.9 0.1 mul.127
  88.1 1.9 collective-permute-start
  90.0 2.4 collective-permute-start.1
  92.4 0.0 collective-permute-done.3
  92.4 0.0 collective-permute-done.2
  92.5 0.0 copy-done.1
  92.5 0.2 fusion.27
  92.6 0.0 collective-permute-done
  92.7 3.3 %collective-permute-done.1 = bf16[2,32,768]{2,1,0:T(8,128)(2,1)S(1)} collective-permute-done((bf16[2,32,768]{2,1,0:T(8,128)(2,1)S(1)}, bf16[2,32,768]{2,1,0:T(8,128)(2,1)S(1)}, u32[]{:S(2)}, u32[]{:S(2)}) %collective-permute-start.1) | collective-permute-done | bytes 98336 | tf_op jit(solution)/shard_map/ppermute | solution.py:18
  96.0 0.0 collective-permute-done.4
  96.0 6.1 %multiply_convert_fusion = (bf16[2,160,768]{2,1,0:T(8,128)(2,1)S(1)}, f32[2,160,768]{2,1,0:T(8,128)}, f32[2,160]{1,0:T(2,128)S(1)}, f32[2,160,768]{2,1,0:T(8,128)S(1)}, f32[2,160,768]{2,1,0:T(8,128)S(1)}) fusion(f32[2,160]{1,0:T(2,128)S(1)} %get-tuple-element.19, bf16[2,16,768]{2,1,0:T(8,128)(2,1)S(1)} %collective-permute-done.3, ...), kind=kOutput, calls=%fused_computation.36 | convolution fusion | flops 1162886912 | bytes 8555009 | tf_op jit(solution)/shard_map/npj,cj->npc/dot_general | solution.py:89
  102.1 0.3 fusion.40
  102.5 1.3 collective-permute-start.5
  103.8 0.1 slice_bitcast_fusion.2
  103.9 21.0 %collective-permute-done.5 = bf16[2,160,768]{2,1,0:T(8,128)(2,1)} collective-permute-done((bf16[2,160,768]{2,1,0:T(8,128)(2,1)S(1)}, bf16[2,160,768]{2,1,0:T(8,128)(2,1)}, u32[]{:S(2)}, u32[]{:S(2)}) %collective-permute-start.5) | collective-permute-done | bytes 491552 | tf_op jit(solution)/shard_map/ppermute | solution.py:26
  124.9 1.1 broadcast_select_fusion
  126.0 1.1 bitcast_convert_fusion
  127.2 1.5 constant_dynamic-slice_fusion.1
  128.7 3.9 %copy.19 = bf16[768,1152]{1,0:T(8,128)(2,1)} copy(bf16[768,1152]{0,1:T(8,128)(2,1)} %get-tuple-element.3) | data formatting | bytes 3538944
  132.5 1.9 collective-permute-start.6
  134.4 2.3 copy.18
  136.7 1.7 collective-permute-done.6
  138.4 2.4 add_convert_fusion
  140.9 47.2 %all_to_all.10 = bf16[32,24,1152]{2,1,0:T(8,128)(2,1)S(1)} all-to-all(bf16[32,24,1152]{2,1,0:T(8,128)(2,1)S(1)} %bitcast.39), channel_id=1, replica_groups=mesh['section'=2,'x'=4,'y'=8,'zl'=8,'core'=2] {'x','y'}, dimensions={0} | all-to-all | bytes 3538944 | tf_op jit(solution)/shard_map/all_to_all | solution.py:144
  188.0 0.3 reduce_sum.51
  188.3 0.8 broadcast_in_dim.32
  189.1 39.2 %all-to-all-start.1 = ((bf16[8,24,1152]{2,1,0:T(8,128)(2,1)}), bf16[8,24,1152]{2,1,0:T(8,128)(2,1)S(1)}, u32[]{:S(2)}, u32[]{:S(2)}) async-start(bf16[8,24,1152]{2,1,0:T(8,128)(2,1)} %broadcast_in_dim.32), calls=%async_computation.1 | async-start | bytes 884736 | tf_op jit(solution)/shard_map/all_to_all | solution.py:147
  228.3 0.0 copy-start.2
  228.3 0.1 slice_bitcast_fusion.3
  228.4 0.1 fusion.48
  228.5 1.3 copy-done.2
  229.8 3.7 %multiply_reduce_fusion.1 = (f32[2,128]{1,0:T(2,128)S(1)}, f32[2,128,768]{2,1,0:T(8,128)S(1)}) fusion(f32[2,160,768]{2,1,0:T(8,128)S(1)} %get-tuple-element.7, f32[2,160,768]{2,1,0:T(8,128)} %get-tuple-element.5, bf16[768,1152]{1,0:T(8,128)(2,1)} %collective-permute-done.4, bf16[768,1152]{1,0:T(8,128)(2,1)S(1)} %bitcast.48, pred[]{:T(512)S(6)} %eq.8, ...), kind=kOutput, calls=%fused_computation.43 | convolution fusion | flops 926023424 | bytes 7078913 | tf_op jit(solution)/shard_map/npj,cj->npc/dot_general | solution.py:89
  233.5 1.0 fusion.41
  234.5 8.8 %all-to-all-done.1 = bf16[8,24,1152]{2,1,0:T(8,128)(2,1)S(1)} async-done(((bf16[8,24,1152]{2,1,0:T(8,128)(2,1)}), bf16[8,24,1152]{2,1,0:T(8,128)(2,1)S(1)}, u32[]{:S(2)}, u32[]{:S(2)}) %all-to-all-start.1) | async-done | bytes 442400 | tf_op jit(solution)/shard_map/all_to_all | solution.py:147
  243.3 0.1 convert_reduce_fusion
  243.4 13.1 %collective-permute-start.7 = (bf16[24,1152]{1,0:T(8,128)(2,1)S(1)}, bf16[24,1152]{1,0:T(8,128)(2,1)S(1)}, u32[]{:S(2)}, u32[]{:S(2)}) collective-permute-start(bf16[24,1152]{1,0:T(8,128)(2,1)S(1)} %multiply_convert_fusion.1), channel_id=1, source_target_pairs={{0,1},{1,0},{2,3},{3,2},{4,5},{5,4},{6,7},{7,6},{8,9},{9,8},{10,11... | collective-permute-start | bytes 165896 | tf_op jit(solution)/shard_map/ppermute | solution.py:149
  256.5 0.8 collective-permute-done.7
  257.4 0.7 maximum_select_fusion.1
  (9 shorter events, 0.1 us)
Async XLA Ops:
  7.2 0.9 copy-start
  7.2 85.3 %copy-start.1 = (bf16[1,2,128,768]{3,2,1,0:T(8,128)(2,1)S(1)}, bf16[1,2,128,768]{3,2,1,0:T(8,128)(2,1)}, u32[]{:S(2)}) copy-start(bf16[1,2,128,768]{3,2,1,0:T(8,128)(2,1)} %param.3) | copy-start | bytes 1179652
  7.2 66.4 %all-gather.3.cloned.1.call-start = ((), (), s32[]{:S(2)}) async-start(), calls=%async_computation.2 | async-start | bytes 1990656 | tf_op jit(solution)/shard_map/all_gather | solution.py:57
  73.6 22.4 %collective-permute-start.4 = (bf16[768,1152]{1,0:T(8,128)(2,1)}, bf16[768,1152]{1,0:T(8,128)(2,1)}, u32[]{:S(2)}, u32[]{:S(2)}) collective-permute-start(bf16[768,1152]{1,0:T(8,128)(2,1)} %bitcast.46), channel_id=1, source_target_pairs={{0,1},{1,0},{2,3},{3,2},{4,5},{5,4},{6,7},{7,6},{8,9},{9,8},{10,11... | collective-permute-start | bytes 5308424 | tf_op jit(solution)/shard_map/ppermute | solution.py:59
  81.1 11.3 %collective-permute-start.3 = (bf16[2,16,768]{2,1,0:T(8,128)(2,1)S(1)}, bf16[2,16,768]{2,1,0:T(8,128)(2,1)S(1)}, u32[]{:S(2)}, u32[]{:S(2)}) collective-permute-start(bf16[2,16,768]{2,1,0:T(8,128)(2,1)S(1)} %get-tuple-element.15), channel_id=1, source_target_pairs={{1,0},{2,1},{3,2},{4,3},{5,4},{6,5},{7,6},{8,7},{9,8},{10,9},{11,1... | collective-permute-start | bytes 147464 | tf_op jit(solution)/shard_map/ppermute | solution.py:18
  83.1 9.4 %collective-permute-start.2 = (bf16[2,16,768]{2,1,0:T(8,128)(2,1)S(1)}, bf16[2,16,768]{2,1,0:T(8,128)(2,1)S(1)}, u32[]{:S(2)}, u32[]{:S(2)}) collective-permute-start(bf16[2,16,768]{2,1,0:T(8,128)(2,1)S(1)} %get-tuple-element.14), channel_id=1, source_target_pairs={{0,1},{1,2},{2,3},{3,4},{4,5},{5,6},{6,7},{7,8},{8,9},{9,10},{10,1... | collective-permute-start | bytes 147464 | tf_op jit(solution)/shard_map/ppermute | solution.py:17
  88.1 4.6 %collective-permute-start = (bf16[2,32,768]{2,1,0:T(8,128)(2,1)S(1)}, bf16[2,32,768]{2,1,0:T(8,128)(2,1)S(1)}, u32[]{:S(2)}, u32[]{:S(2)}) collective-permute-start(bf16[2,32,768]{2,1,0:T(8,128)(2,1)S(1)} %get-tuple-element.16), channel_id=1, source_target_pairs={{0,1},{1,2},{2,3},{3,4},{4,5},{5,6},{6,7},{7,8},{8,9},{9,10},{10,1... | collective-permute-start | bytes 294920 | tf_op jit(solution)/shard_map/ppermute | solution.py:17
  90.0 5.9 %collective-permute-start.1 = (bf16[2,32,768]{2,1,0:T(8,128)(2,1)S(1)}, bf16[2,32,768]{2,1,0:T(8,128)(2,1)S(1)}, u32[]{:S(2)}, u32[]{:S(2)}) collective-permute-start(bf16[2,32,768]{2,1,0:T(8,128)(2,1)S(1)} %get-tuple-element.17), channel_id=1, source_target_pairs={{1,0},{2,1},{3,2},{4,3},{5,4},{6,5},{7,6},{8,7},{9,8},{10,9},{11,1... | collective-permute-start | bytes 294920 | tf_op jit(solution)/shard_map/ppermute | solution.py:18
  102.5 22.4 %collective-permute-start.5 = (bf16[2,160,768]{2,1,0:T(8,128)(2,1)S(1)}, bf16[2,160,768]{2,1,0:T(8,128)(2,1)}, u32[]{:S(2)}, u32[]{:S(2)}) collective-permute-start(bf16[2,160,768]{2,1,0:T(8,128)(2,1)S(1)} %fusion.40), channel_id=1, source_target_pairs={{512,0},{513,1},{514,2},{515,3},{516,4},{517,5},{518,6},{519,7},{5... | collective-permute-start | bytes 1474568 | tf_op jit(solution)/shard_map/ppermute | solution.py:26
  132.5 5.9 %collective-permute-start.6 = (bf16[768,1152]{1,0:T(8,128)(2,1)}, bf16[768,1152]{1,0:T(8,128)(2,1)}, u32[]{:S(2)}, u32[]{:S(2)}) collective-permute-start(bf16[768,1152]{1,0:T(8,128)(2,1)} %copy.19), channel_id=1, source_target_pairs={{0,1},{1,0},{2,3},{3,2},{4,5},{5,4},{6,7},{7,6},{8,9},{9,8},{10,11... | collective-permute-start | bytes 5308424 | tf_op jit(solution)/shard_map/ppermute | solution.py:140
  189.1 54.2 %all-to-all-start.1 = ((bf16[8,24,1152]{2,1,0:T(8,128)(2,1)}), bf16[8,24,1152]{2,1,0:T(8,128)(2,1)S(1)}, u32[]{:S(2)}, u32[]{:S(2)}) async-start(bf16[8,24,1152]{2,1,0:T(8,128)(2,1)} %broadcast_in_dim.32), calls=%async_computation.1 | async-start | bytes 884736 | tf_op jit(solution)/shard_map/all_to_all | solution.py:147
  228.3 1.5 copy-start.2
  243.4 14.0 %collective-permute-start.7 = (bf16[24,1152]{1,0:T(8,128)(2,1)S(1)}, bf16[24,1152]{1,0:T(8,128)(2,1)S(1)}, u32[]{:S(2)}, u32[]{:S(2)}) collective-permute-start(bf16[24,1152]{1,0:T(8,128)(2,1)S(1)} %multiply_convert_fusion.1), channel_id=1, source_target_pairs={{0,1},{1,0},{2,3},{3,2},{4,5},{5,4},{6,7},{7,6},{8,9},{9,8},{10,11... | collective-permute-start | bytes 165896 | tf_op jit(solution)/shard_map/ppermute | solution.py:149
Sparse Core Ops, SparseCore 0:
  19.4 54.1 all-gather.2
